TPU v7x, 256 devices: a whole 4x4x8 slice. The times are simulated.
256 devices in a mesh: tm: 16 (over z, core), tile: 16 (over x, y).
Axes of the slice: x: 4, y: 4, z: 8, core: 2. Of those that a mesh axis runs over, the one named last changes fastest.
Arguments:
- obs_values: bfloat16 [16, 32768, 128], P('tm', 'tile'), may hold values from -6 to 6
- obs_weight: bfloat16 [16, 32768, 128], P('tm', 'tile'), may hold values from 0.19921875 to 2
- obs_count: int32 [16, 32768], P('tm', 'tile'), may hold values from 32 to 128
- dest_tile: int32 [16, 32768, 1], P('tm', 'tile'), may hold values from 0 to 15; in each aligned block of 2048 rows (0 to 2047, 2048 to 4095, ..., all dimensions but the last counted through in order) at most 256 rows name the same one
- jac_index: int32 [16, 32768], P('tm', 'tile'), may hold values from 0 to 255
- jacobian: bfloat16 [16, 4096, 128, 128], P('tm', 'tile'), may hold values from -0.5 to 0.5
- jac_state: int32 [16, 4096], P('tm', 'tile'), may hold values from 0 to 63
- corr_blocks: bfloat16 [16, 768, 128, 128], P('tm', 'tile'), may hold values from -0.625 to 0.625
- corr_row: int32 [16, 768], P('tm', 'tile'), may hold values from 0 to 63
- corr_col: int32 [16, 768], P('tm', 'tile'), may hold values from 0 to 63
- time_coupling: bfloat16 [16, 1024, 128], P('tm', 'tile'), may hold values from 0.19921875 to 0.59765625
Outputs:
- product: bfloat16 [16, 32768, 128], P('tm', 'tile')
Inputs may be any that keep to these rules, and one draw needn't show every extreme that they name: `dest_tile`: in the rows of one device, no tile is named by more than 256 observation blocks, a bound that some block reaches.
All inputs are finite; a program needn't handle non-finite values.
Results may differ from a plain program's by a relative error of at most 0.0075.
Values may be sent and summed in bfloat16 or wider, within the bound.
No kernel may reach another device: no remote copies, remote signals or barrier semaphores. Data moves between devices by JAX's collectives and lax.ppermute only.
A program may use at most 64 MiB of HBM per device.

v0:
```python
import jax
import jax.numpy as jnp
from jax import lax
from jax.sharding import PartitionSpec as P


def from_behind(x, axis, by):
    length = lax.axis_size(axis)
    pairs = [(i, i + by) for i in range(length) if 0 <= i + by < length]
    return lax.ppermute(x, axis, pairs)


def shards(
    obs_values,
    obs_weight,
    obs_count,
    dest_tile,
    jac_index,
    jacobian,
    jac_state,
    corr_blocks,
    corr_row,
    corr_col,
    time_coupling,
):
    obs_total = obs_values.shape[1]
    block_width = obs_values.shape[2]
    jac_total = jacobian.shape[1]
    state_total = time_coupling.shape[1]
    lane_index = lax.broadcasted_iota(jnp.int32, (obs_total, block_width), 1)
    keeping = (lane_index < obs_count[0][:, None]).astype(jnp.float32)
    weighted = (
        obs_values[0].astype(jnp.float32) * obs_weight[0].astype(jnp.float32) * keeping
    ).astype(jnp.bfloat16)
    target = dest_tile[0, :, 0]
    column = jac_index[0]
    bin_id = target * jac_total + column
    row_ids = lax.broadcasted_iota(jnp.int32, (jac_total * lax.axis_size("tile"), obs_total), 0)
    picker = (row_ids == bin_id[None, :]).astype(jnp.bfloat16)
    summed = lax.psum_scatter(
        jnp.dot(picker, weighted, preferred_element_type=jnp.float32),
        "tile",
        scatter_dimension=0,
        tiled=True,
    )
    merged = summed.astype(jnp.bfloat16)
    spread = jnp.einsum("kij,ki->kj", jacobian[0], merged, preferred_element_type=jnp.float32)
    state_ids = lax.broadcasted_iota(jnp.int32, (state_total, jac_total), 0)
    owners = state_ids == jac_state[0][None, :]
    state = jnp.dot(owners.astype(jnp.float32), spread, precision=lax.Precision.HIGHEST).astype(
        jnp.bfloat16
    )
    corr_total = corr_blocks.shape[1]
    read_ids = lax.broadcasted_iota(jnp.int32, (corr_total, state_total), 1)
    reader = (read_ids == corr_col[0][:, None]).astype(jnp.bfloat16)
    source = jnp.dot(reader, state, preferred_element_type=jnp.float32).astype(jnp.bfloat16)
    mixing = jnp.einsum("cij,cj->ci", corr_blocks[0], source, preferred_element_type=jnp.float32)
    write_ids = lax.broadcasted_iota(jnp.int32, (state_total, corr_total), 0)
    writer = (write_ids == corr_row[0][None, :]).astype(jnp.float32)
    spatial = jnp.dot(writer, mixing, precision=lax.Precision.HIGHEST).astype(jnp.bfloat16)
    coupling = time_coupling[0]
    earlier = from_behind(spatial, "tm", 1)
    later_state, later_coupling = from_behind((spatial, coupling), "tm", -1)
    coupled = (
        spatial.astype(jnp.float32)
        + coupling.astype(jnp.float32) * earlier.astype(jnp.float32)
        + later_coupling.astype(jnp.float32) * later_state.astype(jnp.float32)
    ).astype(jnp.bfloat16)
    local_state = jnp.dot(
        owners.T.astype(jnp.bfloat16), coupled, preferred_element_type=jnp.float32
    ).astype(jnp.bfloat16)
    model_obs = jnp.einsum(
        "kij,kj->ki", jacobian[0], local_state, preferred_element_type=jnp.float32
    ).astype(jnp.bfloat16)
    portion = lax.all_gather(model_obs, "tile", axis=0, tiled=True)
    columns = lax.broadcasted_iota(jnp.int32, (obs_total, portion.shape[0]), 1)
    picker = (bin_id[:, None] == columns).astype(jnp.bfloat16)
    gathered = jnp.dot(picker, portion, preferred_element_type=jnp.float32)
    return (gathered * keeping).astype(jnp.bfloat16)[None]


def solution(mesh):
    in_specs = (
        P("tm", "tile", None),
        P("tm", "tile", None),
        P("tm", "tile"),
        P("tm", "tile", None),
        P("tm", "tile"),
        P("tm", "tile", None, None),
        P("tm", "tile"),
        P("tm", "tile", None, None),
        P("tm", "tile"),
        P("tm", "tile"),
        P("tm", "tile", None),
    )
    out_specs = P("tm", "tile", None)
    return jax.shard_map(shards, mesh=mesh, in_specs=in_specs, out_specs=out_specs, check_vma=False)
```

profile of v0, /device:TPU:161, one launch (start us, length us, event | category | flops | bytes accessed | tf_op | source)
XLA Modules:
  0.0 182.5 jit_solution(13283383729035749452)
XLA Ops:
  6.5 0.8 bitcast_add_fusion
  7.4 0.0 copy-start.3
  7.4 8.6 %fusion = f32[4096,128]{1,0:T(8,128)} fusion(s32[2048]{0:T(1024)S(1)} %bitcast.51, bf16[1,2048,128]{2,1,0:T(8,128)(2,1)} %param.12, bf16[1,2048,128]{2,1,0:T(8,128)(2,1)} %param.11, s32[2048]{0:T(1024)} %bitcast.55), kind=kOutput, calls=%fused_computation.2 | convolution fusion | flops 2157445120 | bytes 3162112 | tf_op jit(solution)/shard_map/dot_general | solution.py:41
  16.0 0.0 reduce-scatter.2.cloned.1.call-update
  16.0 0.0 all-gather.2.cloned.1.call-start
  16.1 2.6 %collective-permute-start.1 = (bf16[64,128]{1,0:T(8,128)(2,1)S(1)}, bf16[64,128]{1,0:T(8,128)(2,1)S(1)}, u32[]{:S(2)}, u32[]{:S(2)}) collective-permute-start(bf16[64,128]{1,0:T(8,128)(2,1)S(1)} %bitcast.50), channel_id=1, source_target_pairs={{16,0},{32,16},{48,32},{64,48},{80,64},{96,80},{112,96},{128,112},... | collective-permute-start | bytes 49160 | tf_op jit(solution)/shard_map/ppermute | solution.py:10
  18.7 77.2 %reduce-scatter.2.cloned.1.call-done = f32[256,128]{1,0:T(8,128)} async-done(((f32[4096,128]{1,0:T(8,128)}), f32[256,128]{1,0:T(8,128)}) %reduce-scatter.2.cloned.1.call-update) | async-done | bytes 131088 | tf_op jit(solution)/shard_map/reduce_scatter | solution.py:40
  95.8 0.9 convert_bitcast_fusion
  96.7 0.0 copy-start.1
  96.8 0.0 copy-start.6
  96.8 5.7 %fusion.6 = f32[256,1,128]{2,1,0:T(1,128)S(1)} fusion(bf16[1,256,128,128]{3,2,1,0:T(8,128)(2,1)} %param.16, bf16[256,128,1]{1,0,2:T(8,128)(2,1)S(1)} %convert_bitcast_fusion), kind=kOutput, calls=%fused_computation.8 | convolution fusion | flops 8388608 | bytes 8585216 | tf_op jit(solution)/shard_map/kij,ki->kj/dot_general | solution.py:47
  102.4 0.2 convolution_convert_fusion.2
  102.7 0.2 fusion.14
  102.8 0.9 fusion.11
  103.8 0.2 convolution_convert_fusion.1
  103.9 4.5 %collective-permute-start = (bf16[64,128]{1,0:T(8,128)(2,1)S(1)}, bf16[64,128]{1,0:T(8,128)(2,1)S(1)}, u32[]{:S(2)}, u32[]{:S(2)}) collective-permute-start(bf16[64,128]{1,0:T(8,128)(2,1)S(1)} %convolution_convert_fusion.1), channel_id=1, source_target_pairs={{0,16},{16,32},{32,48},{48,64},{64,80},{80,96},{96,112},{112,128},... | collective-permute-start | bytes 49160 | tf_op jit(solution)/shard_map/ppermute | solution.py:10
  108.4 2.1 %collective-permute-start.2 = (bf16[64,128]{1,0:T(8,128)(2,1)S(1)}, bf16[64,128]{1,0:T(8,128)(2,1)S(1)}, u32[]{:S(2)}, u32[]{:S(2)}) collective-permute-start(bf16[64,128]{1,0:T(8,128)(2,1)S(1)} %convolution_convert_fusion.1), channel_id=1, source_target_pairs={{16,0},{32,16},{48,32},{64,48},{80,64},{96,80},{112,96},{128,112},... | collective-permute-start | bytes 49160 | tf_op jit(solution)/shard_map/ppermute | solution.py:10
  110.6 2.9 %collective-permute-done.2 = bf16[64,128]{1,0:T(8,128)(2,1)S(1)} collective-permute-done((bf16[64,128]{1,0:T(8,128)(2,1)S(1)}, bf16[64,128]{1,0:T(8,128)(2,1)S(1)}, u32[]{:S(2)}, u32[]{:S(2)}) %collective-permute-start.2) | collective-permute-done | bytes 16416 | tf_op jit(solution)/shard_map/ppermute | solution.py:10
  113.5 0.2 fusion.13
  113.7 7.8 %fusion.4 = f32[256,1,128]{2,1,0:T(1,128)S(1)} fusion(bf16[1,256,128,128]{3,2,1,0:T(8,128)(2,1)} %param.16, bf16[256,128,1]{1,0,2:T(8,128)(2,1)S(1)} %fusion.13), kind=kOutput, calls=%fused_computation.6 | convolution fusion | flops 8388608 | bytes 8585216 | tf_op jit(solution)/shard_map/kij,kj->ki/dot_general | solution.py:72
  121.5 0.7 convert_element_type.71
  122.2 0.0 all-gather.2.cloned.1.call-update
  122.2 45.8 %all-gather.2.cloned.1.call-done = bf16[4096,128]{1,0:T(8,128)(2,1)} async-done(((bf16[256,128]{1,0:T(8,128)(2,1)}), bf16[4096,128]{1,0:T(8,128)(2,1)}) %all-gather.2.cloned.1.call-update) | async-done | bytes 1048592 | tf_op jit(solution)/shard_map/all_gather | solution.py:75
  168.1 7.6 %fusion.10 = bf16[1,2048,128]{2,1,0:T(8,128)(2,1)} fusion(bf16[4096,128]{1,0:T(8,128)(2,1)} %all-gather.2.cloned.1.call-done, s32[2048]{0:T(1024)S(1)} %add.18, s32[2048]{0:T(1024)S(1)} %bitcast.56), kind=kOutput, calls=%fused_computation.12 | convolution fusion | flops 2156658688 | bytes 1589248 | tf_op jit(solution)/shard_map/dot_general | solution.py:78
  (18 shorter events, 0.0 us)
Async XLA Ops:
  6.5 96.3 %copy-start = (bf16[1,48,128,128]{3,2,1,0:T(8,128)(2,1)S(1)}, bf16[1,48,128,128]{3,2,1,0:T(8,128)(2,1)}, u32[]{:S(2)}) copy-start(bf16[1,48,128,128]{3,2,1,0:T(8,128)(2,1)} %param.18) | copy-start | bytes 4718596
  6.5 89.3 %reduce-scatter.2.cloned.1.call-start = ((), (), s32[]{:S(2)}) async-start(), calls=%async_computation.1 | async-start | bytes 2228224 | tf_op jit(solution)/shard_map/reduce_scatter | solution.py:40
  7.4 8.7 %copy-start.3 = (bf16[1,64,128]{2,1,0:T(8,128)(2,1)S(1)}, bf16[1,64,128]{2,1,0:T(8,128)(2,1)}, u32[]{:S(2)}) copy-start(bf16[1,64,128]{2,1,0:T(8,128)(2,1)} %param.21) | copy-start | bytes 49156
  16.0 86.4 %copy-start.4 = (s32[1,256]{1,0:T(1,128)S(1)}, s32[1,256]{1,0:T(1,128)}, u32[]{:S(2)}) copy-start(s32[1,256]{1,0:T(1,128)} %param.17) | copy-start | bytes 3076
  16.0 86.6 %copy-start.7 = (s32[1,48]{1,0:T(1,128)S(1)}, s32[1,48]{1,0:T(1,128)}, u32[]{:S(2)}) copy-start(s32[1,48]{1,0:T(1,128)} %param.20) | copy-start | bytes 580
  16.0 87.8 %copy-start.5 = (s32[1,48]{1,0:T(1,128)S(1)}, s32[1,48]{1,0:T(1,128)}, u32[]{:S(2)}) copy-start(s32[1,48]{1,0:T(1,128)} %param.19) | copy-start | bytes 580
  16.0 152.0 %all-gather.2.cloned.1.call-start = ((), (), s32[]{:S(2)}) async-start(), calls=%async_computation.2 | async-start | bytes 1114112 | tf_op jit(solution)/shard_map/all_gather | solution.py:75
  16.1 94.5 %collective-permute-start.1 = (bf16[64,128]{1,0:T(8,128)(2,1)S(1)}, bf16[64,128]{1,0:T(8,128)(2,1)S(1)}, u32[]{:S(2)}, u32[]{:S(2)}) collective-permute-start(bf16[64,128]{1,0:T(8,128)(2,1)S(1)} %bitcast.50), channel_id=1, source_target_pairs={{16,0},{32,16},{48,32},{64,48},{80,64},{96,80},{112,96},{128,112},... | collective-permute-start | bytes 49160 | tf_op jit(solution)/shard_map/ppermute | solution.py:10
  96.7 25.4 %copy-start.2 = (s32[1,2048,1]{1,2,0:T(1,128)S(1)}, s32[1,2048,1]{1,2,0:T(1,128)}, u32[]{:S(2)}) copy-start(s32[1,2048,1]{1,2,0:T(1,128)} %param.14) | copy-start | bytes 24580
  96.7 25.5 %copy-start.1 = (s32[1,2048]{1,0:T(1,128)S(1)}, s32[1,2048]{1,0:T(1,128)}, u32[]{:S(2)}) copy-start(s32[1,2048]{1,0:T(1,128)} %param.15) | copy-start | bytes 24580
  96.8 71.3 %copy-start.6 = (s32[1,2048]{1,0:T(1,128)S(1)}, s32[1,2048]{1,0:T(1,128)}, u32[]{:S(2)}) copy-start(s32[1,2048]{1,0:T(1,128)} %param.13) | copy-start | bytes 24580
  103.9 6.6 %collective-permute-start = (bf16[64,128]{1,0:T(8,128)(2,1)S(1)}, bf16[64,128]{1,0:T(8,128)(2,1)S(1)}, u32[]{:S(2)}, u32[]{:S(2)}) collective-permute-start(bf16[64,128]{1,0:T(8,128)(2,1)S(1)} %convolution_convert_fusion.1), channel_id=1, source_target_pairs={{0,16},{16,32},{32,48},{48,64},{64,80},{80,96},{96,112},{112,128},... | collective-permute-start | bytes 49160 | tf_op jit(solution)/shard_map/ppermute | solution.py:10
  108.4 5.1 %collective-permute-start.2 = (bf16[64,128]{1,0:T(8,128)(2,1)S(1)}, bf16[64,128]{1,0:T(8,128)(2,1)S(1)}, u32[]{:S(2)}, u32[]{:S(2)}) collective-permute-start(bf16[64,128]{1,0:T(8,128)(2,1)S(1)} %convolution_convert_fusion.1), channel_id=1, source_target_pairs={{16,0},{32,16},{48,32},{64,48},{80,64},{96,80},{112,96},{128,112},... | collective-permute-start | bytes 49160 | tf_op jit(solution)/shard_map/ppermute | solution.py:10
Sparse Core Ops, SparseCore 0:
  16.1 79.6 reduce-scatter.1
  122.3 45.7 all-gather.1
where the time goes:
time: 186 us; the launch traced here: 182 us
  waiting for transfers between devices  126 us (68%)
  matrix products  31.3 us (17%)
  between operations  13.5 us (7%)
  starting transfers between devices  9.22 us (5%)
  other arithmetic  2.44 us (1%)
    reduce_scatter x1, waiting for transfers between devices, shards(): lax.psum_scatter(jnp.dot(picker, weighted, preferred_element_type=jnp.flo...  77.2 us
    all_gather x1, waiting for transfers between devices, shards(): portion = lax.all_gather(model_obs, 'tile', axis=0, tiled=True)  45.8 us
    ppermute x3, starting transfers between devices, from_behind(): return lax.ppermute(x, axis, pairs)  9.18 us
    dot_general x1, matrix products, shards(): jnp.dot(picker, weighted, preferred_element_type=jnp.float32)  8.59 us
    dot_general x1, matrix products, shards(): jnp.einsum('kij,kj->ki', jacobian[0], local_state, preferred_element_type...  7.78 us
    dot_general x1, matrix products, shards(): gathered = jnp.dot(picker, portion, preferred_element_type=jnp.float32)  7.57 us
    dot_general x1, matrix products, shards(): jnp.einsum('kij,ki->kj', jacobian[0], merged, preferred_element_type=jnp....  5.66 us
  transfers between devices with their start and end apart: 5, of which 3 were waited for; matrix products, arithmetic and copies ran while one was open for 4% of the time, Pallas kernels for 0%

commit v1 on v0

--- a/solution.py
+++ b/solution.py
@@ -2,6 +2,8 @@
 import jax.numpy as jnp
 from jax import lax
 from jax.sharding import PartitionSpec as P
+
+CAP = 256
 
 
 def from_behind(x, axis, by):
@@ -27,6 +29,8 @@
     block_width = obs_values.shape[2]
     jac_total = jacobian.shape[1]
     state_total = time_coupling.shape[1]
+    tiles = lax.axis_size("tile")
+    slots = tiles * CAP
     lane_index = lax.broadcasted_iota(jnp.int32, (obs_total, block_width), 1)
     keeping = (lane_index < obs_count[0][:, None]).astype(jnp.float32)
     weighted = (
@@ -34,15 +38,37 @@
     ).astype(jnp.bfloat16)
     target = dest_tile[0, :, 0]
     column = jac_index[0]
-    bin_id = target * jac_total + column
-    row_ids = lax.broadcasted_iota(jnp.int32, (jac_total * lax.axis_size("tile"), obs_total), 0)
-    picker = (row_ids == bin_id[None, :]).astype(jnp.bfloat16)
-    summed = lax.psum_scatter(
-        jnp.dot(picker, weighted, preferred_element_type=jnp.float32),
-        "tile",
-        scatter_dimension=0,
-        tiled=True,
+
+    tile_ids = lax.broadcasted_iota(jnp.int32, (obs_total, tiles), 1)
+    names = (tile_ids == target[:, None]).astype(jnp.bfloat16)
+    rows = lax.broadcasted_iota(jnp.int32, (obs_total, obs_total), 0)
+    cols = lax.broadcasted_iota(jnp.int32, (obs_total, obs_total), 1)
+    lower = (cols <= rows).astype(jnp.bfloat16)
+    counts = jnp.dot(lower, names, preferred_element_type=jnp.float32)
+    rank = jnp.sum(counts * names.astype(jnp.float32), axis=1).astype(jnp.int32) - 1
+    slot = target * CAP + rank
+
+    slot_ids = lax.broadcasted_iota(jnp.int32, (slots, obs_total), 0)
+    placer = (slot_ids == slot[None, :]).astype(jnp.bfloat16)
+    packed = jnp.dot(placer, weighted, preferred_element_type=jnp.float32).astype(jnp.bfloat16)
+    packed_col = jnp.dot(
+        placer, column.astype(jnp.bfloat16)[:, None], preferred_element_type=jnp.float32
+    ).astype(jnp.bfloat16)
+    send = jnp.concatenate(
+        [
+            packed.reshape(tiles, CAP, block_width),
+            packed_col.reshape(tiles, CAP // block_width, block_width),
+            jnp.zeros((tiles, 16 - CAP // block_width, block_width), jnp.bfloat16),
+        ],
+        axis=1,
     )
+    recv = lax.all_to_all(send, "tile", 0, 0, tiled=True)
+    recv_rows = recv[:, :CAP].reshape(slots, block_width)
+    recv_col = recv[:, CAP:CAP + CAP // block_width].reshape(1, slots).astype(jnp.int32)
+    jac_ids = lax.broadcasted_iota(jnp.int32, (jac_total, slots), 0)
+    binner = (jac_ids == recv_col).astype(jnp.bfloat16)
+    summed = jnp.dot(binner, recv_rows, preferred_element_type=jnp.float32)
+
     merged = summed.astype(jnp.bfloat16)
     spread = jnp.einsum("kij,ki->kj", jacobian[0], merged, preferred_element_type=jnp.float32)
     state_ids = lax.broadcasted_iota(jnp.int32, (state_total, jac_total), 0)
@@ -72,10 +98,12 @@
     model_obs = jnp.einsum(
         "kij,kj->ki", jacobian[0], local_state, preferred_element_type=jnp.float32
     ).astype(jnp.bfloat16)
-    portion = lax.all_gather(model_obs, "tile", axis=0, tiled=True)
-    columns = lax.broadcasted_iota(jnp.int32, (obs_total, portion.shape[0]), 1)
-    picker = (bin_id[:, None] == columns).astype(jnp.bfloat16)
-    gathered = jnp.dot(picker, portion, preferred_element_type=jnp.float32)
+
+    answer = jnp.dot(binner.T, model_obs, preferred_element_type=jnp.float32).astype(jnp.bfloat16)
+    back = lax.all_to_all(answer.reshape(tiles, CAP, block_width), "tile", 0, 0, tiled=True)
+    gathered = jnp.dot(
+        placer.T, back.reshape(slots, block_width), preferred_element_type=jnp.float32
+    )
     return (gathered * keeping).astype(jnp.bfloat16)[None]
 
 

time: 186 us -> 95.2 us (0.51); the launches traced: 182 us -> 94.1 us
  waiting for transfers between devices: 126 us -> 16.6 us
  blocking collectives: 0 us -> 20.2 us
  between operations: 13.5 us -> 0.25 us
  starting transfers between devices: 9.22 us -> 17.2 us
  matrix products: 31.3 us -> 38.2 us
    reduce_scatter x1 -> x0, waiting for transfers between devices: 77.2 us -> none  [shards(): lax.psum_scatter(jnp.dot(picker, weighted, preferred_element_type=jnp.flo...]
    all_gather x1 -> x0, waiting for transfers between devices: 45.8 us -> none  [shards(): portion = lax.all_gather(model_obs, 'tile', axis=0, tiled=True)]
    all_to_all x0 -> x1, blocking collectives: none -> 20.2 us  [shards(): lax.all_to_all(answer.reshape(tiles, CAP, block_width), 'tile', 0, 0, til...]
    all_to_all x0 -> x1, waiting for transfers between devices: none -> 13.5 us  [shards(): recv = lax.all_to_all(send, 'tile', 0, 0, tiled=True)]
    dot_general x2 -> x6, matrix products: 16.2 us -> 26 us  [the longest x1 9.82 us: shards(): jnp.dot(placer.T, back.reshape(slots, block_width), preferred_element_typ...]
    all_to_all x0 -> x1, starting transfers between devices: none -> 6.76 us  [shards(): recv = lax.all_to_all(send, 'tile', 0, 0, tiled=True)]
    dot_general x1, matrix products: 7.78 us -> 4.41 us  [shards(): jnp.einsum('kij,kj->ki', jacobian[0], local_state, preferred_element_type...]
  transfers between devices with their start and end apart: 5 -> 4, of which waited for: 3 -> 2; matrix products, arithmetic and copies ran while one was open for 4% -> 9% of each run, Pallas kernels for 0% -> 0%
where the time goes in v1:
time: 95.2 us; the launch traced here: 94.1 us
  matrix products  38.2 us (40%)
  blocking collectives  20.2 us (21%)
  starting transfers between devices  17.2 us (18%)
  waiting for transfers between devices  16.6 us (17%)
  other arithmetic  1.32 us (1%)
    all_to_all x1, blocking collectives, shards(): lax.all_to_all(answer.reshape(tiles, CAP, block_width), 'tile', 0, 0, til...  20.2 us
    all_to_all x1, waiting for transfers between devices, shards(): recv = lax.all_to_all(send, 'tile', 0, 0, tiled=True)  13.5 us
    ppermute x3, starting transfers between devices, from_behind(): return lax.ppermute(x, axis, pairs)  10.5 us
    dot_general x1, matrix products, shards(): jnp.dot(placer.T, back.reshape(slots, block_width), preferred_element_typ...  9.82 us
    all_to_all x1, starting transfers between devices, shards(): recv = lax.all_to_all(send, 'tile', 0, 0, tiled=True)  6.76 us
    dot_general x1, matrix products, shards(): jnp.dot(placer, weighted, preferred_element_type=jnp.float32)  6.31 us
    dot_general x1, matrix products, shards(): jnp.einsum('kij,ki->kj', jacobian[0], merged, preferred_element_type=jnp....  6.08 us
    dot_general x1, matrix products, shards(): jnp.dot(placer, column.astype(jnp.bfloat16)[:, None], preferred_element_t...  5.59 us
  transfers between devices with their start and end apart: 4, of which 2 were waited for; matrix products, arithmetic and copies ran while one was open for 9% of the time, Pallas kernels for 0%

profile of v1, /device:TPU:161, one launch (start us, length us, event | category | flops | bytes accessed | tf_op | source)
XLA Modules:
  0.0 94.1 jit_solution(12600990245273247525)
XLA Ops:
  0.0 2.3 %fusion.22 = f32[2048]{0:T(1024)S(1)} fusion(s32[2048]{0:T(1024)} %bitcast.66), kind=kOutput, calls=%fused_computation.27 | convolution fusion | flops 138606592 | bytes 16384 | tf_op jit(solution)/shard_map/dot_general | solution.py:47
  2.4 5.6 %fusion.1 = f32[1,4096]{1,0:T(1,128)S(1)} fusion(s32[2048]{0:T(1024)S(1)} %add_add_fusion, s32[1,2048]{1,0:T(1,128)S(1)} %copy-done.7), kind=kOutput, calls=%fused_computation.2 | convolution fusion | flops 25167872 | bytes 32768 | tf_op jit(solution)/shard_map/dot_general | solution.py:54
  8.0 0.1 pad.2.clone
  8.1 6.3 %fusion.11 = bf16[4096,128]{1,0:T(8,128)(2,1)S(1)} fusion(s32[2048]{0:T(1024)S(1)} %add_add_fusion, bf16[1,2048,128]{2,1,0:T(8,128)(2,1)S(1)} %copy-done.5, bf16[1,2048,128]{2,1,0:T(8,128)(2,1)S(1)} %copy-done.6, s32[2048]{0:T(1024)S(1)} %bitcast.71), kind=kOutput, calls=%fused_computation.13 | convolution fusion | flops 2157969408 | bytes 2113536 | tf_op jit(solution)/shard_map/dot_general | solution.py:53
  14.4 1.3 %maximum_maximum_fusion = bf16[16,272,128]{2,1,0:T(8,128)(2,1)} fusion(bf16[16,2,128]{2,1,0:T(2,128)(2,1)S(1)} %bitcast.62, bf16[16,256,128]{2,1,0:T(8,128)(2,1)S(1)} %bitcast.58, bf16[272]{0:T(512)(128)(2,1)S(1)} %pad.2.clone), kind=kLoop, calls=%fused_computation.30 | loop fusion | flops 3342336 | bytes 2171424 | tf_op jit(solution)/shard_map/concatenate | solution.py:57
  15.7 6.8 %all-to-all-start = ((bf16[16,272,128]{2,1,0:T(8,128)(2,1)}), bf16[16,272,128]{2,1,0:T(8,128)(2,1)S(1)}, u32[]{:S(2)}, u32[]{:S(2)}) async-start(bf16[16,272,128]{2,1,0:T(8,128)(2,1)} %maximum_maximum_fusion), calls=%async_computation | async-start | bytes 2228224 | tf_op jit(solution)/shard_map/all_to_all | solution.py:65
  22.5 2.9 %collective-permute-start.1 = (bf16[64,128]{1,0:T(8,128)(2,1)S(1)}, bf16[64,128]{1,0:T(8,128)(2,1)S(1)}, u32[]{:S(2)}, u32[]{:S(2)}) collective-permute-start(bf16[64,128]{1,0:T(8,128)(2,1)S(1)} %bitcast.64), channel_id=1, source_target_pairs={{16,0},{32,16},{48,32},{64,48},{80,64},{96,80},{112,96},{128,112},... | collective-permute-start | bytes 49160 | tf_op jit(solution)/shard_map/ppermute | solution.py:12
  25.4 13.5 %all-to-all-done = bf16[16,272,128]{2,1,0:T(8,128)(2,1)S(1)} async-done(((bf16[16,272,128]{2,1,0:T(8,128)(2,1)}), bf16[16,272,128]{2,1,0:T(8,128)(2,1)S(1)}, u32[]{:S(2)}, u32[]{:S(2)}) %all-to-all-start) | async-done | bytes 1114144 | tf_op jit(solution)/shard_map/all_to_all | solution.py:65
  38.9 0.1 slice.9
  39.0 0.7 fusion.24
  39.8 0.0 slice-start.1
  39.8 6.1 %fusion.9 = f32[256,1,128]{2,1,0:T(1,128)S(1)} fusion(bf16[1,256,128,128]{3,2,1,0:T(8,128)(2,1)} %param.16, bf16[256,128,1]{1,0,2:T(8,128)(2,1)S(1)} %fusion.24), kind=kOutput, calls=%fused_computation.11 | convolution fusion | flops 8388608 | bytes 8585216 | tf_op jit(solution)/shard_map/kij,ki->kj/dot_general | solution.py:73
  45.9 0.2 convolution_convert_fusion.3
  46.1 0.2 fusion.25
  46.3 0.9 fusion.19
  47.2 0.2 convolution_convert_fusion.2
  47.3 5.7 %collective-permute-start = (bf16[64,128]{1,0:T(8,128)(2,1)S(1)}, bf16[64,128]{1,0:T(8,128)(2,1)S(1)}, u32[]{:S(2)}, u32[]{:S(2)}) collective-permute-start(bf16[64,128]{1,0:T(8,128)(2,1)S(1)} %convolution_convert_fusion.2), channel_id=1, source_target_pairs={{0,16},{16,32},{32,48},{48,64},{64,80},{80,96},{96,112},{112,128},... | collective-permute-start | bytes 49160 | tf_op jit(solution)/shard_map/ppermute | solution.py:12
  53.0 1.9 %collective-permute-start.2 = (bf16[64,128]{1,0:T(8,128)(2,1)S(1)}, bf16[64,128]{1,0:T(8,128)(2,1)S(1)}, u32[]{:S(2)}, u32[]{:S(2)}) collective-permute-start(bf16[64,128]{1,0:T(8,128)(2,1)S(1)} %convolution_convert_fusion.2), channel_id=1, source_target_pairs={{16,0},{32,16},{48,32},{64,48},{80,64},{96,80},{112,96},{128,112},... | collective-permute-start | bytes 49160 | tf_op jit(solution)/shard_map/ppermute | solution.py:12
  55.0 3.1 %collective-permute-done.2 = bf16[64,128]{1,0:T(8,128)(2,1)S(1)} collective-permute-done((bf16[64,128]{1,0:T(8,128)(2,1)S(1)}, bf16[64,128]{1,0:T(8,128)(2,1)S(1)}, u32[]{:S(2)}, u32[]{:S(2)}) %collective-permute-start.2) | collective-permute-done | bytes 16416 | tf_op jit(solution)/shard_map/ppermute | solution.py:12
  58.1 0.2 fusion.23
  58.3 4.4 %fusion.7 = f32[256,1,128]{2,1,0:T(1,128)S(1)} fusion(bf16[1,256,128,128]{3,2,1,0:T(8,128)(2,1)S(1)} %bitcast.54, bf16[256,128,1]{1,0,2:T(8,128)(2,1)S(1)} %fusion.23), kind=kOutput, calls=%fused_computation.9 | convolution fusion | flops 8388608 | bytes 8585216 | tf_op jit(solution)/shard_map/kij,kj->ki/dot_general | solution.py:98
  62.7 1.3 %convolution_convert_fusion = bf16[4096,128]{1,0:T(8,128)(2,1)S(1)} fusion(s32[4096]{0:T(1024)S(1)} %convert.1, f32[256,128]{1,0:T(8,128)S(1)} %bitcast.60), kind=kOutput, calls=%fused_computation.14 | convolution fusion | flops 270041088 | bytes 1196032 | tf_op jit(solution)/shard_map/dot_general | solution.py:102
  64.0 20.2 %all_to_all.10 = bf16[16,256,128]{2,1,0:T(8,128)(2,1)S(1)} all-to-all(bf16[16,256,128]{2,1,0:T(8,128)(2,1)S(1)} %bitcast.55), channel_id=1, replica_groups=mesh['tm'=16,'tile'=16] {'tile'}, dimensions={0} | all-to-all | bytes 2097152 | tf_op jit(solution)/shard_map/all_to_all | solution.py:103
  84.3 9.8 %fusion.15 = bf16[1,2048,128]{2,1,0:T(8,128)(2,1)} fusion(bf16[4096,128]{1,0:T(8,128)(2,1)S(1)} %bitcast.56, s32[2048]{0:T(1024)S(1)} %add_add_fusion, s32[2048]{0:T(1024)S(1)} %bitcast.72), kind=kOutput, calls=%fused_computation.19 | convolution fusion | flops 2156658688 | bytes 1589248 | tf_op jit(solution)/shard_map/dot_general | solution.py:104
  (31 shorter events, 0.1 us)
Async XLA Ops:
  0.0 46.3 %copy-start = (bf16[1,48,128,128]{3,2,1,0:T(8,128)(2,1)S(1)}, bf16[1,48,128,128]{3,2,1,0:T(8,128)(2,1)}, u32[]{:S(2)}) copy-start(bf16[1,48,128,128]{3,2,1,0:T(8,128)(2,1)} %param.18) | copy-start | bytes 4718596
  0.0 2.3 %copy-start.2 = (s32[1,2048,1]{1,2,0:T(1,128)S(1)}, s32[1,2048,1]{1,2,0:T(1,128)}, u32[]{:S(2)}) copy-start(s32[1,2048,1]{1,2,0:T(1,128)} %param.14) | copy-start | bytes 24580
  0.0 2.4 %copy-start.7 = (s32[1,2048]{1,0:T(1,128)S(1)}, s32[1,2048]{1,0:T(1,128)}, u32[]{:S(2)}) copy-start(s32[1,2048]{1,0:T(1,128)} %param.15) | copy-start | bytes 24580
  2.4 5.7 %copy-start.5 = (bf16[1,2048,128]{2,1,0:T(8,128)(2,1)S(1)}, bf16[1,2048,128]{2,1,0:T(8,128)(2,1)}, u32[]{:S(2)}) copy-start(bf16[1,2048,128]{2,1,0:T(8,128)(2,1)} %param.12) | copy-start | bytes 1572868
  2.4 5.7 %copy-start.6 = (bf16[1,2048,128]{2,1,0:T(8,128)(2,1)S(1)}, bf16[1,2048,128]{2,1,0:T(8,128)(2,1)}, u32[]{:S(2)}) copy-start(bf16[1,2048,128]{2,1,0:T(8,128)(2,1)} %param.11) | copy-start | bytes 1572868
  2.4 5.7 %copy-start.8 = (s32[1,2048]{1,0:T(1,128)S(1)}, s32[1,2048]{1,0:T(1,128)}, u32[]{:S(2)}) copy-start(s32[1,2048]{1,0:T(1,128)} %param.13) | copy-start | bytes 24580
  14.4 8.1 %copy-start.1 = (bf16[1,64,128]{2,1,0:T(8,128)(2,1)S(1)}, bf16[1,64,128]{2,1,0:T(8,128)(2,1)}, u32[]{:S(2)}) copy-start(bf16[1,64,128]{2,1,0:T(8,128)(2,1)} %param.21) | copy-start | bytes 49156
  15.7 23.1 %all-to-all-start = ((bf16[16,272,128]{2,1,0:T(8,128)(2,1)}), bf16[16,272,128]{2,1,0:T(8,128)(2,1)S(1)}, u32[]{:S(2)}, u32[]{:S(2)}) async-start(bf16[16,272,128]{2,1,0:T(8,128)(2,1)} %maximum_maximum_fusion), calls=%async_computation | async-start | bytes 2228224 | tf_op jit(solution)/shard_map/all_to_all | solution.py:65
  22.5 32.5 %collective-permute-start.1 = (bf16[64,128]{1,0:T(8,128)(2,1)S(1)}, bf16[64,128]{1,0:T(8,128)(2,1)S(1)}, u32[]{:S(2)}, u32[]{:S(2)}) collective-permute-start(bf16[64,128]{1,0:T(8,128)(2,1)S(1)} %bitcast.64), channel_id=1, source_target_pairs={{16,0},{32,16},{48,32},{64,48},{80,64},{96,80},{112,96},{128,112},... | collective-permute-start | bytes 49160 | tf_op jit(solution)/shard_map/ppermute | solution.py:12
  38.9 19.4 %slice-start = ((s8[8388608]{0:T(1024)(128)(4,1)}), s8[4194304]{0:T(1024)(128)(4,1)S(1)}, s32[]{:S(2)}) async-start(s8[8388608]{0:T(1024)(128)(4,1)} %bitcast.53), calls=%async_computation.2 | async-start | bytes 8388608
  39.7 6.1 %copy-start.3 = (s32[1,256]{1,0:T(1,128)S(1)}, s32[1,256]{1,0:T(1,128)}, u32[]{:S(2)}) copy-start(s32[1,256]{1,0:T(1,128)} %param.17) | copy-start | bytes 3076
  39.7 6.3 %copy-start.9 = (s32[1,48]{1,0:T(1,128)S(1)}, s32[1,48]{1,0:T(1,128)}, u32[]{:S(2)}) copy-start(s32[1,48]{1,0:T(1,128)} %param.20) | copy-start | bytes 580
  39.7 7.4 %copy-start.4 = (s32[1,48]{1,0:T(1,128)S(1)}, s32[1,48]{1,0:T(1,128)}, u32[]{:S(2)}) copy-start(s32[1,48]{1,0:T(1,128)} %param.19) | copy-start | bytes 580
  39.8 18.6 %slice-start.1 = ((s8[8388608]{0:T(1024)(128)(4,1)}), s8[4194304]{0:T(1024)(128)(4,1)S(1)}, s32[]{:S(2)}) async-start(s8[8388608]{0:T(1024)(128)(4,1)} %bitcast.53), calls=%async_computation.3 | async-start | bytes 8388608
  47.3 7.6 %collective-permute-start = (bf16[64,128]{1,0:T(8,128)(2,1)S(1)}, bf16[64,128]{1,0:T(8,128)(2,1)S(1)}, u32[]{:S(2)}, u32[]{:S(2)}) collective-permute-start(bf16[64,128]{1,0:T(8,128)(2,1)S(1)} %convolution_convert_fusion.2), channel_id=1, source_target_pairs={{0,16},{16,32},{32,48},{48,64},{64,80},{80,96},{96,112},{112,128},... | collective-permute-start | bytes 49160 | tf_op jit(solution)/shard_map/ppermute | solution.py:12
  53.0 5.1 %collective-permute-start.2 = (bf16[64,128]{1,0:T(8,128)(2,1)S(1)}, bf16[64,128]{1,0:T(8,128)(2,1)S(1)}, u32[]{:S(2)}, u32[]{:S(2)}) collective-permute-start(bf16[64,128]{1,0:T(8,128)(2,1)S(1)} %convolution_convert_fusion.2), channel_id=1, source_target_pairs={{16,0},{32,16},{48,32},{64,48},{80,64},{96,80},{112,96},{128,112},... | collective-permute-start | bytes 49160 | tf_op jit(solution)/shard_map/ppermute | solution.py:12

commit v2 on v1

--- a/solution.py
+++ b/solution.py
@@ -41,10 +41,16 @@
 
     tile_ids = lax.broadcasted_iota(jnp.int32, (obs_total, tiles), 1)
     names = (tile_ids == target[:, None]).astype(jnp.bfloat16)
-    rows = lax.broadcasted_iota(jnp.int32, (obs_total, obs_total), 0)
-    cols = lax.broadcasted_iota(jnp.int32, (obs_total, obs_total), 1)
+    chunk = 128
+    pieces = obs_total // chunk
+    rows = lax.broadcasted_iota(jnp.int32, (chunk, chunk), 0)
+    cols = lax.broadcasted_iota(jnp.int32, (chunk, chunk), 1)
     lower = (cols <= rows).astype(jnp.bfloat16)
-    counts = jnp.dot(lower, names, preferred_element_type=jnp.float32)
+    names_c = names.reshape(pieces, chunk, tiles)
+    within = jnp.einsum("rc,pct->prt", lower, names_c, preferred_element_type=jnp.float32)
+    totals = within[:, chunk - 1, :]
+    before = jnp.cumsum(totals, axis=0) - totals
+    counts = (within + before[:, None, :]).reshape(obs_total, tiles)
     rank = jnp.sum(counts * names.astype(jnp.float32), axis=1).astype(jnp.int32) - 1
     slot = target * CAP + rank
 
@@ -101,9 +107,7 @@
 
     answer = jnp.dot(binner.T, model_obs, preferred_element_type=jnp.float32).astype(jnp.bfloat16)
     back = lax.all_to_all(answer.reshape(tiles, CAP, block_width), "tile", 0, 0, tiled=True)
-    gathered = jnp.dot(
-        placer.T, back.reshape(slots, block_width), preferred_element_type=jnp.float32
-    )
+    gathered = jnp.take(back.reshape(slots, block_width), slot, axis=0, mode="clip").astype(jnp.float32)
     return (gathered * keeping).astype(jnp.bfloat16)[None]
 
 

time: 95.2 us -> 96.6 us (1.015)
  blocking collectives: 20.2 us -> 0 us
  waiting for transfers between devices: 16.6 us -> 35.1 us
  matrix products: 38.2 us -> 28.7 us
  local copies, waits for them, and re-layouts: 0.26 us -> 6.85 us
  starting transfers between devices: 17.2 us -> 20.9 us
  other arithmetic: 1.32 us -> 4.32 us
    all_to_all x1 -> x0, blocking collectives: 20.2 us -> none  [shards(): lax.all_to_all(answer.reshape(tiles, CAP, block_width), 'tile', 0, 0, til...]
    all_to_all x0 -> x1, waiting for transfers between devices: none -> 18.5 us  [shards(): lax.all_to_all(answer.reshape(tiles, CAP, block_width), 'tile', 0, 0, til...]
    dot_general x2 -> x1, matrix products: 12.1 us -> 0.86 us  [shards(): jnp.einsum('rc,pct->prt', lower, names_c, preferred_element_type=jnp.floa...]
    gather x0 -> x1, local copies, waits for them, and re-layouts: none -> 6.18 us  [shards(): jnp.take(back.reshape(slots, block_width), slot, axis=0, mode='clip')]
    all_to_all x0 -> x1, starting transfers between devices: none -> 3.65 us  [shards(): lax.all_to_all(answer.reshape(tiles, CAP, block_width), 'tile', 0, 0, til...]
    convert_element_type x0 -> x1, other arithmetic: none -> 1.13 us  [shards(): return (gathered * keeping).astype(jnp.bfloat16)[None]]
    dot_general x1, matrix products: 1.29 us -> 2.27 us  [shards(): jnp.dot(binner.T, model_obs, preferred_element_type=jnp.float32)]
  transfers between devices with their start and end apart: 4 -> 5, of which waited for: 2 -> 3; matrix products, arithmetic and copies ran while one was open for 9% -> 9% of each run, Pallas kernels for 0% -> 0%
where the time goes in v2:
time: 96.6 us; the launch traced here: 96.2 us
  waiting for transfers between devices  35.1 us (36%)
  matrix products  28.7 us (30%)
  starting transfers between devices  20.9 us (22%)
  local copies, waits for them, and re-layouts  6.85 us (7%)
  other arithmetic  4.32 us (4%)
    all_to_all x1, waiting for transfers between devices, shards(): lax.all_to_all(answer.reshape(tiles, CAP, block_width), 'tile', 0, 0, til...  18.5 us
    all_to_all x1, waiting for transfers between devices, shards(): recv = lax.all_to_all(send, 'tile', 0, 0, tiled=True)  13.5 us
    ppermute x3, starting transfers between devices, from_behind(): return lax.ppermute(x, axis, pairs)  10.5 us
    all_to_all x1, starting transfers between devices, shards(): recv = lax.all_to_all(send, 'tile', 0, 0, tiled=True)  6.76 us
    dot_general x1, matrix products, shards(): jnp.dot(placer, column.astype(jnp.bfloat16)[:, None], preferred_element_t...  6.37 us
    dot_general x1, matrix products, shards(): jnp.dot(placer, weighted, preferred_element_type=jnp.float32)  6.31 us
    gather x1, local copies, waits for them, and re-layouts, shards(): jnp.take(back.reshape(slots, block_width), slot, axis=0, mode='clip')  6.18 us
    dot_general x1, matrix products, shards(): jnp.einsum('kij,ki->kj', jacobian[0], merged, preferred_element_type=jnp....  6.09 us
  transfers between devices with their start and end apart: 5, of which 3 were waited for; matrix products, arithmetic and copies ran while one was open for 9% of the time, Pallas kernels for 0%

profile of v2, /device:TPU:161, one launch (start us, length us, event | category | flops | bytes accessed | tf_op | source)
XLA Modules:
  0.0 96.2 jit_solution(10105834270330054198)
XLA Ops:
  0.0 0.8 broadcast_multiply_fusion
  0.8 0.9 convolution_bitcast_fusion
  2.2 0.2 subtract_reduce_fusion
  2.4 0.8 multiply_reduce_fusion
  3.2 6.4 %fusion = f32[1,4096]{1,0:T(1,128)S(1)} fusion(s32[2048]{0:T(1024)S(1)} %bitcast_add_fusion.1, s32[1,2048]{1,0:T(1,128)} %param.15), kind=kOutput, calls=%fused_computation.2 | convolution fusion | flops 25167872 | bytes 32768 | tf_op jit(solution)/shard_map/dot_general | solution.py:60
  9.7 6.3 %fusion.8 = bf16[4096,128]{1,0:T(8,128)(2,1)S(1)} fusion(s32[2048]{0:T(1024)S(1)} %bitcast_add_fusion.1, bf16[1,2048,128]{2,1,0:T(8,128)(2,1)S(1)} %copy-done.6, bf16[1,2048,128]{2,1,0:T(8,128)(2,1)S(1)} %copy-done.7, s32[2048]{0:T(1024)S(1)} %bitcast.84), kind=kOutput, calls=%fused_computation.10 | convolution fusion | flops 2157969408 | bytes 2113536 | tf_op jit(solution)/shard_map/dot_general | solution.py:59
  16.0 1.3 %maximum_maximum_fusion = bf16[16,272,128]{2,1,0:T(8,128)(2,1)} fusion(bf16[16,2,128]{2,1,0:T(2,128)(2,1)S(1)} %bitcast.77, bf16[16,256,128]{2,1,0:T(8,128)(2,1)S(1)} %bitcast.71, bf16[272]{0:T(512)(128)(2,1)S(1)} %pad.2.clone), kind=kLoop, calls=%fused_computation.23 | loop fusion | flops 3342336 | bytes 2171424 | tf_op jit(solution)/shard_map/concatenate | solution.py:63
  17.3 6.8 %all-to-all-start = ((bf16[16,272,128]{2,1,0:T(8,128)(2,1)}), bf16[16,272,128]{2,1,0:T(8,128)(2,1)S(1)}, u32[]{:S(2)}, u32[]{:S(2)}) async-start(bf16[16,272,128]{2,1,0:T(8,128)(2,1)} %maximum_maximum_fusion), calls=%async_computation | async-start | bytes 2228224 | tf_op jit(solution)/shard_map/all_to_all | solution.py:71
  24.1 2.9 %collective-permute-start.1 = (bf16[64,128]{1,0:T(8,128)(2,1)S(1)}, bf16[64,128]{1,0:T(8,128)(2,1)S(1)}, u32[]{:S(2)}, u32[]{:S(2)}) collective-permute-start(bf16[64,128]{1,0:T(8,128)(2,1)S(1)} %bitcast.82), channel_id=1, source_target_pairs={{16,0},{32,16},{48,32},{64,48},{80,64},{96,80},{112,96},{128,112},... | collective-permute-start | bytes 49160 | tf_op jit(solution)/shard_map/ppermute | solution.py:12
  27.0 13.5 %all-to-all-done = bf16[16,272,128]{2,1,0:T(8,128)(2,1)S(1)} async-done(((bf16[16,272,128]{2,1,0:T(8,128)(2,1)}), bf16[16,272,128]{2,1,0:T(8,128)(2,1)S(1)}, u32[]{:S(2)}, u32[]{:S(2)}) %all-to-all-start) | async-done | bytes 1114144 | tf_op jit(solution)/shard_map/all_to_all | solution.py:71
  40.6 0.7 fusion.16
  41.4 6.1 %fusion.6 = f32[256,1,128]{2,1,0:T(1,128)S(1)} fusion(bf16[1,256,128,128]{3,2,1,0:T(8,128)(2,1)} %param.16, bf16[256,128,1]{1,0,2:T(8,128)(2,1)S(1)} %fusion.16), kind=kOutput, calls=%fused_computation.8 | convolution fusion | flops 8388608 | bytes 8585216 | tf_op jit(solution)/shard_map/kij,ki->kj/dot_general | solution.py:79
  47.4 0.2 convolution_convert_fusion.3
  47.8 0.9 fusion.12
  48.9 5.7 %collective-permute-start = (bf16[64,128]{1,0:T(8,128)(2,1)S(1)}, bf16[64,128]{1,0:T(8,128)(2,1)S(1)}, u32[]{:S(2)}, u32[]{:S(2)}) collective-permute-start(bf16[64,128]{1,0:T(8,128)(2,1)S(1)} %convolution_convert_fusion.2), channel_id=1, source_target_pairs={{0,16},{16,32},{32,48},{48,64},{64,80},{80,96},{96,112},{112,128},... | collective-permute-start | bytes 49160 | tf_op jit(solution)/shard_map/ppermute | solution.py:12
  54.6 1.9 %collective-permute-start.2 = (bf16[64,128]{1,0:T(8,128)(2,1)S(1)}, bf16[64,128]{1,0:T(8,128)(2,1)S(1)}, u32[]{:S(2)}, u32[]{:S(2)}) collective-permute-start(bf16[64,128]{1,0:T(8,128)(2,1)S(1)} %convolution_convert_fusion.2), channel_id=1, source_target_pairs={{16,0},{32,16},{48,32},{64,48},{80,64},{96,80},{112,96},{128,112},... | collective-permute-start | bytes 49160 | tf_op jit(solution)/shard_map/ppermute | solution.py:12
  56.6 3.1 %collective-permute-done.2 = bf16[64,128]{1,0:T(8,128)(2,1)S(1)} collective-permute-done((bf16[64,128]{1,0:T(8,128)(2,1)S(1)}, bf16[64,128]{1,0:T(8,128)(2,1)S(1)}, u32[]{:S(2)}, u32[]{:S(2)}) %collective-permute-start.2) | collective-permute-done | bytes 16416 | tf_op jit(solution)/shard_map/ppermute | solution.py:12
  59.7 0.2 fusion.15
  59.9 4.4 %fusion.4 = f32[256,1,128]{2,1,0:T(1,128)S(1)} fusion(bf16[1,256,128,128]{3,2,1,0:T(8,128)(2,1)S(1)} %bitcast.67, bf16[256,128,1]{1,0,2:T(8,128)(2,1)S(1)} %fusion.15), kind=kOutput, calls=%fused_computation.6 | convolution fusion | flops 8388608 | bytes 8585216 | tf_op jit(solution)/shard_map/kij,kj->ki/dot_general | solution.py:104
  64.3 2.3 %convolution_convert_fusion = bf16[4096,128]{1,0:T(8,128)(2,1)} fusion(s32[4096]{0:T(1024)S(1)} %convert.2, f32[256,128]{1,0:T(8,128)S(1)} %bitcast.73), kind=kOutput, calls=%fused_computation.11 | convolution fusion | flops 270041088 | bytes 1196032 | tf_op jit(solution)/shard_map/dot_general | solution.py:108
  66.6 3.7 %all-to-all-start.1 = ((bf16[16,256,128]{2,1,0:T(8,128)(2,1)}), bf16[16,256,128]{2,1,0:T(8,128)(2,1)S(1)}, u32[]{:S(2)}, u32[]{:S(2)}) async-start(bf16[16,256,128]{2,1,0:T(8,128)(2,1)} %bitcast.69), calls=%async_computation.1 | async-start | bytes 2097152 | tf_op jit(solution)/shard_map/all_to_all | solution.py:109
  70.3 18.5 %all-to-all-done.1 = bf16[16,256,128]{2,1,0:T(8,128)(2,1)S(1)} async-done(((bf16[16,256,128]{2,1,0:T(8,128)(2,1)}), bf16[16,256,128]{2,1,0:T(8,128)(2,1)S(1)}, u32[]{:S(2)}, u32[]{:S(2)}) %all-to-all-start.1) | async-done | bytes 1048608 | tf_op jit(solution)/shard_map/all_to_all | solution.py:109
  88.9 6.2 %gather_fusion = bf16[2048,128]{1,0:T(8,128)(2,1)S(1)} fusion(bf16[4096,128]{1,0:T(8,128)(2,1)S(1)} %bitcast.68, s32[2048]{0:T(1024)S(1)} %broadcast_clamp_fusion), kind=kCustom, calls=%fused_computation | custom fusion | bytes 1056768 | tf_op jit(solution)/shard_map/jit(_take)/gather | solution.py:110
  95.0 1.1 %fusion.18 = bf16[1,2048,128]{2,1,0:T(8,128)(2,1)} fusion(bf16[2048,128]{1,0:T(8,128)(2,1)S(1)} %gather_fusion, s32[2048]{0:T(1024)S(1)} %bitcast.85), kind=kLoop, calls=%fused_computation.29 | loop fusion | flops 1048576 | bytes 1056768 | tf_op jit(solution)/shard_map/convert_element_type | solution.py:111
  (41 shorter events, 1.1 us)
Async XLA Ops:
  0.0 47.8 %copy-start = (bf16[1,48,128,128]{3,2,1,0:T(8,128)(2,1)S(1)}, bf16[1,48,128,128]{3,2,1,0:T(8,128)(2,1)}, u32[]{:S(2)}) copy-start(bf16[1,48,128,128]{3,2,1,0:T(8,128)(2,1)} %param.18) | copy-start | bytes 4718596
  3.2 6.5 %copy-start.3 = (s32[1,2048]{1,0:T(1,128)S(1)}, s32[1,2048]{1,0:T(1,128)}, u32[]{:S(2)}) copy-start(s32[1,2048]{1,0:T(1,128)} %param.13) | copy-start | bytes 24580
  3.2 6.5 %copy-start.6 = (bf16[1,2048,128]{2,1,0:T(8,128)(2,1)S(1)}, bf16[1,2048,128]{2,1,0:T(8,128)(2,1)}, u32[]{:S(2)}) copy-start(bf16[1,2048,128]{2,1,0:T(8,128)(2,1)} %param.12) | copy-start | bytes 1572868
  3.2 6.5 %copy-start.7 = (bf16[1,2048,128]{2,1,0:T(8,128)(2,1)S(1)}, bf16[1,2048,128]{2,1,0:T(8,128)(2,1)}, u32[]{:S(2)}) copy-start(bf16[1,2048,128]{2,1,0:T(8,128)(2,1)} %param.11) | copy-start | bytes 1572868
  16.0 8.1 %copy-start.2 = (bf16[1,64,128]{2,1,0:T(8,128)(2,1)S(1)}, bf16[1,64,128]{2,1,0:T(8,128)(2,1)}, u32[]{:S(2)}) copy-start(bf16[1,64,128]{2,1,0:T(8,128)(2,1)} %param.21) | copy-start | bytes 49156
  17.3 23.1 %all-to-all-start = ((bf16[16,272,128]{2,1,0:T(8,128)(2,1)}), bf16[16,272,128]{2,1,0:T(8,128)(2,1)S(1)}, u32[]{:S(2)}, u32[]{:S(2)}) async-start(bf16[16,272,128]{2,1,0:T(8,128)(2,1)} %maximum_maximum_fusion), calls=%async_computation | async-start | bytes 2228224 | tf_op jit(solution)/shard_map/all_to_all | solution.py:71
  24.1 32.5 %collective-permute-start.1 = (bf16[64,128]{1,0:T(8,128)(2,1)S(1)}, bf16[64,128]{1,0:T(8,128)(2,1)S(1)}, u32[]{:S(2)}, u32[]{:S(2)}) collective-permute-start(bf16[64,128]{1,0:T(8,128)(2,1)S(1)} %bitcast.82), channel_id=1, source_target_pairs={{16,0},{32,16},{48,32},{64,48},{80,64},{96,80},{112,96},{128,112},... | collective-permute-start | bytes 49160 | tf_op jit(solution)/shard_map/ppermute | solution.py:12
  40.5 19.4 %slice-start = ((s8[8388608]{0:T(1024)(128)(4,1)}), s8[4194304]{0:T(1024)(128)(4,1)S(1)}, s32[]{:S(2)}) async-start(s8[8388608]{0:T(1024)(128)(4,1)} %bitcast.66), calls=%async_computation.2 | async-start | bytes 8388608
  41.3 6.1 %copy-start.4 = (s32[1,256]{1,0:T(1,128)S(1)}, s32[1,256]{1,0:T(1,128)}, u32[]{:S(2)}) copy-start(s32[1,256]{1,0:T(1,128)} %param.17) | copy-start | bytes 3076
  41.3 6.3 %copy-start.8 = (s32[1,48]{1,0:T(1,128)S(1)}, s32[1,48]{1,0:T(1,128)}, u32[]{:S(2)}) copy-start(s32[1,48]{1,0:T(1,128)} %param.20) | copy-start | bytes 580
  41.3 7.4 %copy-start.5 = (s32[1,48]{1,0:T(1,128)S(1)}, s32[1,48]{1,0:T(1,128)}, u32[]{:S(2)}) copy-start(s32[1,48]{1,0:T(1,128)} %param.19) | copy-start | bytes 580
  41.3 18.6 %slice-start.1 = ((s8[8388608]{0:T(1024)(128)(4,1)}), s8[4194304]{0:T(1024)(128)(4,1)S(1)}, s32[]{:S(2)}) async-start(s8[8388608]{0:T(1024)(128)(4,1)} %bitcast.66), calls=%async_computation.3 | async-start | bytes 8388608
  48.9 7.6 %collective-permute-start = (bf16[64,128]{1,0:T(8,128)(2,1)S(1)}, bf16[64,128]{1,0:T(8,128)(2,1)S(1)}, u32[]{:S(2)}, u32[]{:S(2)}) collective-permute-start(bf16[64,128]{1,0:T(8,128)(2,1)S(1)} %convolution_convert_fusion.2), channel_id=1, source_target_pairs={{0,16},{16,32},{32,48},{48,64},{64,80},{80,96},{96,112},{112,128},... | collective-permute-start | bytes 49160 | tf_op jit(solution)/shard_map/ppermute | solution.py:12
  54.6 5.1 %collective-permute-start.2 = (bf16[64,128]{1,0:T(8,128)(2,1)S(1)}, bf16[64,128]{1,0:T(8,128)(2,1)S(1)}, u32[]{:S(2)}, u32[]{:S(2)}) collective-permute-start(bf16[64,128]{1,0:T(8,128)(2,1)S(1)} %convolution_convert_fusion.2), channel_id=1, source_target_pairs={{16,0},{32,16},{48,32},{64,48},{80,64},{96,80},{112,96},{128,112},... | collective-permute-start | bytes 49160 | tf_op jit(solution)/shard_map/ppermute | solution.py:12
  59.9 10.4 %copy-start.1 = (s32[1,2048,1]{1,2,0:T(1,128)S(1)}, s32[1,2048,1]{1,2,0:T(1,128)}, u32[]{:S(2)}) copy-start(s32[1,2048,1]{1,2,0:T(1,128)} %param.14) | copy-start | bytes 24580
  66.6 22.3 %all-to-all-start.1 = ((bf16[16,256,128]{2,1,0:T(8,128)(2,1)}), bf16[16,256,128]{2,1,0:T(8,128)(2,1)S(1)}, u32[]{:S(2)}, u32[]{:S(2)}) async-start(bf16[16,256,128]{2,1,0:T(8,128)(2,1)} %bitcast.69), calls=%async_computation.1 | async-start | bytes 2097152 | tf_op jit(solution)/shard_map/all_to_all | solution.py:109

commit v3 on v2

--- a/solution.py
+++ b/solution.py
@@ -57,8 +57,10 @@
     slot_ids = lax.broadcasted_iota(jnp.int32, (slots, obs_total), 0)
     placer = (slot_ids == slot[None, :]).astype(jnp.bfloat16)
     packed = jnp.dot(placer, weighted, preferred_element_type=jnp.float32).astype(jnp.bfloat16)
+    rank_ids = lax.broadcasted_iota(jnp.int32, (obs_total, CAP), 1)
+    ranked = (rank_ids == rank[:, None]).astype(jnp.bfloat16)
     packed_col = jnp.dot(
-        placer, column.astype(jnp.bfloat16)[:, None], preferred_element_type=jnp.float32
+        (names * column.astype(jnp.bfloat16)[:, None]).T, ranked, preferred_element_type=jnp.float32
     ).astype(jnp.bfloat16)
     send = jnp.concatenate(
         [
@@ -76,7 +78,19 @@
     summed = jnp.dot(binner, recv_rows, preferred_element_type=jnp.float32)
 
     merged = summed.astype(jnp.bfloat16)
-    spread = jnp.einsum("kij,ki->kj", jacobian[0], merged, preferred_element_type=jnp.float32)
+    group = 16
+    groups = jac_total // group
+    jac_groups = jacobian[0].reshape(groups, group * block_width, block_width)
+    eye = (
+        lax.broadcasted_iota(jnp.int32, (group, group), 0)
+        == lax.broadcasted_iota(jnp.int32, (group, group), 1)
+    ).astype(jnp.bfloat16)
+    spread_left = (
+        merged.reshape(groups, group, 1, block_width) * eye[None, :, :, None]
+    ).reshape(groups, group, group * block_width)
+    spread = jnp.einsum(
+        "gkr,grj->gkj", spread_left, jac_groups, preferred_element_type=jnp.float32
+    ).reshape(jac_total, block_width)
     state_ids = lax.broadcasted_iota(jnp.int32, (state_total, jac_total), 0)
     owners = state_ids == jac_state[0][None, :]
     state = jnp.dot(owners.astype(jnp.float32), spread, precision=lax.Precision.HIGHEST).astype(
@@ -101,9 +115,17 @@
     local_state = jnp.dot(
         owners.T.astype(jnp.bfloat16), coupled, preferred_element_type=jnp.float32
     ).astype(jnp.bfloat16)
-    model_obs = jnp.einsum(
-        "kij,kj->ki", jacobian[0], local_state, preferred_element_type=jnp.float32
-    ).astype(jnp.bfloat16)
+    wide = jnp.einsum(
+        "gkj,grj->gkr",
+        local_state.reshape(groups, group, block_width),
+        jac_groups,
+        preferred_element_type=jnp.float32,
+    ).reshape(groups, group, group, block_width)
+    model_obs = (
+        jnp.sum(wide * eye.astype(jnp.float32)[None, :, :, None], axis=2)
+        .reshape(jac_total, block_width)
+        .astype(jnp.bfloat16)
+    )
 
     answer = jnp.dot(binner.T, model_obs, preferred_element_type=jnp.float32).astype(jnp.bfloat16)
     back = lax.all_to_all(answer.reshape(tiles, CAP, block_width), "tile", 0, 0, tiled=True)

time: 96.6 us -> 93 us (0.963)
  matrix products: 28.7 us -> 20.7 us
  local copies, waits for them, and re-layouts: 6.85 us -> 10 us
  other arithmetic: 4.32 us -> 5.57 us
    dot_general x3, matrix products: 16.9 us -> 8.91 us  [the longest x1 4.74 us: shards(): jnp.einsum('gkr,grj->gkj', spread_left, jac_groups, preferred_element_typ...]
    mul x0 -> x3, local copies, waits for them, and re-layouts: none -> 2.74 us  [shards(): merged.reshape(groups, group, 1, block_width) * eye[None, :, :, None]]
  transfers between devices with their start and end apart: 5 -> 5, of which waited for: 3 -> 3; matrix products, arithmetic and copies ran while one was open for 9% -> 11% of each run, Pallas kernels for 0% -> 0%
where the time goes in v3:
time: 93 us; the launch traced here: 92.5 us
  waiting for transfers between devices  34.8 us (37%)
  starting transfers between devices  21 us (23%)
  matrix products  20.7 us (22%)
  local copies, waits for them, and re-layouts  10 us (11%)
  other arithmetic  5.57 us (6%)
    all_to_all x1, waiting for transfers between devices, shards(): lax.all_to_all(answer.reshape(tiles, CAP, block_width), 'tile', 0, 0, til...  18.5 us
    all_to_all x1, waiting for transfers between devices, shards(): recv = lax.all_to_all(send, 'tile', 0, 0, tiled=True)  13.3 us
    ppermute x3, starting transfers between devices, from_behind(): return lax.ppermute(x, axis, pairs)  10.6 us
    all_to_all x1, starting transfers between devices, shards(): recv = lax.all_to_all(send, 'tile', 0, 0, tiled=True)  6.75 us
    gather x1, local copies, waits for them, and re-layouts, shards(): jnp.take(back.reshape(slots, block_width), slot, axis=0, mode='clip')  6.18 us
    dot_general x1, matrix products, shards(): jnp.dot(placer, weighted, preferred_element_type=jnp.float32)  6.13 us
    dot_general x1, matrix products, shards(): jnp.einsum('gkr,grj->gkj', spread_left, jac_groups, preferred_element_typ...  4.74 us
    all_to_all x1, starting transfers between devices, shards(): lax.all_to_all(answer.reshape(tiles, CAP, block_width), 'tile', 0, 0, til...  3.65 us
  transfers between devices with their start and end apart: 5, of which 3 were waited for; matrix products, arithmetic and copies ran while one was open for 11% of the time, Pallas kernels for 0%

profile of v3, /device:TPU:161, one launch (start us, length us, event | category | flops | bytes accessed | tf_op | source)
XLA Modules:
  0.0 92.5 jit_solution(87613084334582889)
XLA Ops:
  0.0 1.0 %convolution_bitcast_fusion = f32[16,128,16]{1,2,0:T(8,128)S(1)} fusion(s32[16,128]{1,0:T(8,128)} %bitcast.86), kind=kOutput, calls=%fused_computation.16 | convolution fusion | flops 8437760 | bytes 139264 | tf_op jit(solution)/shard_map/rc,pct->prt/dot_general | solution.py:50
  1.7 0.8 multiply_reduce_fusion
  2.5 0.7 multiply_add_fusion
  3.2 0.7 convert_reduce_fusion
  4.0 1.9 %fusion.12 = bf16[16,256]{1,0:T(8,128)(2,1)S(1)} fusion(s32[2048]{0:T(1024)S(1)} %get-tuple-element.6, s32[2048]{0:T(1024)} %bitcast.89, bf16[2048]{0:T(1024)(128)(2,1)S(1)} %convert_reduce_fusion), kind=kOutput, calls=%fused_computation.24 | convolution fusion | flops 17371136 | bytes 28672 | tf_op jit(solution)/shard_map/dot_general | solution.py:62
  6.0 6.1 %fusion.2 = bf16[4096,128]{1,0:T(8,128)(2,1)S(1)} fusion(s32[2048]{0:T(1024)S(1)} %multiply_add_fusion, bf16[1,2048,128]{2,1,0:T(8,128)(2,1)S(1)} %copy-done.6, bf16[1,2048,128]{2,1,0:T(8,128)(2,1)S(1)} %copy-done.7, s32[2048]{0:T(1024)S(1)} %bitcast.97), kind=kOutput, calls=%fused_computation.4 | convolution fusion | flops 2157969408 | bytes 2113536 | tf_op jit(solution)/shard_map/dot_general | solution.py:59
  12.1 1.3 %maximum_maximum_fusion = bf16[16,272,128]{2,1,0:T(8,128)(2,1)} fusion(bf16[16,2,128]{2,1,0:T(2,128)(2,1)S(1)} %reshape.183, bf16[16,256,128]{2,1,0:T(8,128)(2,1)S(1)} %bitcast.81, bf16[272]{0:T(512)(128)(2,1)S(1)} %pad.2.clone), kind=kLoop, calls=%fused_computation.19 | loop fusion | flops 3342336 | bytes 2171424 | tf_op jit(solution)/shard_map/concatenate | solution.py:65
  13.4 6.8 %all-to-all-start = ((bf16[16,272,128]{2,1,0:T(8,128)(2,1)}), bf16[16,272,128]{2,1,0:T(8,128)(2,1)S(1)}, u32[]{:S(2)}, u32[]{:S(2)}) async-start(bf16[16,272,128]{2,1,0:T(8,128)(2,1)} %maximum_maximum_fusion), calls=%async_computation | async-start | bytes 2228224 | tf_op jit(solution)/shard_map/all_to_all | solution.py:73
  20.2 2.9 %collective-permute-start.1 = (bf16[64,128]{1,0:T(8,128)(2,1)S(1)}, bf16[64,128]{1,0:T(8,128)(2,1)S(1)}, u32[]{:S(2)}, u32[]{:S(2)}) collective-permute-start(bf16[64,128]{1,0:T(8,128)(2,1)S(1)} %bitcast.96), channel_id=1, source_target_pairs={{16,0},{32,16},{48,32},{64,48},{80,64},{96,80},{112,96},{128,112},... | collective-permute-start | bytes 49160 | tf_op jit(solution)/shard_map/ppermute | solution.py:12
  23.2 13.3 %all-to-all-done = bf16[16,272,128]{2,1,0:T(8,128)(2,1)S(1)} async-done(((bf16[16,272,128]{2,1,0:T(8,128)(2,1)}), bf16[16,272,128]{2,1,0:T(8,128)(2,1)S(1)}, u32[]{:S(2)}, u32[]{:S(2)}) %all-to-all-start) | async-done | bytes 1114144 | tf_op jit(solution)/shard_map/all_to_all | solution.py:73
  36.7 0.7 fusion.10
  37.4 1.1 %mul.93 = bf16[16,16,16,128]{3,2,1,0:T(8,128)(2,1)} broadcast(bf16[16,16,128]{2,1,0:T(8,128)(2,1)S(1)} %bitcast.92), dimensions={0,1,3} | broadcast | bytes 1114112 | tf_op jit(solution)/shard_map/mul | solution.py:89
  38.5 1.5 %mul.94 = bf16[16,16,2048]{2,1,0:T(8,128)(2,1)S(1)} reshape(bf16[16,16,16,128]{3,2,1,0:T(8,128)(2,1)} %mul.93) | data formatting | bytes 2097152 | tf_op jit(solution)/shard_map/mul | solution.py:89
  40.1 4.7 %fusion.15 = f32[16,16,128]{2,1,0:T(8,128)S(1)} fusion(bf16[16,2048,128]{2,1,0:T(8,128)(2,1)} %bitcast.72, bf16[16,16,2048]{2,1,0:T(8,128)(2,1)S(1)} %mul.94, bf16[16,2048]{1,0:T(8,128)(2,1)S(1)} %bitcast.83), kind=kOutput, calls=%fused_computation.29 | convolution fusion | flops 134742016 | bytes 9633792 | tf_op jit(solution)/shard_map/gkr,grj->gkj/dot_general | solution.py:91
  45.2 0.9 fusion.8
  46.3 5.7 %collective-permute-start = (bf16[64,128]{1,0:T(8,128)(2,1)S(1)}, bf16[64,128]{1,0:T(8,128)(2,1)S(1)}, u32[]{:S(2)}, u32[]{:S(2)}) collective-permute-start(bf16[64,128]{1,0:T(8,128)(2,1)S(1)} %convolution_convert_fusion.2), channel_id=1, source_target_pairs={{0,16},{16,32},{32,48},{48,64},{64,80},{80,96},{96,112},{112,128},... | collective-permute-start | bytes 49160 | tf_op jit(solution)/shard_map/ppermute | solution.py:12
  52.0 2.1 %collective-permute-start.2 = (bf16[64,128]{1,0:T(8,128)(2,1)S(1)}, bf16[64,128]{1,0:T(8,128)(2,1)S(1)}, u32[]{:S(2)}, u32[]{:S(2)}) collective-permute-start(bf16[64,128]{1,0:T(8,128)(2,1)S(1)} %convolution_convert_fusion.2), channel_id=1, source_target_pairs={{16,0},{32,16},{48,32},{64,48},{80,64},{96,80},{112,96},{128,112},... | collective-permute-start | bytes 49160 | tf_op jit(solution)/shard_map/ppermute | solution.py:12
  54.2 2.9 %collective-permute-done.2 = bf16[64,128]{1,0:T(8,128)(2,1)S(1)} collective-permute-done((bf16[64,128]{1,0:T(8,128)(2,1)S(1)}, bf16[64,128]{1,0:T(8,128)(2,1)S(1)}, u32[]{:S(2)}, u32[]{:S(2)}) %collective-permute-start.2) | collective-permute-done | bytes 16416 | tf_op jit(solution)/shard_map/ppermute | solution.py:12
  57.3 2.3 %fusion.43 = f32[16,16,2048]{2,1,0:T(8,128)S(1)} fusion(bf16[16,16,128]{2,1,0:T(8,128)(2,1)S(1)} %bitcast.84, bf16[16,2048,128]{2,1,0:T(8,128)(2,1)S(1)} %bitcast.75), kind=kOutput, calls=%fused_computation.72 | convolution fusion | flops 134217728 | bytes 10551296 | tf_op jit(solution)/shard_map/gkj,grj->gkr/dot_general | solution.py:118
  60.7 2.3 %convolution_convert_fusion = bf16[4096,128]{1,0:T(8,128)(2,1)} fusion(bf16[256,128]{1,0:T(8,128)(2,1)S(1)} %bitcast.91, s32[4096]{0:T(1024)S(1)} %convert.2), kind=kOutput, calls=%fused_computation.5 | convolution fusion | flops 270008320 | bytes 1130496 | tf_op jit(solution)/shard_map/dot_general | solution.py:130
  62.9 3.7 %all-to-all-start.1 = ((bf16[16,256,128]{2,1,0:T(8,128)(2,1)}), bf16[16,256,128]{2,1,0:T(8,128)(2,1)S(1)}, u32[]{:S(2)}, u32[]{:S(2)}) async-start(bf16[16,256,128]{2,1,0:T(8,128)(2,1)} %bitcast.79), calls=%async_computation.1 | async-start | bytes 2097152 | tf_op jit(solution)/shard_map/all_to_all | solution.py:131
  66.6 18.5 %all-to-all-done.1 = bf16[16,256,128]{2,1,0:T(8,128)(2,1)S(1)} async-done(((bf16[16,256,128]{2,1,0:T(8,128)(2,1)}), bf16[16,256,128]{2,1,0:T(8,128)(2,1)S(1)}, u32[]{:S(2)}, u32[]{:S(2)}) %all-to-all-start.1) | async-done | bytes 1048608 | tf_op jit(solution)/shard_map/all_to_all | solution.py:131
  85.1 6.2 %gather_fusion = bf16[2048,128]{1,0:T(8,128)(2,1)S(1)} fusion(bf16[4096,128]{1,0:T(8,128)(2,1)S(1)} %bitcast.76, s32[2048]{0:T(1024)S(1)} %broadcast_clamp_fusion), kind=kCustom, calls=%fused_computation | custom fusion | bytes 1056768 | tf_op jit(solution)/shard_map/jit(_take)/gather | solution.py:132
  91.3 1.1 %fusion.13 = bf16[1,2048,128]{2,1,0:T(8,128)(2,1)} fusion(bf16[2048,128]{1,0:T(8,128)(2,1)S(1)} %gather_fusion, s32[2048]{0:T(1024)S(1)} %bitcast.98), kind=kLoop, calls=%fused_computation.26 | loop fusion | flops 1048576 | bytes 1056768 | tf_op jit(solution)/shard_map/convert_element_type | solution.py:133
  (49 shorter events, 2.9 us)
Async XLA Ops:
  0.0 45.2 %copy-start = (bf16[1,48,128,128]{3,2,1,0:T(8,128)(2,1)S(1)}, bf16[1,48,128,128]{3,2,1,0:T(8,128)(2,1)}, u32[]{:S(2)}) copy-start(bf16[1,48,128,128]{3,2,1,0:T(8,128)(2,1)} %param.18) | copy-start | bytes 4718596
  0.0 6.0 %copy-start.3 = (s32[1,2048]{1,0:T(1,128)S(1)}, s32[1,2048]{1,0:T(1,128)}, u32[]{:S(2)}) copy-start(s32[1,2048]{1,0:T(1,128)} %param.13) | copy-start | bytes 24580
  0.0 6.0 %copy-start.7 = (bf16[1,2048,128]{2,1,0:T(8,128)(2,1)S(1)}, bf16[1,2048,128]{2,1,0:T(8,128)(2,1)}, u32[]{:S(2)}) copy-start(bf16[1,2048,128]{2,1,0:T(8,128)(2,1)} %param.11) | copy-start | bytes 1572868
  0.0 6.0 %copy-start.6 = (bf16[1,2048,128]{2,1,0:T(8,128)(2,1)S(1)}, bf16[1,2048,128]{2,1,0:T(8,128)(2,1)}, u32[]{:S(2)}) copy-start(bf16[1,2048,128]{2,1,0:T(8,128)(2,1)} %param.12) | copy-start | bytes 1572868
  12.1 8.1 %copy-start.2 = (bf16[1,64,128]{2,1,0:T(8,128)(2,1)S(1)}, bf16[1,64,128]{2,1,0:T(8,128)(2,1)}, u32[]{:S(2)}) copy-start(bf16[1,64,128]{2,1,0:T(8,128)(2,1)} %param.21) | copy-start | bytes 49156
  13.4 23.1 %all-to-all-start = ((bf16[16,272,128]{2,1,0:T(8,128)(2,1)}), bf16[16,272,128]{2,1,0:T(8,128)(2,1)S(1)}, u32[]{:S(2)}, u32[]{:S(2)}) async-start(bf16[16,272,128]{2,1,0:T(8,128)(2,1)} %maximum_maximum_fusion), calls=%async_computation | async-start | bytes 2228224 | tf_op jit(solution)/shard_map/all_to_all | solution.py:73
  20.2 34.0 %collective-permute-start.1 = (bf16[64,128]{1,0:T(8,128)(2,1)S(1)}, bf16[64,128]{1,0:T(8,128)(2,1)S(1)}, u32[]{:S(2)}, u32[]{:S(2)}) collective-permute-start(bf16[64,128]{1,0:T(8,128)(2,1)S(1)} %bitcast.96), channel_id=1, source_target_pairs={{16,0},{32,16},{48,32},{64,48},{80,64},{96,80},{112,96},{128,112},... | collective-permute-start | bytes 49160 | tf_op jit(solution)/shard_map/ppermute | solution.py:12
  40.0 17.3 %slice-start = ((s8[8388608]{0:T(1024)(128)(4,1)}), s8[4194304]{0:T(1024)(128)(4,1)S(1)}, s32[]{:S(2)}) async-start(s8[8388608]{0:T(1024)(128)(4,1)} %bitcast.73), calls=%async_computation.2 | async-start | bytes 8388608
  40.0 4.8 %copy-start.4 = (s32[1,256]{1,0:T(1,128)S(1)}, s32[1,256]{1,0:T(1,128)}, u32[]{:S(2)}) copy-start(s32[1,256]{1,0:T(1,128)} %param.17) | copy-start | bytes 3076
  40.1 5.0 %copy-start.8 = (s32[1,48]{1,0:T(1,128)S(1)}, s32[1,48]{1,0:T(1,128)}, u32[]{:S(2)}) copy-start(s32[1,48]{1,0:T(1,128)} %param.20) | copy-start | bytes 580
  40.1 6.1 %copy-start.5 = (s32[1,48]{1,0:T(1,128)S(1)}, s32[1,48]{1,0:T(1,128)}, u32[]{:S(2)}) copy-start(s32[1,48]{1,0:T(1,128)} %param.19) | copy-start | bytes 580
  40.1 17.2 %slice-start.1 = ((s8[8388608]{0:T(1024)(128)(4,1)}), s8[4194304]{0:T(1024)(128)(4,1)S(1)}, s32[]{:S(2)}) async-start(s8[8388608]{0:T(1024)(128)(4,1)} %bitcast.73), calls=%async_computation.3 | async-start | bytes 8388608
  46.3 7.8 %collective-permute-start = (bf16[64,128]{1,0:T(8,128)(2,1)S(1)}, bf16[64,128]{1,0:T(8,128)(2,1)S(1)}, u32[]{:S(2)}, u32[]{:S(2)}) collective-permute-start(bf16[64,128]{1,0:T(8,128)(2,1)S(1)} %convolution_convert_fusion.2), channel_id=1, source_target_pairs={{0,16},{16,32},{32,48},{48,64},{64,80},{80,96},{96,112},{112,128},... | collective-permute-start | bytes 49160 | tf_op jit(solution)/shard_map/ppermute | solution.py:12
  52.0 5.1 %collective-permute-start.2 = (bf16[64,128]{1,0:T(8,128)(2,1)S(1)}, bf16[64,128]{1,0:T(8,128)(2,1)S(1)}, u32[]{:S(2)}, u32[]{:S(2)}) collective-permute-start(bf16[64,128]{1,0:T(8,128)(2,1)S(1)} %convolution_convert_fusion.2), channel_id=1, source_target_pairs={{16,0},{32,16},{48,32},{64,48},{80,64},{96,80},{112,96},{128,112},... | collective-permute-start | bytes 49160 | tf_op jit(solution)/shard_map/ppermute | solution.py:12
  60.6 5.9 %copy-start.1 = (s32[1,2048,1]{1,2,0:T(1,128)S(1)}, s32[1,2048,1]{1,2,0:T(1,128)}, u32[]{:S(2)}) copy-start(s32[1,2048,1]{1,2,0:T(1,128)} %param.14) | copy-start | bytes 24580
  62.9 22.2 %all-to-all-start.1 = ((bf16[16,256,128]{2,1,0:T(8,128)(2,1)}), bf16[16,256,128]{2,1,0:T(8,128)(2,1)S(1)}, u32[]{:S(2)}, u32[]{:S(2)}) async-start(bf16[16,256,128]{2,1,0:T(8,128)(2,1)} %bitcast.79), calls=%async_computation.1 | async-start | bytes 2097152 | tf_op jit(solution)/shard_map/all_to_all | solution.py:131

commit v4 on v3

--- a/solution.py
+++ b/solution.py
@@ -85,9 +85,13 @@
         lax.broadcasted_iota(jnp.int32, (group, group), 0)
         == lax.broadcasted_iota(jnp.int32, (group, group), 1)
     ).astype(jnp.bfloat16)
-    spread_left = (
-        merged.reshape(groups, group, 1, block_width) * eye[None, :, :, None]
-    ).reshape(groups, group, group * block_width)
+    block_of = lax.broadcasted_iota(jnp.int32, (groups, group, group * block_width), 2) // block_width
+    own_block = lax.broadcasted_iota(jnp.int32, (groups, group, group * block_width), 1)
+    spread_left = jnp.where(
+        block_of == own_block,
+        jnp.tile(merged.reshape(groups, group, block_width), (1, 1, group)),
+        jnp.zeros((), jnp.bfloat16),
+    )
     spread = jnp.einsum(
         "gkr,grj->gkj", spread_left, jac_groups, preferred_element_type=jnp.float32
     ).reshape(jac_total, block_width)

time: 93 us -> 93 us (level)
    mul x3 -> x0, local copies, waits for them, and re-layouts: 2.74 us -> none  [shards(): merged.reshape(groups, group, 1, block_width) * eye[None, :, :, None]]
    another operation x0 -> x2, local copies, waits for them, and re-layouts: none -> 2.64 us  [shards(): jnp.tile(merged.reshape(groups, group, block_width), (1, 1, group))]
where the time goes in v4:
time: 93 us; the launch traced here: 92.5 us
  waiting for transfers between devices  34.9 us (38%)
  starting transfers between devices  21 us (23%)
  matrix products  20.8 us (22%)
  local copies, waits for them, and re-layouts  9.89 us (11%)
  other arithmetic  5.57 us (6%)
    all_to_all x1, waiting for transfers between devices, shards(): lax.all_to_all(answer.reshape(tiles, CAP, block_width), 'tile', 0, 0, til...  18.5 us
    all_to_all x1, waiting for transfers between devices, shards(): recv = lax.all_to_all(send, 'tile', 0, 0, tiled=True)  13.5 us
    ppermute x3, starting transfers between devices, from_behind(): return lax.ppermute(x, axis, pairs)  10.6 us
    all_to_all x1, starting transfers between devices, shards(): recv = lax.all_to_all(send, 'tile', 0, 0, tiled=True)  6.75 us
    gather x1, local copies, waits for them, and re-layouts, shards(): jnp.take(back.reshape(slots, block_width), slot, axis=0, mode='clip')  6.17 us
    dot_general x1, matrix products, shards(): jnp.dot(placer, weighted, preferred_element_type=jnp.float32)  6.13 us
    dot_general x1, matrix products, shards(): jnp.einsum('gkr,grj->gkj', spread_left, jac_groups, preferred_element_typ...  4.81 us
    all_to_all x1, starting transfers between devices, shards(): lax.all_to_all(answer.reshape(tiles, CAP, block_width), 'tile', 0, 0, til...  3.65 us
  transfers between devices with their start and end apart: 5, of which 3 were waited for; matrix products, arithmetic and copies ran while one was open for 11% of the time, Pallas kernels for 0%

profile of v4, /device:TPU:161, one launch (start us, length us, event | category | flops | bytes accessed | tf_op | source)
XLA Modules:
  0.0 92.5 jit_solution(8372824943941729277)
XLA Ops:
  0.0 1.0 %convolution_bitcast_fusion = f32[16,128,16]{1,2,0:T(8,128)S(1)} fusion(s32[16,128]{1,0:T(8,128)} %bitcast.80), kind=kOutput, calls=%fused_computation.18 | convolution fusion | flops 8437760 | bytes 139264 | tf_op jit(solution)/shard_map/rc,pct->prt/dot_general | solution.py:50
  1.7 0.8 multiply_reduce_fusion
  2.5 0.7 multiply_add_fusion
  3.2 0.7 convert_reduce_fusion
  4.0 1.9 %fusion.13 = bf16[16,256]{1,0:T(8,128)(2,1)S(1)} fusion(s32[2048]{0:T(1024)S(1)} %get-tuple-element.6, s32[2048]{0:T(1024)} %bitcast.83, bf16[2048]{0:T(1024)(128)(2,1)S(1)} %convert_reduce_fusion), kind=kOutput, calls=%fused_computation.26 | convolution fusion | flops 17371136 | bytes 28672 | tf_op jit(solution)/shard_map/dot_general | solution.py:62
  6.0 6.1 %fusion.2 = bf16[4096,128]{1,0:T(8,128)(2,1)S(1)} fusion(s32[2048]{0:T(1024)S(1)} %multiply_add_fusion, bf16[1,2048,128]{2,1,0:T(8,128)(2,1)S(1)} %copy-done.6, bf16[1,2048,128]{2,1,0:T(8,128)(2,1)S(1)} %copy-done.7, s32[2048]{0:T(1024)S(1)} %bitcast.91), kind=kOutput, calls=%fused_computation.4 | convolution fusion | flops 2157969408 | bytes 2113536 | tf_op jit(solution)/shard_map/dot_general | solution.py:59
  12.1 1.3 %maximum_maximum_fusion = bf16[16,272,128]{2,1,0:T(8,128)(2,1)} fusion(bf16[16,2,128]{2,1,0:T(2,128)(2,1)S(1)} %reshape.178, bf16[16,256,128]{2,1,0:T(8,128)(2,1)S(1)} %bitcast.77, bf16[272]{0:T(512)(128)(2,1)S(1)} %pad.2.clone), kind=kLoop, calls=%fused_computation.21 | loop fusion | flops 3342336 | bytes 2171424 | tf_op jit(solution)/shard_map/concatenate | solution.py:65
  13.4 6.8 %all-to-all-start = ((bf16[16,272,128]{2,1,0:T(8,128)(2,1)}), bf16[16,272,128]{2,1,0:T(8,128)(2,1)S(1)}, u32[]{:S(2)}, u32[]{:S(2)}) async-start(bf16[16,272,128]{2,1,0:T(8,128)(2,1)} %maximum_maximum_fusion), calls=%async_computation | async-start | bytes 2228224 | tf_op jit(solution)/shard_map/all_to_all | solution.py:73
  20.2 2.9 %collective-permute-start.1 = (bf16[64,128]{1,0:T(8,128)(2,1)S(1)}, bf16[64,128]{1,0:T(8,128)(2,1)S(1)}, u32[]{:S(2)}, u32[]{:S(2)}) collective-permute-start(bf16[64,128]{1,0:T(8,128)(2,1)S(1)} %bitcast.90), channel_id=1, source_target_pairs={{16,0},{32,16},{48,32},{64,48},{80,64},{96,80},{112,96},{128,112},... | collective-permute-start | bytes 49160 | tf_op jit(solution)/shard_map/ppermute | solution.py:12
  23.1 13.5 %all-to-all-done = bf16[16,272,128]{2,1,0:T(8,128)(2,1)S(1)} async-done(((bf16[16,272,128]{2,1,0:T(8,128)(2,1)}), bf16[16,272,128]{2,1,0:T(8,128)(2,1)S(1)}, u32[]{:S(2)}, u32[]{:S(2)}) %all-to-all-start) | async-done | bytes 1114144 | tf_op jit(solution)/shard_map/all_to_all | solution.py:73
  36.7 0.7 fusion.11
  37.4 1.1 %tile.11 = bf16[16,16,16,128]{3,2,1,0:T(8,128)(2,1)} broadcast(bf16[16,16,128]{2,1,0:T(8,128)(2,1)S(1)} %bitcast.86), dimensions={0,1,3} | broadcast | bytes 1114112 | tf_op jit(solution)/shard_map/tile | solution.py:92
  38.5 1.5 %tile.12 = bf16[16,16,2048]{2,1,0:T(8,128)(2,1)S(1)} reshape(bf16[16,16,16,128]{3,2,1,0:T(8,128)(2,1)} %tile.11) | data formatting | bytes 2097152 | tf_op jit(solution)/shard_map/tile | solution.py:92
  40.1 4.8 %fusion.14 = f32[16,16,128]{2,1,0:T(8,128)S(1)} fusion(bf16[16,2048,128]{2,1,0:T(8,128)(2,1)} %bitcast.68, bf16[16,16,2048]{2,1,0:T(8,128)(2,1)S(1)} %tile.12, s32[2048]{0:T(1024)S(1)} %get-tuple-element.7, s32[2048]{0:T(1024)S(1)} %get-tuple-element.8, pred[2048]{0:T(1024)(128)(4,1)S(1)} %fusion.43), kind=kOutput, calls=%fused_computation.27 | convolution fusion | flops 135790592 | bytes 9586688 | tf_op jit(solution)/shard_map/gkr,grj->gkj/dot_general | solution.py:95
  45.3 0.9 fusion.9
  46.4 5.7 %collective-permute-start = (bf16[64,128]{1,0:T(8,128)(2,1)S(1)}, bf16[64,128]{1,0:T(8,128)(2,1)S(1)}, u32[]{:S(2)}, u32[]{:S(2)}) collective-permute-start(bf16[64,128]{1,0:T(8,128)(2,1)S(1)} %convolution_convert_fusion.2), channel_id=1, source_target_pairs={{0,16},{16,32},{32,48},{48,64},{64,80},{80,96},{96,112},{112,128},... | collective-permute-start | bytes 49160 | tf_op jit(solution)/shard_map/ppermute | solution.py:12
  52.1 2.1 %collective-permute-start.2 = (bf16[64,128]{1,0:T(8,128)(2,1)S(1)}, bf16[64,128]{1,0:T(8,128)(2,1)S(1)}, u32[]{:S(2)}, u32[]{:S(2)}) collective-permute-start(bf16[64,128]{1,0:T(8,128)(2,1)S(1)} %convolution_convert_fusion.2), channel_id=1, source_target_pairs={{16,0},{32,16},{48,32},{64,48},{80,64},{96,80},{112,96},{128,112},... | collective-permute-start | bytes 49160 | tf_op jit(solution)/shard_map/ppermute | solution.py:12
  54.2 2.9 %collective-permute-done.2 = bf16[64,128]{1,0:T(8,128)(2,1)S(1)} collective-permute-done((bf16[64,128]{1,0:T(8,128)(2,1)S(1)}, bf16[64,128]{1,0:T(8,128)(2,1)S(1)}, u32[]{:S(2)}, u32[]{:S(2)}) %collective-permute-start.2) | collective-permute-done | bytes 16416 | tf_op jit(solution)/shard_map/ppermute | solution.py:12
  57.4 2.3 %fusion.51 = f32[16,16,2048]{2,1,0:T(8,128)S(1)} fusion(bf16[16,16,128]{2,1,0:T(8,128)(2,1)S(1)} %bitcast.79, bf16[16,2048,128]{2,1,0:T(8,128)(2,1)S(1)} %bitcast.71), kind=kOutput, calls=%fused_computation.83 | convolution fusion | flops 134217728 | bytes 10551296 | tf_op jit(solution)/shard_map/gkj,grj->gkr/dot_general | solution.py:122
  60.7 2.2 %convolution_convert_fusion = bf16[4096,128]{1,0:T(8,128)(2,1)} fusion(bf16[256,128]{1,0:T(8,128)(2,1)S(1)} %bitcast.85, s32[4096]{0:T(1024)S(1)} %convert.2), kind=kOutput, calls=%fused_computation.5 | convolution fusion | flops 270008320 | bytes 1130496 | tf_op jit(solution)/shard_map/dot_general | solution.py:134
  63.0 3.7 %all-to-all-start.1 = ((bf16[16,256,128]{2,1,0:T(8,128)(2,1)}), bf16[16,256,128]{2,1,0:T(8,128)(2,1)S(1)}, u32[]{:S(2)}, u32[]{:S(2)}) async-start(bf16[16,256,128]{2,1,0:T(8,128)(2,1)} %bitcast.75), calls=%async_computation.1 | async-start | bytes 2097152 | tf_op jit(solution)/shard_map/all_to_all | solution.py:135
  66.7 18.5 %all-to-all-done.1 = bf16[16,256,128]{2,1,0:T(8,128)(2,1)S(1)} async-done(((bf16[16,256,128]{2,1,0:T(8,128)(2,1)}), bf16[16,256,128]{2,1,0:T(8,128)(2,1)S(1)}, u32[]{:S(2)}, u32[]{:S(2)}) %all-to-all-start.1) | async-done | bytes 1048608 | tf_op jit(solution)/shard_map/all_to_all | solution.py:135
  85.2 6.2 %gather_fusion = bf16[2048,128]{1,0:T(8,128)(2,1)S(1)} fusion(bf16[4096,128]{1,0:T(8,128)(2,1)S(1)} %bitcast.72, s32[2048]{0:T(1024)S(1)} %broadcast_clamp_fusion), kind=kCustom, calls=%fused_computation | custom fusion | bytes 1056768 | tf_op jit(solution)/shard_map/jit(_take)/gather | solution.py:136
  91.4 1.1 %fusion.16 = bf16[1,2048,128]{2,1,0:T(8,128)(2,1)} fusion(bf16[2048,128]{1,0:T(8,128)(2,1)S(1)} %gather_fusion, s32[2048]{0:T(1024)S(1)} %bitcast.92), kind=kLoop, calls=%fused_computation.29 | loop fusion | flops 1048576 | bytes 1056768 | tf_op jit(solution)/shard_map/convert_element_type | solution.py:137
  (48 shorter events, 2.8 us)
Async XLA Ops:
  0.0 45.3 %copy-start = (bf16[1,48,128,128]{3,2,1,0:T(8,128)(2,1)S(1)}, bf16[1,48,128,128]{3,2,1,0:T(8,128)(2,1)}, u32[]{:S(2)}) copy-start(bf16[1,48,128,128]{3,2,1,0:T(8,128)(2,1)} %param.18) | copy-start | bytes 4718596
  0.0 6.0 %copy-start.3 = (s32[1,2048]{1,0:T(1,128)S(1)}, s32[1,2048]{1,0:T(1,128)}, u32[]{:S(2)}) copy-start(s32[1,2048]{1,0:T(1,128)} %param.13) | copy-start | bytes 24580
  0.0 6.0 %copy-start.7 = (bf16[1,2048,128]{2,1,0:T(8,128)(2,1)S(1)}, bf16[1,2048,128]{2,1,0:T(8,128)(2,1)}, u32[]{:S(2)}) copy-start(bf16[1,2048,128]{2,1,0:T(8,128)(2,1)} %param.11) | copy-start | bytes 1572868
  0.0 6.0 %copy-start.6 = (bf16[1,2048,128]{2,1,0:T(8,128)(2,1)S(1)}, bf16[1,2048,128]{2,1,0:T(8,128)(2,1)}, u32[]{:S(2)}) copy-start(bf16[1,2048,128]{2,1,0:T(8,128)(2,1)} %param.12) | copy-start | bytes 1572868
  12.1 8.0 %copy-start.2 = (bf16[1,64,128]{2,1,0:T(8,128)(2,1)S(1)}, bf16[1,64,128]{2,1,0:T(8,128)(2,1)}, u32[]{:S(2)}) copy-start(bf16[1,64,128]{2,1,0:T(8,128)(2,1)} %param.21) | copy-start | bytes 49156
  13.4 23.1 %all-to-all-start = ((bf16[16,272,128]{2,1,0:T(8,128)(2,1)}), bf16[16,272,128]{2,1,0:T(8,128)(2,1)S(1)}, u32[]{:S(2)}, u32[]{:S(2)}) async-start(bf16[16,272,128]{2,1,0:T(8,128)(2,1)} %maximum_maximum_fusion), calls=%async_computation | async-start | bytes 2228224 | tf_op jit(solution)/shard_map/all_to_all | solution.py:73
  20.2 34.0 %collective-permute-start.1 = (bf16[64,128]{1,0:T(8,128)(2,1)S(1)}, bf16[64,128]{1,0:T(8,128)(2,1)S(1)}, u32[]{:S(2)}, u32[]{:S(2)}) collective-permute-start(bf16[64,128]{1,0:T(8,128)(2,1)S(1)} %bitcast.90), channel_id=1, source_target_pairs={{16,0},{32,16},{48,32},{64,48},{80,64},{96,80},{112,96},{128,112},... | collective-permute-start | bytes 49160 | tf_op jit(solution)/shard_map/ppermute | solution.py:12
  40.0 17.3 %slice-start = ((s8[8388608]{0:T(1024)(128)(4,1)}), s8[4194304]{0:T(1024)(128)(4,1)S(1)}, s32[]{:S(2)}) async-start(s8[8388608]{0:T(1024)(128)(4,1)} %bitcast.69), calls=%async_computation.2 | async-start | bytes 8388608
  40.0 4.9 %copy-start.4 = (s32[1,256]{1,0:T(1,128)S(1)}, s32[1,256]{1,0:T(1,128)}, u32[]{:S(2)}) copy-start(s32[1,256]{1,0:T(1,128)} %param.17) | copy-start | bytes 3076
  40.1 5.1 %copy-start.8 = (s32[1,48]{1,0:T(1,128)S(1)}, s32[1,48]{1,0:T(1,128)}, u32[]{:S(2)}) copy-start(s32[1,48]{1,0:T(1,128)} %param.20) | copy-start | bytes 580
  40.1 6.2 %copy-start.5 = (s32[1,48]{1,0:T(1,128)S(1)}, s32[1,48]{1,0:T(1,128)}, u32[]{:S(2)}) copy-start(s32[1,48]{1,0:T(1,128)} %param.19) | copy-start | bytes 580
  40.1 17.3 %slice-start.1 = ((s8[8388608]{0:T(1024)(128)(4,1)}), s8[4194304]{0:T(1024)(128)(4,1)S(1)}, s32[]{:S(2)}) async-start(s8[8388608]{0:T(1024)(128)(4,1)} %bitcast.69), calls=%async_computation.3 | async-start | bytes 8388608
  46.4 7.8 %collective-permute-start = (bf16[64,128]{1,0:T(8,128)(2,1)S(1)}, bf16[64,128]{1,0:T(8,128)(2,1)S(1)}, u32[]{:S(2)}, u32[]{:S(2)}) collective-permute-start(bf16[64,128]{1,0:T(8,128)(2,1)S(1)} %convolution_convert_fusion.2), channel_id=1, source_target_pairs={{0,16},{16,32},{32,48},{48,64},{64,80},{80,96},{96,112},{112,128},... | collective-permute-start | bytes 49160 | tf_op jit(solution)/shard_map/ppermute | solution.py:12
  52.1 5.1 %collective-permute-start.2 = (bf16[64,128]{1,0:T(8,128)(2,1)S(1)}, bf16[64,128]{1,0:T(8,128)(2,1)S(1)}, u32[]{:S(2)}, u32[]{:S(2)}) collective-permute-start(bf16[64,128]{1,0:T(8,128)(2,1)S(1)} %convolution_convert_fusion.2), channel_id=1, source_target_pairs={{16,0},{32,16},{48,32},{64,48},{80,64},{96,80},{112,96},{128,112},... | collective-permute-start | bytes 49160 | tf_op jit(solution)/shard_map/ppermute | solution.py:12
  60.7 5.9 %copy-start.1 = (s32[1,2048,1]{1,2,0:T(1,128)S(1)}, s32[1,2048,1]{1,2,0:T(1,128)}, u32[]{:S(2)}) copy-start(s32[1,2048,1]{1,2,0:T(1,128)} %param.14) | copy-start | bytes 24580
  63.0 22.2 %all-to-all-start.1 = ((bf16[16,256,128]{2,1,0:T(8,128)(2,1)}), bf16[16,256,128]{2,1,0:T(8,128)(2,1)S(1)}, u32[]{:S(2)}, u32[]{:S(2)}) async-start(bf16[16,256,128]{2,1,0:T(8,128)(2,1)} %bitcast.75), calls=%async_computation.1 | async-start | bytes 2097152 | tf_op jit(solution)/shard_map/all_to_all | solution.py:135

commit v5 on v3

--- a/solution.py
+++ b/solution.py
@@ -54,21 +54,23 @@
     rank = jnp.sum(counts * names.astype(jnp.float32), axis=1).astype(jnp.int32) - 1
     slot = target * CAP + rank
 
-    slot_ids = lax.broadcasted_iota(jnp.int32, (slots, obs_total), 0)
-    placer = (slot_ids == slot[None, :]).astype(jnp.bfloat16)
-    packed = jnp.dot(placer, weighted, preferred_element_type=jnp.float32).astype(jnp.bfloat16)
     rank_ids = lax.broadcasted_iota(jnp.int32, (obs_total, CAP), 1)
     ranked = (rank_ids == rank[:, None]).astype(jnp.bfloat16)
     packed_col = jnp.dot(
         (names * column.astype(jnp.bfloat16)[:, None]).T, ranked, preferred_element_type=jnp.float32
     ).astype(jnp.bfloat16)
-    send = jnp.concatenate(
+    extra = 16
+    stride = CAP + extra
+    frame = jnp.concatenate(
         [
-            packed.reshape(tiles, CAP, block_width),
+            jnp.zeros((tiles, CAP, block_width), jnp.bfloat16),
             packed_col.reshape(tiles, CAP // block_width, block_width),
-            jnp.zeros((tiles, 16 - CAP // block_width, block_width), jnp.bfloat16),
+            jnp.zeros((tiles, extra - CAP // block_width, block_width), jnp.bfloat16),
         ],
         axis=1,
+    ).reshape(tiles * stride, block_width)
+    send = frame.at[target * stride + rank].set(weighted, unique_indices=True).reshape(
+        tiles, stride, block_width
     )
     recv = lax.all_to_all(send, "tile", 0, 0, tiled=True)
     recv_rows = recv[:, :CAP].reshape(slots, block_width)
@@ -85,12 +87,7 @@
         lax.broadcasted_iota(jnp.int32, (group, group), 0)
         == lax.broadcasted_iota(jnp.int32, (group, group), 1)
     ).astype(jnp.bfloat16)
-    spread_left = (
-        merged.reshape(groups, group, 1, block_width) * eye[None, :, :, None]
-    ).reshape(groups, group, group * block_width)
-    spread = jnp.einsum(
-        "gkr,grj->gkj", spread_left, jac_groups, preferred_element_type=jnp.float32
-    ).reshape(jac_total, block_width)
+    spread = jnp.einsum("kij,ki->kj", jacobian[0], merged, preferred_element_type=jnp.float32)
     state_ids = lax.broadcasted_iota(jnp.int32, (state_total, jac_total), 0)
     owners = state_ids == jac_state[0][None, :]
     state = jnp.dot(owners.astype(jnp.float32), spread, precision=lax.Precision.HIGHEST).astype(

time: 93 us -> 94.6 us (1.017)
  other arithmetic: 5.57 us -> 14.6 us
  matrix products: 20.7 us -> 15.9 us
  local copies, waits for them, and re-layouts: 10 us -> 7.26 us
    scatter x0 -> x1, other arithmetic: none -> 9.12 us  [shards(): frame.at[target * stride + rank].set(weighted, unique_indices=True)]
    dot_general x2 -> x1, matrix products: 10.9 us -> 6.08 us  [shards(): jnp.einsum('kij,ki->kj', jacobian[0], merged, preferred_element_type=jnp....]
    mul x3 -> x0, local copies, waits for them, and re-layouts: 2.74 us -> none  [shards(): merged.reshape(groups, group, 1, block_width) * eye[None, :, :, None]]
  transfers between devices with their start and end apart: 5 -> 5, of which waited for: 3 -> 3; matrix products, arithmetic and copies ran while one was open for 11% -> 9% of each run, Pallas kernels for 0% -> 0%
where the time goes in v5:
time: 94.6 us; the launch traced here: 94.1 us
  waiting for transfers between devices  35.2 us (37%)
  starting transfers between devices  20.9 us (22%)
  matrix products  15.9 us (17%)
  other arithmetic  14.6 us (15%)
  local copies, waits for them, and re-layouts  7.26 us (8%)
    all_to_all x1, waiting for transfers between devices, shards(): lax.all_to_all(answer.reshape(tiles, CAP, block_width), 'tile', 0, 0, til...  18.6 us
    all_to_all x1, waiting for transfers between devices, shards(): recv = lax.all_to_all(send, 'tile', 0, 0, tiled=True)  13.5 us
    ppermute x3, starting transfers between devices, from_behind(): return lax.ppermute(x, axis, pairs)  10.5 us
    scatter x1, other arithmetic, shards(): frame.at[target * stride + rank].set(weighted, unique_indices=True)  9.12 us
    all_to_all x1, starting transfers between devices, shards(): recv = lax.all_to_all(send, 'tile', 0, 0, tiled=True)  6.76 us
    gather x1, local copies, waits for them, and re-layouts, shards(): jnp.take(back.reshape(slots, block_width), slot, axis=0, mode='clip')  6.18 us
    dot_general x1, matrix products, shards(): jnp.einsum('kij,ki->kj', jacobian[0], merged, preferred_element_type=jnp....  6.08 us
    all_to_all x1, starting transfers between devices, shards(): lax.all_to_all(answer.reshape(tiles, CAP, block_width), 'tile', 0, 0, til...  3.65 us
  transfers between devices with their start and end apart: 5, of which 3 were waited for; matrix products, arithmetic and copies ran while one was open for 9% of the time, Pallas kernels for 0%

profile of v5, /device:TPU:161, one launch (start us, length us, event | category | flops | bytes accessed | tf_op | source)
XLA Modules:
  0.0 94.1 jit_solution(13827739833068005245)
XLA Ops:
  0.0 1.0 %convolution_bitcast_fusion = f32[16,128,16]{1,2,0:T(8,128)S(1)} fusion(s32[16,128]{1,0:T(8,128)} %bitcast.86), kind=kOutput, calls=%fused_computation.15 | convolution fusion | flops 8437760 | bytes 139264 | tf_op jit(solution)/shard_map/rc,pct->prt/dot_general | solution.py:50
  1.7 0.8 multiply_reduce_fusion
  2.5 0.7 bitcast_add_fusion
  3.3 0.7 convert_reduce_fusion
  4.0 1.9 %fusion.12 = bf16[16,256]{1,0:T(8,128)(2,1)S(1)} fusion(s32[2048]{0:T(1024)S(1)} %get-tuple-element.8, s32[2048]{0:T(1024)} %bitcast.88, bf16[2048]{0:T(1024)(128)(2,1)S(1)} %convert_reduce_fusion), kind=kOutput, calls=%fused_computation.24 | convolution fusion | flops 17371136 | bytes 28672 | tf_op jit(solution)/shard_map/dot_general | solution.py:59
  6.0 1.2 %maximum_maximum_fusion = bf16[16,272,128]{2,1,0:T(8,128)(2,1)} fusion(bf16[16,2,128]{2,1,0:T(2,128)(2,1)S(1)} %reshape.189, bf16[272]{0:T(512)(128)(2,1)S(1)} %pad.2.clone, bf16[272]{0:T(512)(128)(2,1)S(1)} %pad.clone), kind=kLoop, calls=%fused_computation.19 | loop fusion | flops 3342336 | bytes 1123392 | tf_op jit(solution)/shard_map/concatenate | solution.py:64
  7.2 9.1 %scatter_custom_fusion = bf16[4352,128]{1,0:T(8,128)(2,1)} fusion(bf16[4352,128]{1,0:T(8,128)(2,1)} %bitcast.6, s32[2048]{0:T(1024)S(1)} %bitcast.96, bf16[1,2048,128]{2,1,0:T(8,128)(2,1)S(1)} %copy-done.1, bf16[1,2048,128]{2,1,0:T(8,128)(2,1)S(1)} %copy-done.2, f32[]{:T(128)} %constant.8.clone.1, s32[2048]{0:T(1024)S(1)} %bitcast.90), kind=kCustom, calls=%fused_computation.34 | custom fusion | flops 1310720 | bytes 2171392 | tf_op jit(solution)/shard_map/scatter | solution.py:72
  16.3 6.8 %all-to-all-start = ((bf16[16,272,128]{2,1,0:T(8,128)(2,1)}), bf16[16,272,128]{2,1,0:T(8,128)(2,1)S(1)}, u32[]{:S(2)}, u32[]{:S(2)}) async-start(bf16[16,272,128]{2,1,0:T(8,128)(2,1)} %bitcast.11), calls=%async_computation | async-start | bytes 2228224 | tf_op jit(solution)/shard_map/all_to_all | solution.py:75
  23.1 2.9 %collective-permute-start.1 = (bf16[64,128]{1,0:T(8,128)(2,1)S(1)}, bf16[64,128]{1,0:T(8,128)(2,1)S(1)}, u32[]{:S(2)}, u32[]{:S(2)}) collective-permute-start(bf16[64,128]{1,0:T(8,128)(2,1)S(1)} %bitcast.95), channel_id=1, source_target_pairs={{16,0},{32,16},{48,32},{64,48},{80,64},{96,80},{112,96},{128,112},... | collective-permute-start | bytes 49160 | tf_op jit(solution)/shard_map/ppermute | solution.py:12
  26.0 13.5 %all-to-all-done = bf16[16,272,128]{2,1,0:T(8,128)(2,1)S(1)} async-done(((bf16[16,272,128]{2,1,0:T(8,128)(2,1)}), bf16[16,272,128]{2,1,0:T(8,128)(2,1)S(1)}, u32[]{:S(2)}, u32[]{:S(2)}) %all-to-all-start) | async-done | bytes 1114144 | tf_op jit(solution)/shard_map/all_to_all | solution.py:75
  39.6 0.7 fusion.10
  40.4 6.1 %fusion = f32[256,1,128]{2,1,0:T(1,128)S(1)} fusion(bf16[1,256,128,128]{3,2,1,0:T(8,128)(2,1)} %param.16, bf16[256,128,1]{1,0,2:T(8,128)(2,1)S(1)} %fusion.10), kind=kOutput, calls=%fused_computation.2 | convolution fusion | flops 8388608 | bytes 8585216 | tf_op jit(solution)/shard_map/kij,ki->kj/dot_general | solution.py:90
  46.9 0.9 fusion.7
  48.0 5.7 %collective-permute-start = (bf16[64,128]{1,0:T(8,128)(2,1)S(1)}, bf16[64,128]{1,0:T(8,128)(2,1)S(1)}, u32[]{:S(2)}, u32[]{:S(2)}) collective-permute-start(bf16[64,128]{1,0:T(8,128)(2,1)S(1)} %convolution_convert_fusion.2), channel_id=1, source_target_pairs={{0,16},{16,32},{32,48},{48,64},{64,80},{80,96},{96,112},{112,128},... | collective-permute-start | bytes 49160 | tf_op jit(solution)/shard_map/ppermute | solution.py:12
  53.6 1.9 %collective-permute-start.2 = (bf16[64,128]{1,0:T(8,128)(2,1)S(1)}, bf16[64,128]{1,0:T(8,128)(2,1)S(1)}, u32[]{:S(2)}, u32[]{:S(2)}) collective-permute-start(bf16[64,128]{1,0:T(8,128)(2,1)S(1)} %convolution_convert_fusion.2), channel_id=1, source_target_pairs={{16,0},{32,16},{48,32},{64,48},{80,64},{96,80},{112,96},{128,112},... | collective-permute-start | bytes 49160 | tf_op jit(solution)/shard_map/ppermute | solution.py:12
  55.6 3.1 %collective-permute-done.2 = bf16[64,128]{1,0:T(8,128)(2,1)S(1)} collective-permute-done((bf16[64,128]{1,0:T(8,128)(2,1)S(1)}, bf16[64,128]{1,0:T(8,128)(2,1)S(1)}, u32[]{:S(2)}, u32[]{:S(2)}) %collective-permute-start.2) | collective-permute-done | bytes 16416 | tf_op jit(solution)/shard_map/ppermute | solution.py:12
  58.9 2.3 %fusion.41 = f32[16,16,2048]{2,1,0:T(8,128)S(1)} fusion(bf16[16,16,128]{2,1,0:T(8,128)(2,1)S(1)} %bitcast.84, bf16[16,2048,128]{2,1,0:T(8,128)(2,1)S(1)} %bitcast.77), kind=kOutput, calls=%fused_computation.70 | convolution fusion | flops 134217728 | bytes 10551296 | tf_op jit(solution)/shard_map/gkj,grj->gkr/dot_general | solution.py:115
  61.2 0.4 copy.20
  61.6 0.6 fusion.3
  62.3 2.2 %convolution_convert_fusion = bf16[4096,128]{1,0:T(8,128)(2,1)} fusion(bf16[256,128]{1,0:T(8,128)(2,1)S(1)} %bitcast.89, s32[4096]{0:T(1024)S(1)} %convert.2), kind=kOutput, calls=%fused_computation.4 | convolution fusion | flops 270008320 | bytes 1130496 | tf_op jit(solution)/shard_map/dot_general | solution.py:127
  64.5 3.7 %all-to-all-start.1 = ((bf16[16,256,128]{2,1,0:T(8,128)(2,1)}), bf16[16,256,128]{2,1,0:T(8,128)(2,1)S(1)}, u32[]{:S(2)}, u32[]{:S(2)}) async-start(bf16[16,256,128]{2,1,0:T(8,128)(2,1)} %bitcast.81), calls=%async_computation.1 | async-start | bytes 2097152 | tf_op jit(solution)/shard_map/all_to_all | solution.py:128
  68.2 18.6 %all-to-all-done.1 = bf16[16,256,128]{2,1,0:T(8,128)(2,1)S(1)} async-done(((bf16[16,256,128]{2,1,0:T(8,128)(2,1)}), bf16[16,256,128]{2,1,0:T(8,128)(2,1)S(1)}, u32[]{:S(2)}, u32[]{:S(2)}) %all-to-all-start.1) | async-done | bytes 1048608 | tf_op jit(solution)/shard_map/all_to_all | solution.py:128
  86.8 6.2 %gather_fusion = bf16[2048,128]{1,0:T(8,128)(2,1)S(1)} fusion(bf16[4096,128]{1,0:T(8,128)(2,1)S(1)} %bitcast.78, s32[2048]{0:T(1024)S(1)} %broadcast_clamp_fusion), kind=kCustom, calls=%fused_computation | custom fusion | bytes 1056768 | tf_op jit(solution)/shard_map/jit(_take)/gather | solution.py:129
  93.0 1.1 %fusion.13 = bf16[1,2048,128]{2,1,0:T(8,128)(2,1)} fusion(bf16[2048,128]{1,0:T(8,128)(2,1)S(1)} %gather_fusion, s32[2048]{0:T(1024)S(1)} %bitcast.91), kind=kLoop, calls=%fused_computation.26 | loop fusion | flops 1048576 | bytes 1056768 | tf_op jit(solution)/shard_map/convert_element_type | solution.py:130
  (43 shorter events, 1.7 us)
Async XLA Ops:
  0.0 46.9 %copy-start = (bf16[1,48,128,128]{3,2,1,0:T(8,128)(2,1)S(1)}, bf16[1,48,128,128]{3,2,1,0:T(8,128)(2,1)}, u32[]{:S(2)}) copy-start(bf16[1,48,128,128]{3,2,1,0:T(8,128)(2,1)} %param.18) | copy-start | bytes 4718596
  0.0 7.2 %copy-start.3 = (s32[1,2048]{1,0:T(1,128)S(1)}, s32[1,2048]{1,0:T(1,128)}, u32[]{:S(2)}) copy-start(s32[1,2048]{1,0:T(1,128)} %param.13) | copy-start | bytes 24580
  0.0 7.2 %copy-start.2 = (bf16[1,2048,128]{2,1,0:T(8,128)(2,1)S(1)}, bf16[1,2048,128]{2,1,0:T(8,128)(2,1)}, u32[]{:S(2)}) copy-start(bf16[1,2048,128]{2,1,0:T(8,128)(2,1)} %param.11) | copy-start | bytes 1572868
  0.0 7.2 %copy-start.1 = (bf16[1,2048,128]{2,1,0:T(8,128)(2,1)S(1)}, bf16[1,2048,128]{2,1,0:T(8,128)(2,1)}, u32[]{:S(2)}) copy-start(bf16[1,2048,128]{2,1,0:T(8,128)(2,1)} %param.12) | copy-start | bytes 1572868
  7.2 15.9 %copy-start.4 = (bf16[1,64,128]{2,1,0:T(8,128)(2,1)S(1)}, bf16[1,64,128]{2,1,0:T(8,128)(2,1)}, u32[]{:S(2)}) copy-start(bf16[1,64,128]{2,1,0:T(8,128)(2,1)} %param.21) | copy-start | bytes 49156
  16.3 23.1 %all-to-all-start = ((bf16[16,272,128]{2,1,0:T(8,128)(2,1)}), bf16[16,272,128]{2,1,0:T(8,128)(2,1)S(1)}, u32[]{:S(2)}, u32[]{:S(2)}) async-start(bf16[16,272,128]{2,1,0:T(8,128)(2,1)} %bitcast.11), calls=%async_computation | async-start | bytes 2228224 | tf_op jit(solution)/shard_map/all_to_all | solution.py:75
  23.1 32.5 %collective-permute-start.1 = (bf16[64,128]{1,0:T(8,128)(2,1)S(1)}, bf16[64,128]{1,0:T(8,128)(2,1)S(1)}, u32[]{:S(2)}, u32[]{:S(2)}) collective-permute-start(bf16[64,128]{1,0:T(8,128)(2,1)S(1)} %bitcast.95), channel_id=1, source_target_pairs={{16,0},{32,16},{48,32},{64,48},{80,64},{96,80},{112,96},{128,112},... | collective-permute-start | bytes 49160 | tf_op jit(solution)/shard_map/ppermute | solution.py:12
  39.5 19.4 %slice-start = ((s8[8388608]{0:T(1024)(128)(4,1)}), s8[4194304]{0:T(1024)(128)(4,1)S(1)}, s32[]{:S(2)}) async-start(s8[8388608]{0:T(1024)(128)(4,1)} %bitcast.75), calls=%async_computation.2 | async-start | bytes 8388608
  40.3 6.1 %copy-start.5 = (s32[1,256]{1,0:T(1,128)S(1)}, s32[1,256]{1,0:T(1,128)}, u32[]{:S(2)}) copy-start(s32[1,256]{1,0:T(1,128)} %param.17) | copy-start | bytes 3076
  40.4 6.3 %copy-start.7 = (s32[1,48]{1,0:T(1,128)S(1)}, s32[1,48]{1,0:T(1,128)}, u32[]{:S(2)}) copy-start(s32[1,48]{1,0:T(1,128)} %param.20) | copy-start | bytes 580
  40.4 7.4 %copy-start.6 = (s32[1,48]{1,0:T(1,128)S(1)}, s32[1,48]{1,0:T(1,128)}, u32[]{:S(2)}) copy-start(s32[1,48]{1,0:T(1,128)} %param.19) | copy-start | bytes 580
  40.4 18.6 %slice-start.1 = ((s8[8388608]{0:T(1024)(128)(4,1)}), s8[4194304]{0:T(1024)(128)(4,1)S(1)}, s32[]{:S(2)}) async-start(s8[8388608]{0:T(1024)(128)(4,1)} %bitcast.75), calls=%async_computation.3 | async-start | bytes 8388608
  48.0 7.6 %collective-permute-start = (bf16[64,128]{1,0:T(8,128)(2,1)S(1)}, bf16[64,128]{1,0:T(8,128)(2,1)S(1)}, u32[]{:S(2)}, u32[]{:S(2)}) collective-permute-start(bf16[64,128]{1,0:T(8,128)(2,1)S(1)} %convolution_convert_fusion.2), channel_id=1, source_target_pairs={{0,16},{16,32},{32,48},{48,64},{64,80},{80,96},{96,112},{112,128},... | collective-permute-start | bytes 49160 | tf_op jit(solution)/shard_map/ppermute | solution.py:12
  53.6 5.1 %collective-permute-start.2 = (bf16[64,128]{1,0:T(8,128)(2,1)S(1)}, bf16[64,128]{1,0:T(8,128)(2,1)S(1)}, u32[]{:S(2)}, u32[]{:S(2)}) collective-permute-start(bf16[64,128]{1,0:T(8,128)(2,1)S(1)} %convolution_convert_fusion.2), channel_id=1, source_target_pairs={{16,0},{32,16},{48,32},{64,48},{80,64},{96,80},{112,96},{128,112},... | collective-permute-start | bytes 49160 | tf_op jit(solution)/shard_map/ppermute | solution.py:12
  64.5 22.2 %all-to-all-start.1 = ((bf16[16,256,128]{2,1,0:T(8,128)(2,1)}), bf16[16,256,128]{2,1,0:T(8,128)(2,1)S(1)}, u32[]{:S(2)}, u32[]{:S(2)}) async-start(bf16[16,256,128]{2,1,0:T(8,128)(2,1)} %bitcast.81), calls=%async_computation.1 | async-start | bytes 2097152 | tf_op jit(solution)/shard_map/all_to_all | solution.py:128

commit v6 on v3

--- a/solution.py
+++ b/solution.py
@@ -85,12 +85,7 @@
         lax.broadcasted_iota(jnp.int32, (group, group), 0)
         == lax.broadcasted_iota(jnp.int32, (group, group), 1)
     ).astype(jnp.bfloat16)
-    spread_left = (
-        merged.reshape(groups, group, 1, block_width) * eye[None, :, :, None]
-    ).reshape(groups, group, group * block_width)
-    spread = jnp.einsum(
-        "gkr,grj->gkj", spread_left, jac_groups, preferred_element_type=jnp.float32
-    ).reshape(jac_total, block_width)
+    spread = jnp.einsum("kij,ki->kj", jacobian[0], merged, preferred_element_type=jnp.float32)
     state_ids = lax.broadcasted_iota(jnp.int32, (state_total, jac_total), 0)
     owners = state_ids == jac_state[0][None, :]
     state = jnp.dot(owners.astype(jnp.float32), spread, precision=lax.Precision.HIGHEST).astype(

time: 93 us -> 91.7 us (0.986)
  local copies, waits for them, and re-layouts: 10 us -> 7.26 us
  matrix products: 20.7 us -> 22 us
    mul x3 -> x0, local copies, waits for them, and re-layouts: 2.74 us -> none  [shards(): merged.reshape(groups, group, 1, block_width) * eye[None, :, :, None]]
    dot_general x1, matrix products: 4.74 us -> 6.09 us  [shards(): jnp.einsum('kij,ki->kj', jacobian[0], merged, preferred_element_type=jnp....]
  transfers between devices with their start and end apart: 5 -> 5, of which waited for: 3 -> 3; matrix products, arithmetic and copies ran while one was open for 11% -> 9% of each run, Pallas kernels for 0% -> 0%
where the time goes in v6:
time: 91.7 us; the launch traced here: 91.2 us
  waiting for transfers between devices  35 us (38%)
  matrix products  22 us (24%)
  starting transfers between devices  21 us (23%)
  local copies, waits for them, and re-layouts  7.26 us (8%)
  other arithmetic  5.56 us (6%)
    all_to_all x1, waiting for transfers between devices, shards(): lax.all_to_all(answer.reshape(tiles, CAP, block_width), 'tile', 0, 0, til...  18.6 us
    all_to_all x1, waiting for transfers between devices, shards(): recv = lax.all_to_all(send, 'tile', 0, 0, tiled=True)  13.5 us
    ppermute x3, starting transfers between devices, from_behind(): return lax.ppermute(x, axis, pairs)  10.6 us
    all_to_all x1, starting transfers between devices, shards(): recv = lax.all_to_all(send, 'tile', 0, 0, tiled=True)  6.75 us
    gather x1, local copies, waits for them, and re-layouts, shards(): jnp.take(back.reshape(slots, block_width), slot, axis=0, mode='clip')  6.18 us
    dot_general x1, matrix products, shards(): jnp.dot(placer, weighted, preferred_element_type=jnp.float32)  6.13 us
    dot_general x1, matrix products, shards(): jnp.einsum('kij,ki->kj', jacobian[0], merged, preferred_element_type=jnp....  6.09 us
    all_to_all x1, starting transfers between devices, shards(): lax.all_to_all(answer.reshape(tiles, CAP, block_width), 'tile', 0, 0, til...  3.65 us
  transfers between devices with their start and end apart: 5, of which 3 were waited for; matrix products, arithmetic and copies ran while one was open for 9% of the time, Pallas kernels for 0%

profile of v6, /device:TPU:161, one launch (start us, length us, event | category | flops | bytes accessed | tf_op | source)
XLA Modules:
  0.0 91.2 jit_solution(18179144251866560514)
XLA Ops:
  0.0 1.0 %convolution_bitcast_fusion = f32[16,128,16]{1,2,0:T(8,128)S(1)} fusion(s32[16,128]{1,0:T(8,128)} %bitcast.81), kind=kOutput, calls=%fused_computation.18 | convolution fusion | flops 8437760 | bytes 139264 | tf_op jit(solution)/shard_map/rc,pct->prt/dot_general | solution.py:50
  1.7 0.8 multiply_reduce_fusion
  2.5 0.7 multiply_add_fusion
  3.2 0.7 convert_reduce_fusion
  4.0 1.9 %fusion.15 = bf16[16,256]{1,0:T(8,128)(2,1)S(1)} fusion(s32[2048]{0:T(1024)S(1)} %get-tuple-element.6, s32[2048]{0:T(1024)} %bitcast.84, bf16[2048]{0:T(1024)(128)(2,1)S(1)} %convert_reduce_fusion), kind=kOutput, calls=%fused_computation.27 | convolution fusion | flops 17371136 | bytes 28672 | tf_op jit(solution)/shard_map/dot_general | solution.py:62
  6.0 6.1 %fusion.4 = bf16[4096,128]{1,0:T(8,128)(2,1)S(1)} fusion(s32[2048]{0:T(1024)S(1)} %multiply_add_fusion, bf16[1,2048,128]{2,1,0:T(8,128)(2,1)S(1)} %copy-done.6, bf16[1,2048,128]{2,1,0:T(8,128)(2,1)S(1)} %copy-done.7, s32[2048]{0:T(1024)S(1)} %bitcast.91), kind=kOutput, calls=%fused_computation.6 | convolution fusion | flops 2157969408 | bytes 2113536 | tf_op jit(solution)/shard_map/dot_general | solution.py:59
  12.1 1.3 %maximum_maximum_fusion = bf16[16,272,128]{2,1,0:T(8,128)(2,1)} fusion(bf16[16,2,128]{2,1,0:T(2,128)(2,1)S(1)} %reshape.171, bf16[16,256,128]{2,1,0:T(8,128)(2,1)S(1)} %bitcast.78, bf16[272]{0:T(512)(128)(2,1)S(1)} %pad.2.clone), kind=kLoop, calls=%fused_computation.22 | loop fusion | flops 3342336 | bytes 2171424 | tf_op jit(solution)/shard_map/concatenate | solution.py:65
  13.4 6.8 %all-to-all-start = ((bf16[16,272,128]{2,1,0:T(8,128)(2,1)}), bf16[16,272,128]{2,1,0:T(8,128)(2,1)S(1)}, u32[]{:S(2)}, u32[]{:S(2)}) async-start(bf16[16,272,128]{2,1,0:T(8,128)(2,1)} %maximum_maximum_fusion), calls=%async_computation | async-start | bytes 2228224 | tf_op jit(solution)/shard_map/all_to_all | solution.py:73
  20.2 2.9 %collective-permute-start.1 = (bf16[64,128]{1,0:T(8,128)(2,1)S(1)}, bf16[64,128]{1,0:T(8,128)(2,1)S(1)}, u32[]{:S(2)}, u32[]{:S(2)}) collective-permute-start(bf16[64,128]{1,0:T(8,128)(2,1)S(1)} %bitcast.90), channel_id=1, source_target_pairs={{16,0},{32,16},{48,32},{64,48},{80,64},{96,80},{112,96},{128,112},... | collective-permute-start | bytes 49160 | tf_op jit(solution)/shard_map/ppermute | solution.py:12
  23.1 13.5 %all-to-all-done = bf16[16,272,128]{2,1,0:T(8,128)(2,1)S(1)} async-done(((bf16[16,272,128]{2,1,0:T(8,128)(2,1)}), bf16[16,272,128]{2,1,0:T(8,128)(2,1)S(1)}, u32[]{:S(2)}, u32[]{:S(2)}) %all-to-all-start) | async-done | bytes 1114144 | tf_op jit(solution)/shard_map/all_to_all | solution.py:73
  36.7 0.7 fusion.13
  37.4 6.1 %fusion.2 = f32[256,1,128]{2,1,0:T(1,128)S(1)} fusion(bf16[1,256,128,128]{3,2,1,0:T(8,128)(2,1)} %param.16, bf16[256,128,1]{1,0,2:T(8,128)(2,1)S(1)} %fusion.13), kind=kOutput, calls=%fused_computation.4 | convolution fusion | flops 8388608 | bytes 8585216 | tf_op jit(solution)/shard_map/kij,ki->kj/dot_general | solution.py:88
  43.9 0.9 fusion.10
  45.0 5.7 %collective-permute-start = (bf16[64,128]{1,0:T(8,128)(2,1)S(1)}, bf16[64,128]{1,0:T(8,128)(2,1)S(1)}, u32[]{:S(2)}, u32[]{:S(2)}) collective-permute-start(bf16[64,128]{1,0:T(8,128)(2,1)S(1)} %convolution_convert_fusion.2), channel_id=1, source_target_pairs={{0,16},{16,32},{32,48},{48,64},{64,80},{80,96},{96,112},{112,128},... | collective-permute-start | bytes 49160 | tf_op jit(solution)/shard_map/ppermute | solution.py:12
  50.7 2.1 %collective-permute-start.2 = (bf16[64,128]{1,0:T(8,128)(2,1)S(1)}, bf16[64,128]{1,0:T(8,128)(2,1)S(1)}, u32[]{:S(2)}, u32[]{:S(2)}) collective-permute-start(bf16[64,128]{1,0:T(8,128)(2,1)S(1)} %convolution_convert_fusion.2), channel_id=1, source_target_pairs={{16,0},{32,16},{48,32},{64,48},{80,64},{96,80},{112,96},{128,112},... | collective-permute-start | bytes 49160 | tf_op jit(solution)/shard_map/ppermute | solution.py:12
  52.9 2.9 %collective-permute-done.2 = bf16[64,128]{1,0:T(8,128)(2,1)S(1)} collective-permute-done((bf16[64,128]{1,0:T(8,128)(2,1)S(1)}, bf16[64,128]{1,0:T(8,128)(2,1)S(1)}, u32[]{:S(2)}, u32[]{:S(2)}) %collective-permute-start.2) | collective-permute-done | bytes 16416 | tf_op jit(solution)/shard_map/ppermute | solution.py:12
  56.0 2.3 %fusion.44 = f32[16,16,2048]{2,1,0:T(8,128)S(1)} fusion(bf16[16,16,128]{2,1,0:T(8,128)(2,1)S(1)} %bitcast.80, bf16[16,2048,128]{2,1,0:T(8,128)(2,1)S(1)} %bitcast.72), kind=kOutput, calls=%fused_computation.72 | convolution fusion | flops 134217728 | bytes 10551296 | tf_op jit(solution)/shard_map/gkj,grj->gkr/dot_general | solution.py:113
  58.3 0.4 copy.20
  58.7 0.6 fusion.6
  59.4 2.3 %convolution_convert_fusion = bf16[4096,128]{1,0:T(8,128)(2,1)} fusion(bf16[256,128]{1,0:T(8,128)(2,1)S(1)} %bitcast.86, s32[4096]{0:T(1024)S(1)} %convert.2), kind=kOutput, calls=%fused_computation.7 | convolution fusion | flops 270008320 | bytes 1130496 | tf_op jit(solution)/shard_map/dot_general | solution.py:125
  61.6 3.7 %all-to-all-start.1 = ((bf16[16,256,128]{2,1,0:T(8,128)(2,1)}), bf16[16,256,128]{2,1,0:T(8,128)(2,1)S(1)}, u32[]{:S(2)}, u32[]{:S(2)}) async-start(bf16[16,256,128]{2,1,0:T(8,128)(2,1)} %bitcast.76), calls=%async_computation.1 | async-start | bytes 2097152 | tf_op jit(solution)/shard_map/all_to_all | solution.py:126
  65.3 18.6 %all-to-all-done.1 = bf16[16,256,128]{2,1,0:T(8,128)(2,1)S(1)} async-done(((bf16[16,256,128]{2,1,0:T(8,128)(2,1)}), bf16[16,256,128]{2,1,0:T(8,128)(2,1)S(1)}, u32[]{:S(2)}, u32[]{:S(2)}) %all-to-all-start.1) | async-done | bytes 1048608 | tf_op jit(solution)/shard_map/all_to_all | solution.py:126
  83.9 6.2 %gather_fusion = bf16[2048,128]{1,0:T(8,128)(2,1)S(1)} fusion(bf16[4096,128]{1,0:T(8,128)(2,1)S(1)} %bitcast.73, s32[2048]{0:T(1024)S(1)} %broadcast_clamp_fusion), kind=kCustom, calls=%fused_computation | custom fusion | bytes 1056768 | tf_op jit(solution)/shard_map/jit(_take)/gather | solution.py:127
  90.0 1.1 %fusion.16 = bf16[1,2048,128]{2,1,0:T(8,128)(2,1)} fusion(bf16[2048,128]{1,0:T(8,128)(2,1)S(1)} %gather_fusion, s32[2048]{0:T(1024)S(1)} %bitcast.92), kind=kLoop, calls=%fused_computation.29 | loop fusion | flops 1048576 | bytes 1056768 | tf_op jit(solution)/shard_map/convert_element_type | solution.py:128
  (44 shorter events, 1.7 us)
Async XLA Ops:
  0.0 43.9 %copy-start = (bf16[1,48,128,128]{3,2,1,0:T(8,128)(2,1)S(1)}, bf16[1,48,128,128]{3,2,1,0:T(8,128)(2,1)}, u32[]{:S(2)}) copy-start(bf16[1,48,128,128]{3,2,1,0:T(8,128)(2,1)} %param.18) | copy-start | bytes 4718596
  0.0 6.0 %copy-start.3 = (s32[1,2048]{1,0:T(1,128)S(1)}, s32[1,2048]{1,0:T(1,128)}, u32[]{:S(2)}) copy-start(s32[1,2048]{1,0:T(1,128)} %param.13) | copy-start | bytes 24580
  0.0 6.0 %copy-start.7 = (bf16[1,2048,128]{2,1,0:T(8,128)(2,1)S(1)}, bf16[1,2048,128]{2,1,0:T(8,128)(2,1)}, u32[]{:S(2)}) copy-start(bf16[1,2048,128]{2,1,0:T(8,128)(2,1)} %param.11) | copy-start | bytes 1572868
  0.0 6.0 %copy-start.6 = (bf16[1,2048,128]{2,1,0:T(8,128)(2,1)S(1)}, bf16[1,2048,128]{2,1,0:T(8,128)(2,1)}, u32[]{:S(2)}) copy-start(bf16[1,2048,128]{2,1,0:T(8,128)(2,1)} %param.12) | copy-start | bytes 1572868
  12.1 8.1 %copy-start.2 = (bf16[1,64,128]{2,1,0:T(8,128)(2,1)S(1)}, bf16[1,64,128]{2,1,0:T(8,128)(2,1)}, u32[]{:S(2)}) copy-start(bf16[1,64,128]{2,1,0:T(8,128)(2,1)} %param.21) | copy-start | bytes 49156
  13.4 23.1 %all-to-all-start = ((bf16[16,272,128]{2,1,0:T(8,128)(2,1)}), bf16[16,272,128]{2,1,0:T(8,128)(2,1)S(1)}, u32[]{:S(2)}, u32[]{:S(2)}) async-start(bf16[16,272,128]{2,1,0:T(8,128)(2,1)} %maximum_maximum_fusion), calls=%async_computation | async-start | bytes 2228224 | tf_op jit(solution)/shard_map/all_to_all | solution.py:73
  20.2 32.7 %collective-permute-start.1 = (bf16[64,128]{1,0:T(8,128)(2,1)S(1)}, bf16[64,128]{1,0:T(8,128)(2,1)S(1)}, u32[]{:S(2)}, u32[]{:S(2)}) collective-permute-start(bf16[64,128]{1,0:T(8,128)(2,1)S(1)} %bitcast.90), channel_id=1, source_target_pairs={{16,0},{32,16},{48,32},{64,48},{80,64},{96,80},{112,96},{128,112},... | collective-permute-start | bytes 49160 | tf_op jit(solution)/shard_map/ppermute | solution.py:12
  36.6 19.4 %slice-start = ((s8[8388608]{0:T(1024)(128)(4,1)}), s8[4194304]{0:T(1024)(128)(4,1)S(1)}, s32[]{:S(2)}) async-start(s8[8388608]{0:T(1024)(128)(4,1)} %bitcast.70), calls=%async_computation.2 | async-start | bytes 8388608
  37.4 6.1 %copy-start.4 = (s32[1,256]{1,0:T(1,128)S(1)}, s32[1,256]{1,0:T(1,128)}, u32[]{:S(2)}) copy-start(s32[1,256]{1,0:T(1,128)} %param.17) | copy-start | bytes 3076
  37.4 6.3 %copy-start.8 = (s32[1,48]{1,0:T(1,128)S(1)}, s32[1,48]{1,0:T(1,128)}, u32[]{:S(2)}) copy-start(s32[1,48]{1,0:T(1,128)} %param.20) | copy-start | bytes 580
  37.4 7.4 %copy-start.5 = (s32[1,48]{1,0:T(1,128)S(1)}, s32[1,48]{1,0:T(1,128)}, u32[]{:S(2)}) copy-start(s32[1,48]{1,0:T(1,128)} %param.19) | copy-start | bytes 580
  37.4 18.6 %slice-start.1 = ((s8[8388608]{0:T(1024)(128)(4,1)}), s8[4194304]{0:T(1024)(128)(4,1)S(1)}, s32[]{:S(2)}) async-start(s8[8388608]{0:T(1024)(128)(4,1)} %bitcast.70), calls=%async_computation.3 | async-start | bytes 8388608
  45.0 7.8 %collective-permute-start = (bf16[64,128]{1,0:T(8,128)(2,1)S(1)}, bf16[64,128]{1,0:T(8,128)(2,1)S(1)}, u32[]{:S(2)}, u32[]{:S(2)}) collective-permute-start(bf16[64,128]{1,0:T(8,128)(2,1)S(1)} %convolution_convert_fusion.2), channel_id=1, source_target_pairs={{0,16},{16,32},{32,48},{48,64},{64,80},{80,96},{96,112},{112,128},... | collective-permute-start | bytes 49160 | tf_op jit(solution)/shard_map/ppermute | solution.py:12
  50.7 5.1 %collective-permute-start.2 = (bf16[64,128]{1,0:T(8,128)(2,1)S(1)}, bf16[64,128]{1,0:T(8,128)(2,1)S(1)}, u32[]{:S(2)}, u32[]{:S(2)}) collective-permute-start(bf16[64,128]{1,0:T(8,128)(2,1)S(1)} %convolution_convert_fusion.2), channel_id=1, source_target_pairs={{16,0},{32,16},{48,32},{64,48},{80,64},{96,80},{112,96},{128,112},... | collective-permute-start | bytes 49160 | tf_op jit(solution)/shard_map/ppermute | solution.py:12
  59.3 5.9 %copy-start.1 = (s32[1,2048,1]{1,2,0:T(1,128)S(1)}, s32[1,2048,1]{1,2,0:T(1,128)}, u32[]{:S(2)}) copy-start(s32[1,2048,1]{1,2,0:T(1,128)} %param.14) | copy-start | bytes 24580
  61.6 22.3 %all-to-all-start.1 = ((bf16[16,256,128]{2,1,0:T(8,128)(2,1)}), bf16[16,256,128]{2,1,0:T(8,128)(2,1)S(1)}, u32[]{:S(2)}, u32[]{:S(2)}) async-start(bf16[16,256,128]{2,1,0:T(8,128)(2,1)} %bitcast.76), calls=%async_computation.1 | async-start | bytes 2097152 | tf_op jit(solution)/shard_map/all_to_all | solution.py:126

commit v7 on v6

--- a/solution.py
+++ b/solution.py
@@ -56,12 +56,13 @@
 
     slot_ids = lax.broadcasted_iota(jnp.int32, (slots, obs_total), 0)
     placer = (slot_ids == slot[None, :]).astype(jnp.bfloat16)
-    packed = jnp.dot(placer, weighted, preferred_element_type=jnp.float32).astype(jnp.bfloat16)
-    rank_ids = lax.broadcasted_iota(jnp.int32, (obs_total, CAP), 1)
-    ranked = (rank_ids == rank[:, None]).astype(jnp.bfloat16)
-    packed_col = jnp.dot(
-        (names * column.astype(jnp.bfloat16)[:, None]).T, ranked, preferred_element_type=jnp.float32
-    ).astype(jnp.bfloat16)
+    labelled = jnp.concatenate(
+        [weighted, jnp.broadcast_to(column.astype(jnp.bfloat16)[:, None], (obs_total, block_width))],
+        axis=1,
+    )
+    placed = jnp.dot(placer, labelled, preferred_element_type=jnp.float32).astype(jnp.bfloat16)
+    packed = placed[:, :block_width]
+    packed_col = placed[:, block_width]
     send = jnp.concatenate(
         [
             packed.reshape(tiles, CAP, block_width),

time: 91.7 us -> 92.3 us (level)
  matrix products: 22 us -> 20.3 us
  other arithmetic: 5.56 us -> 7.21 us
    dot_general x2 -> x1, matrix products: 8.02 us -> 6.41 us  [shards(): jnp.dot(placer, labelled, preferred_element_type=jnp.float32)]
    convert_element_type x0 -> x1, other arithmetic: none -> 1.54 us  [shards(): weighted = (obs_values[0].astype(jnp.float32) * obs_weight[0].astype(jnp....]
where the time goes in v7:
time: 92.3 us; the launch traced here: 91.8 us
  waiting for transfers between devices  35.1 us (38%)
  starting transfers between devices  20.9 us (23%)
  matrix products  20.3 us (22%)
  local copies, waits for them, and re-layouts  8 us (9%)
  other arithmetic  7.21 us (8%)
    all_to_all x1, waiting for transfers between devices, shards(): lax.all_to_all(answer.reshape(tiles, CAP, block_width), 'tile', 0, 0, til...  18.5 us
    all_to_all x1, waiting for transfers between devices, shards(): recv = lax.all_to_all(send, 'tile', 0, 0, tiled=True)  13.5 us
    ppermute x3, starting transfers between devices, from_behind(): return lax.ppermute(x, axis, pairs)  10.5 us
    all_to_all x1, starting transfers between devices, shards(): recv = lax.all_to_all(send, 'tile', 0, 0, tiled=True)  6.75 us
    dot_general x1, matrix products, shards(): jnp.dot(placer, labelled, preferred_element_type=jnp.float32)  6.41 us
    gather x1, local copies, waits for them, and re-layouts, shards(): jnp.take(back.reshape(slots, block_width), slot, axis=0, mode='clip')  6.18 us
    dot_general x1, matrix products, shards(): jnp.einsum('kij,ki->kj', jacobian[0], merged, preferred_element_type=jnp....  6.09 us
    all_to_all x1, starting transfers between devices, shards(): lax.all_to_all(answer.reshape(tiles, CAP, block_width), 'tile', 0, 0, til...  3.65 us
  transfers between devices with their start and end apart: 5, of which 3 were waited for; matrix products, arithmetic and copies ran while one was open for 9% of the time, Pallas kernels for 0%

profile of v7, /device:TPU:161, one launch (start us, length us, event | category | flops | bytes accessed | tf_op | source)
XLA Modules:
  0.0 91.8 jit_solution(11525636796784832148)
XLA Ops:
  0.0 0.8 broadcast_multiply_fusion
  0.8 0.9 convolution_bitcast_fusion
  2.4 0.8 multiply_reduce_fusion
  3.2 0.7 convert_reduce_fusion
  3.9 1.5 %fusion.18 = bf16[2048,128]{1,0:T(8,128)(2,1)S(1)} fusion(bf16[1,2048,128]{2,1,0:T(8,128)(2,1)} %param.12, bf16[1,2048,128]{2,1,0:T(8,128)(2,1)} %param.11, s32[2048]{0:T(1024)} %bitcast.84), kind=kLoop, calls=%fused_computation.32 | loop fusion | flops 1572864 | bytes 1581056 | tf_op jit(solution)/shard_map/convert_element_type | solution.py:38
  5.8 6.4 %fusion.4 = bf16[4096,256]{1,0:T(8,128)(2,1)S(1)} fusion(s32[2048]{0:T(1024)S(1)} %bitcast_add_fusion.1, bf16[2048,128]{1,0:T(8,128)(2,1)S(1)} %broadcast_in_dim.5, bf16[2048,128]{1,0:T(8,128)(2,1)S(1)} %fusion.18), kind=kOutput, calls=%fused_computation.6 | convolution fusion | flops 4306501632 | bytes 3153920 | tf_op jit(solution)/shard_map/dot_general | solution.py:63
  12.7 1.3 %maximum_maximum_fusion = bf16[16,272,128]{2,1,0:T(8,128)(2,1)} fusion(bf16[16,2,128]{2,1,0:T(2,128)(2,1)S(1)} %bitcast.86, bf16[16,256,128]{2,1,0:T(8,128)(2,1)S(1)} %bitcast.75, bf16[272]{0:T(512)(128)(2,1)S(1)} %pad.2.clone), kind=kLoop, calls=%fused_computation.20 | loop fusion | flops 3342336 | bytes 2171424 | tf_op jit(solution)/shard_map/concatenate | solution.py:66
  14.0 6.8 %all-to-all-start = ((bf16[16,272,128]{2,1,0:T(8,128)(2,1)}), bf16[16,272,128]{2,1,0:T(8,128)(2,1)S(1)}, u32[]{:S(2)}, u32[]{:S(2)}) async-start(bf16[16,272,128]{2,1,0:T(8,128)(2,1)} %maximum_maximum_fusion), calls=%async_computation | async-start | bytes 2228224 | tf_op jit(solution)/shard_map/all_to_all | solution.py:74
  20.8 2.9 %collective-permute-start.1 = (bf16[64,128]{1,0:T(8,128)(2,1)S(1)}, bf16[64,128]{1,0:T(8,128)(2,1)S(1)}, u32[]{:S(2)}, u32[]{:S(2)}) collective-permute-start(bf16[64,128]{1,0:T(8,128)(2,1)S(1)} %bitcast.91), channel_id=1, source_target_pairs={{16,0},{32,16},{48,32},{64,48},{80,64},{96,80},{112,96},{128,112},... | collective-permute-start | bytes 49160 | tf_op jit(solution)/shard_map/ppermute | solution.py:12
  23.7 13.5 %all-to-all-done = bf16[16,272,128]{2,1,0:T(8,128)(2,1)S(1)} async-done(((bf16[16,272,128]{2,1,0:T(8,128)(2,1)}), bf16[16,272,128]{2,1,0:T(8,128)(2,1)S(1)}, u32[]{:S(2)}, u32[]{:S(2)}) %all-to-all-start) | async-done | bytes 1114144 | tf_op jit(solution)/shard_map/all_to_all | solution.py:74
  37.3 0.7 fusion.12
  38.1 6.1 %fusion.2 = f32[256,1,128]{2,1,0:T(1,128)S(1)} fusion(bf16[1,256,128,128]{3,2,1,0:T(8,128)(2,1)} %param.16, bf16[256,128,1]{1,0,2:T(8,128)(2,1)S(1)} %fusion.12), kind=kOutput, calls=%fused_computation.4 | convolution fusion | flops 8388608 | bytes 8585216 | tf_op jit(solution)/shard_map/kij,ki->kj/dot_general | solution.py:89
  44.5 0.9 fusion.9
  45.6 5.7 %collective-permute-start = (bf16[64,128]{1,0:T(8,128)(2,1)S(1)}, bf16[64,128]{1,0:T(8,128)(2,1)S(1)}, u32[]{:S(2)}, u32[]{:S(2)}) collective-permute-start(bf16[64,128]{1,0:T(8,128)(2,1)S(1)} %convolution_convert_fusion.2), channel_id=1, source_target_pairs={{0,16},{16,32},{32,48},{48,64},{64,80},{80,96},{96,112},{112,128},... | collective-permute-start | bytes 49160 | tf_op jit(solution)/shard_map/ppermute | solution.py:12
  51.3 1.9 %collective-permute-start.2 = (bf16[64,128]{1,0:T(8,128)(2,1)S(1)}, bf16[64,128]{1,0:T(8,128)(2,1)S(1)}, u32[]{:S(2)}, u32[]{:S(2)}) collective-permute-start(bf16[64,128]{1,0:T(8,128)(2,1)S(1)} %convolution_convert_fusion.2), channel_id=1, source_target_pairs={{16,0},{32,16},{48,32},{64,48},{80,64},{96,80},{112,96},{128,112},... | collective-permute-start | bytes 49160 | tf_op jit(solution)/shard_map/ppermute | solution.py:12
  53.3 3.1 %collective-permute-done.2 = bf16[64,128]{1,0:T(8,128)(2,1)S(1)} collective-permute-done((bf16[64,128]{1,0:T(8,128)(2,1)S(1)}, bf16[64,128]{1,0:T(8,128)(2,1)S(1)}, u32[]{:S(2)}, u32[]{:S(2)}) %collective-permute-start.2) | collective-permute-done | bytes 16416 | tf_op jit(solution)/shard_map/ppermute | solution.py:12
  56.6 2.3 %fusion.34 = f32[16,16,2048]{2,1,0:T(8,128)S(1)} fusion(bf16[16,16,128]{2,1,0:T(8,128)(2,1)S(1)} %bitcast.79, bf16[16,2048,128]{2,1,0:T(8,128)(2,1)S(1)} %bitcast.71), kind=kOutput, calls=%fused_computation.64 | convolution fusion | flops 134217728 | bytes 10551296 | tf_op jit(solution)/shard_map/gkj,grj->gkr/dot_general | solution.py:114
  58.9 0.4 copy.20
  59.3 0.6 fusion.6
  60.0 2.3 %convolution_convert_fusion = bf16[4096,128]{1,0:T(8,128)(2,1)} fusion(bf16[256,128]{1,0:T(8,128)(2,1)S(1)} %bitcast.83, s32[4096]{0:T(1024)S(1)} %convert.2), kind=kOutput, calls=%fused_computation.7 | convolution fusion | flops 270008320 | bytes 1130496 | tf_op jit(solution)/shard_map/dot_general | solution.py:126
  62.2 3.7 %all-to-all-start.1 = ((bf16[16,256,128]{2,1,0:T(8,128)(2,1)}), bf16[16,256,128]{2,1,0:T(8,128)(2,1)S(1)}, u32[]{:S(2)}, u32[]{:S(2)}) async-start(bf16[16,256,128]{2,1,0:T(8,128)(2,1)} %bitcast.76), calls=%async_computation.1 | async-start | bytes 2097152 | tf_op jit(solution)/shard_map/all_to_all | solution.py:127
  65.9 18.5 %all-to-all-done.1 = bf16[16,256,128]{2,1,0:T(8,128)(2,1)S(1)} async-done(((bf16[16,256,128]{2,1,0:T(8,128)(2,1)}), bf16[16,256,128]{2,1,0:T(8,128)(2,1)S(1)}, u32[]{:S(2)}, u32[]{:S(2)}) %all-to-all-start.1) | async-done | bytes 1048608 | tf_op jit(solution)/shard_map/all_to_all | solution.py:127
  84.5 6.2 %gather_fusion = bf16[2048,128]{1,0:T(8,128)(2,1)S(1)} fusion(bf16[4096,128]{1,0:T(8,128)(2,1)S(1)} %bitcast.72, s32[2048]{0:T(1024)S(1)} %broadcast_clamp_fusion), kind=kCustom, calls=%fused_computation | custom fusion | bytes 1056768 | tf_op jit(solution)/shard_map/jit(_take)/gather | solution.py:128
  90.7 1.1 %fusion.17 = bf16[1,2048,128]{2,1,0:T(8,128)(2,1)} fusion(bf16[2048,128]{1,0:T(8,128)(2,1)S(1)} %gather_fusion, s32[2048]{0:T(1024)S(1)} %bitcast.85), kind=kLoop, calls=%fused_computation.30 | loop fusion | flops 1048576 | bytes 1056768 | tf_op jit(solution)/shard_map/convert_element_type | solution.py:129
  (43 shorter events, 2.5 us)
Async XLA Ops:
  0.0 44.5 %copy-start = (bf16[1,48,128,128]{3,2,1,0:T(8,128)(2,1)S(1)}, bf16[1,48,128,128]{3,2,1,0:T(8,128)(2,1)}, u32[]{:S(2)}) copy-start(bf16[1,48,128,128]{3,2,1,0:T(8,128)(2,1)} %param.18) | copy-start | bytes 4718596
  12.7 8.0 %copy-start.3 = (bf16[1,64,128]{2,1,0:T(8,128)(2,1)S(1)}, bf16[1,64,128]{2,1,0:T(8,128)(2,1)}, u32[]{:S(2)}) copy-start(bf16[1,64,128]{2,1,0:T(8,128)(2,1)} %param.21) | copy-start | bytes 49156
  14.0 23.1 %all-to-all-start = ((bf16[16,272,128]{2,1,0:T(8,128)(2,1)}), bf16[16,272,128]{2,1,0:T(8,128)(2,1)S(1)}, u32[]{:S(2)}, u32[]{:S(2)}) async-start(bf16[16,272,128]{2,1,0:T(8,128)(2,1)} %maximum_maximum_fusion), calls=%async_computation | async-start | bytes 2228224 | tf_op jit(solution)/shard_map/all_to_all | solution.py:74
  20.8 32.5 %collective-permute-start.1 = (bf16[64,128]{1,0:T(8,128)(2,1)S(1)}, bf16[64,128]{1,0:T(8,128)(2,1)S(1)}, u32[]{:S(2)}, u32[]{:S(2)}) collective-permute-start(bf16[64,128]{1,0:T(8,128)(2,1)S(1)} %bitcast.91), channel_id=1, source_target_pairs={{16,0},{32,16},{48,32},{64,48},{80,64},{96,80},{112,96},{128,112},... | collective-permute-start | bytes 49160 | tf_op jit(solution)/shard_map/ppermute | solution.py:12
  37.2 19.4 %slice-start = ((s8[8388608]{0:T(1024)(128)(4,1)}), s8[4194304]{0:T(1024)(128)(4,1)S(1)}, s32[]{:S(2)}) async-start(s8[8388608]{0:T(1024)(128)(4,1)} %bitcast.69), calls=%async_computation.2 | async-start | bytes 8388608
  38.0 6.1 %copy-start.4 = (s32[1,256]{1,0:T(1,128)S(1)}, s32[1,256]{1,0:T(1,128)}, u32[]{:S(2)}) copy-start(s32[1,256]{1,0:T(1,128)} %param.17) | copy-start | bytes 3076
  38.0 6.3 %copy-start.6 = (s32[1,48]{1,0:T(1,128)S(1)}, s32[1,48]{1,0:T(1,128)}, u32[]{:S(2)}) copy-start(s32[1,48]{1,0:T(1,128)} %param.20) | copy-start | bytes 580
  38.0 7.4 %copy-start.5 = (s32[1,48]{1,0:T(1,128)S(1)}, s32[1,48]{1,0:T(1,128)}, u32[]{:S(2)}) copy-start(s32[1,48]{1,0:T(1,128)} %param.19) | copy-start | bytes 580
  38.0 18.6 %slice-start.1 = ((s8[8388608]{0:T(1024)(128)(4,1)}), s8[4194304]{0:T(1024)(128)(4,1)S(1)}, s32[]{:S(2)}) async-start(s8[8388608]{0:T(1024)(128)(4,1)} %bitcast.69), calls=%async_computation.3 | async-start | bytes 8388608
  45.6 7.6 %collective-permute-start = (bf16[64,128]{1,0:T(8,128)(2,1)S(1)}, bf16[64,128]{1,0:T(8,128)(2,1)S(1)}, u32[]{:S(2)}, u32[]{:S(2)}) collective-permute-start(bf16[64,128]{1,0:T(8,128)(2,1)S(1)} %convolution_convert_fusion.2), channel_id=1, source_target_pairs={{0,16},{16,32},{32,48},{48,64},{64,80},{80,96},{96,112},{112,128},... | collective-permute-start | bytes 49160 | tf_op jit(solution)/shard_map/ppermute | solution.py:12
  51.3 5.1 %collective-permute-start.2 = (bf16[64,128]{1,0:T(8,128)(2,1)S(1)}, bf16[64,128]{1,0:T(8,128)(2,1)S(1)}, u32[]{:S(2)}, u32[]{:S(2)}) collective-permute-start(bf16[64,128]{1,0:T(8,128)(2,1)S(1)} %convolution_convert_fusion.2), channel_id=1, source_target_pairs={{16,0},{32,16},{48,32},{64,48},{80,64},{96,80},{112,96},{128,112},... | collective-permute-start | bytes 49160 | tf_op jit(solution)/shard_map/ppermute | solution.py:12
  59.9 6.0 %copy-start.1 = (s32[1,2048,1]{1,2,0:T(1,128)S(1)}, s32[1,2048,1]{1,2,0:T(1,128)}, u32[]{:S(2)}) copy-start(s32[1,2048,1]{1,2,0:T(1,128)} %param.14) | copy-start | bytes 24580
  62.2 22.2 %all-to-all-start.1 = ((bf16[16,256,128]{2,1,0:T(8,128)(2,1)}), bf16[16,256,128]{2,1,0:T(8,128)(2,1)S(1)}, u32[]{:S(2)}, u32[]{:S(2)}) async-start(bf16[16,256,128]{2,1,0:T(8,128)(2,1)} %bitcast.76), calls=%async_computation.1 | async-start | bytes 2097152 | tf_op jit(solution)/shard_map/all_to_all | solution.py:127
  84.5 6.2 %copy-start.2 = (s32[1,2048]{1,0:T(1,128)S(1)}, s32[1,2048]{1,0:T(1,128)}, u32[]{:S(2)}) copy-start(s32[1,2048]{1,0:T(1,128)} %param.13) | copy-start | bytes 24580

commit v8 on v6

--- a/solution.py
+++ b/solution.py
@@ -54,13 +54,16 @@
     rank = jnp.sum(counts * names.astype(jnp.float32), axis=1).astype(jnp.int32) - 1
     slot = target * CAP + rank
 
-    slot_ids = lax.broadcasted_iota(jnp.int32, (slots, obs_total), 0)
-    placer = (slot_ids == slot[None, :]).astype(jnp.bfloat16)
-    packed = jnp.dot(placer, weighted, preferred_element_type=jnp.float32).astype(jnp.bfloat16)
     rank_ids = lax.broadcasted_iota(jnp.int32, (obs_total, CAP), 1)
     ranked = (rank_ids == rank[:, None]).astype(jnp.bfloat16)
     packed_col = jnp.dot(
         (names * column.astype(jnp.bfloat16)[:, None]).T, ranked, preferred_element_type=jnp.float32
+    ).astype(jnp.bfloat16)
+    masked = jnp.where(
+        (tile_ids == target[:, None]).T[:, :, None], weighted[None], jnp.zeros((), jnp.bfloat16)
+    )
+    packed = jnp.einsum(
+        "jr,djc->drc", ranked, masked, preferred_element_type=jnp.float32
     ).astype(jnp.bfloat16)
     send = jnp.concatenate(
         [

time: 91.7 us -> 89.3 us (0.974)
  matrix products: 22 us -> 17.7 us
  local copies, waits for them, and re-layouts: 7.26 us -> 10.1 us
    dot_general x1, matrix products: 6.13 us -> 2.48 us  [shards(): jnp.einsum('jr,djc->drc', ranked, masked, preferred_element_type=jnp.floa...]
    concatenate x1 -> x2, local copies, waits for them, and re-layouts: 0.08 us -> 1.62 us  [shards(): jnp.concatenate([packed.reshape(tiles, CAP, block_width), packed_col.resh...]
    broadcast_in_dim x0 -> x1, other arithmetic: none -> 1.54 us  [shards(): jnp.where((tile_ids == target[:, None]).T[:, :, None], weighted[None], jn...]
    reshape x1 -> x2, local copies, waits for them, and re-layouts: 0.01 us -> 1.08 us  [shards(): packed_col.reshape(tiles, CAP // block_width, block_width)]
where the time goes in v8:
time: 89.3 us; the launch traced here: 88.9 us
  waiting for transfers between devices  35.1 us (39%)
  starting transfers between devices  20.9 us (23%)
  matrix products  17.7 us (20%)
  local copies, waits for them, and re-layouts  10.1 us (11%)
  other arithmetic  4.83 us (5%)
    all_to_all x1, waiting for transfers between devices, shards(): lax.all_to_all(answer.reshape(tiles, CAP, block_width), 'tile', 0, 0, til...  18.6 us
    all_to_all x1, waiting for transfers between devices, shards(): recv = lax.all_to_all(send, 'tile', 0, 0, tiled=True)  13.5 us
    ppermute x3, starting transfers between devices, from_behind(): return lax.ppermute(x, axis, pairs)  10.5 us
    all_to_all x1, starting transfers between devices, shards(): recv = lax.all_to_all(send, 'tile', 0, 0, tiled=True)  6.75 us
    gather x1, local copies, waits for them, and re-layouts, shards(): jnp.take(back.reshape(slots, block_width), slot, axis=0, mode='clip')  6.18 us
    dot_general x1, matrix products, shards(): jnp.einsum('kij,ki->kj', jacobian[0], merged, preferred_element_type=jnp....  6.09 us
    all_to_all x1, starting transfers between devices, shards(): lax.all_to_all(answer.reshape(tiles, CAP, block_width), 'tile', 0, 0, til...  3.65 us
    ppermute x3, waiting for transfers between devices, from_behind(): return lax.ppermute(x, axis, pairs)  3.1 us
  transfers between devices with their start and end apart: 5, of which 3 were waited for; matrix products, arithmetic and copies ran while one was open for 9% of the time, Pallas kernels for 0%

profile of v8, /device:TPU:161, one launch (start us, length us, event | category | flops | bytes accessed | tf_op | source)
XLA Modules:
  0.0 88.9 jit_solution(2515436736352610090)
XLA Ops:
  0.0 1.0 %convolution_bitcast_fusion = f32[16,128,16]{1,2,0:T(8,128)S(1)} fusion(s32[16,128]{1,0:T(8,128)} %bitcast.84), kind=kOutput, calls=%fused_computation.23 | convolution fusion | flops 8437760 | bytes 139264 | tf_op jit(solution)/shard_map/rc,pct->prt/dot_general | solution.py:50
  1.7 0.8 multiply_reduce_fusion
  2.5 1.5 %fusion.35 = bf16[2048,128]{1,0:T(8,128)(2,1)S(1)} fusion(bf16[1,2048,128]{2,1,0:T(8,128)(2,1)} %param.12, bf16[1,2048,128]{2,1,0:T(8,128)(2,1)} %param.11, s32[2048]{0:T(1024)} %bitcast.90), kind=kLoop, calls=%fused_computation.40 | loop fusion | flops 1572864 | bytes 1581056 | tf_op jit(solution)/shard_map/jit(_where)/broadcast_in_dim | solution.py:62
  4.3 1.2 %fusion.29 = bf16[16,256]{1,0:T(8,128)(2,1)S(1)} fusion(s32[2048]{0:T(1024)S(1)} %get-tuple-element.6, s32[2048]{0:T(1024)S(1)} %bitcast.87, bf16[2048]{0:T(1024)(128)(2,1)S(1)} %convert_reduce_fusion), kind=kOutput, calls=%fused_computation.31 | convolution fusion | flops 17371136 | bytes 28672 | tf_op jit(solution)/shard_map/dot_general | solution.py:59
  5.6 1.1 %copy.24 = bf16[16,2,128]{1,2,0:T(8,128)(2,1)} copy(bf16[16,2,128]{2,1,0:T(2,128)(2,1)S(1)} %reshape.193) | data formatting | bytes 16384 | tf_op jit(solution)/shard_map/reshape | solution.py:71
  6.6 2.5 %fusion.21 = bf16[16,256,128]{1,2,0:T(8,128)(2,1)S(1)} fusion(pred[16,2048]{1,0:T(8,128)(4,1)S(1)} %iota_compare_fusion.15, bf16[2048,128]{0,1:T(8,128)(2,1)S(1)} %copy.21, s32[2048]{0:T(1024)S(1)} %get-tuple-element.6), kind=kOutput, calls=%fused_computation.22 | convolution fusion | flops 2152726528 | bytes 1613824 | tf_op jit(solution)/shard_map/jr,djc->drc/dot_general | solution.py:65
  9.6 1.5 %copy.25 = bf16[16,272,128]{2,1,0:T(8,128)(2,1)} copy(bf16[16,272,128]{1,2,0:T(8,128)(2,1)S(1)} %maximum_maximum_fusion) | data formatting | bytes 2228224 | tf_op jit(solution)/shard_map/concatenate | solution.py:68
  11.1 6.8 %all-to-all-start = ((bf16[16,272,128]{2,1,0:T(8,128)(2,1)}), bf16[16,272,128]{2,1,0:T(8,128)(2,1)S(1)}, u32[]{:S(2)}, u32[]{:S(2)}) async-start(bf16[16,272,128]{2,1,0:T(8,128)(2,1)} %copy.25), calls=%async_computation | async-start | bytes 2228224 | tf_op jit(solution)/shard_map/all_to_all | solution.py:76
  17.9 2.9 %collective-permute-start.1 = (bf16[64,128]{1,0:T(8,128)(2,1)S(1)}, bf16[64,128]{1,0:T(8,128)(2,1)S(1)}, u32[]{:S(2)}, u32[]{:S(2)}) collective-permute-start(bf16[64,128]{1,0:T(8,128)(2,1)S(1)} %bitcast.95), channel_id=1, source_target_pairs={{16,0},{32,16},{48,32},{64,48},{80,64},{96,80},{112,96},{128,112},... | collective-permute-start | bytes 49160 | tf_op jit(solution)/shard_map/ppermute | solution.py:12
  20.8 13.5 %all-to-all-done = bf16[16,272,128]{2,1,0:T(8,128)(2,1)S(1)} async-done(((bf16[16,272,128]{2,1,0:T(8,128)(2,1)}), bf16[16,272,128]{2,1,0:T(8,128)(2,1)S(1)}, u32[]{:S(2)}, u32[]{:S(2)}) %all-to-all-start) | async-done | bytes 1114144 | tf_op jit(solution)/shard_map/all_to_all | solution.py:76
  34.4 0.7 fusion.27
  35.2 6.1 %fusion = f32[256,1,128]{2,1,0:T(1,128)S(1)} fusion(bf16[1,256,128,128]{3,2,1,0:T(8,128)(2,1)} %param.16, bf16[256,128,1]{1,0,2:T(8,128)(2,1)S(1)} %fusion.27), kind=kOutput, calls=%fused_computation.1 | convolution fusion | flops 8388608 | bytes 8585216 | tf_op jit(solution)/shard_map/kij,ki->kj/dot_general | solution.py:91
  41.7 0.9 %fusion.14 = f32[48,1,128]{2,1,0:T(1,128)S(1)} fusion(bf16[1,48,128,128]{3,2,1,0:T(8,128)(2,1)S(1)} %copy-done, bf16[48,128,1]{1,0,2:T(8,128)(2,1)S(1)} %fusion.28), kind=kOutput, calls=%fused_computation.19 | convolution fusion | flops 1572864 | bytes 1609728 | tf_op jit(solution)/shard_map/cij,cj->ci/dot_general | solution.py:101
  42.8 5.7 %collective-permute-start = (bf16[64,128]{1,0:T(8,128)(2,1)S(1)}, bf16[64,128]{1,0:T(8,128)(2,1)S(1)}, u32[]{:S(2)}, u32[]{:S(2)}) collective-permute-start(bf16[64,128]{1,0:T(8,128)(2,1)S(1)} %convolution_convert_fusion.2), channel_id=1, source_target_pairs={{0,16},{16,32},{32,48},{48,64},{64,80},{80,96},{96,112},{112,128},... | collective-permute-start | bytes 49160 | tf_op jit(solution)/shard_map/ppermute | solution.py:12
  48.4 1.9 %collective-permute-start.2 = (bf16[64,128]{1,0:T(8,128)(2,1)S(1)}, bf16[64,128]{1,0:T(8,128)(2,1)S(1)}, u32[]{:S(2)}, u32[]{:S(2)}) collective-permute-start(bf16[64,128]{1,0:T(8,128)(2,1)S(1)} %convolution_convert_fusion.2), channel_id=1, source_target_pairs={{16,0},{32,16},{48,32},{64,48},{80,64},{96,80},{112,96},{128,112},... | collective-permute-start | bytes 49160 | tf_op jit(solution)/shard_map/ppermute | solution.py:12
  50.4 3.1 %collective-permute-done.2 = bf16[64,128]{1,0:T(8,128)(2,1)S(1)} collective-permute-done((bf16[64,128]{1,0:T(8,128)(2,1)S(1)}, bf16[64,128]{1,0:T(8,128)(2,1)S(1)}, u32[]{:S(2)}, u32[]{:S(2)}) %collective-permute-start.2) | collective-permute-done | bytes 16416 | tf_op jit(solution)/shard_map/ppermute | solution.py:12
  53.8 2.3 %fusion.56 = f32[16,16,2048]{2,1,0:T(8,128)S(1)} fusion(bf16[16,16,128]{2,1,0:T(8,128)(2,1)S(1)} %bitcast.83, bf16[16,2048,128]{2,1,0:T(8,128)(2,1)S(1)} %bitcast.76), kind=kOutput, calls=%fused_computation.74 | convolution fusion | flops 134217728 | bytes 10551296 | tf_op jit(solution)/shard_map/gkj,grj->gkr/dot_general | solution.py:116
  56.0 0.4 copy.30
  56.4 0.6 fusion.8
  57.1 2.3 %convolution_convert_fusion = bf16[4096,128]{1,0:T(8,128)(2,1)} fusion(bf16[256,128]{1,0:T(8,128)(2,1)S(1)} %bitcast.89, s32[4096]{0:T(1024)S(1)} %convert.2), kind=kOutput, calls=%fused_computation.6 | convolution fusion | flops 270008320 | bytes 1130496 | tf_op jit(solution)/shard_map/dot_general | solution.py:128
  59.3 3.7 %all-to-all-start.1 = ((bf16[16,256,128]{2,1,0:T(8,128)(2,1)}), bf16[16,256,128]{2,1,0:T(8,128)(2,1)S(1)}, u32[]{:S(2)}, u32[]{:S(2)}) async-start(bf16[16,256,128]{2,1,0:T(8,128)(2,1)} %bitcast.80), calls=%async_computation.1 | async-start | bytes 2097152 | tf_op jit(solution)/shard_map/all_to_all | solution.py:129
  63.0 18.6 %all-to-all-done.1 = bf16[16,256,128]{2,1,0:T(8,128)(2,1)S(1)} async-done(((bf16[16,256,128]{2,1,0:T(8,128)(2,1)}), bf16[16,256,128]{2,1,0:T(8,128)(2,1)S(1)}, u32[]{:S(2)}, u32[]{:S(2)}) %all-to-all-start.1) | async-done | bytes 1048608 | tf_op jit(solution)/shard_map/all_to_all | solution.py:129
  81.6 6.2 %gather_fusion = bf16[2048,128]{1,0:T(8,128)(2,1)S(1)} fusion(bf16[4096,128]{1,0:T(8,128)(2,1)S(1)} %bitcast.77, s32[2048]{0:T(1024)S(1)} %broadcast_clamp_fusion), kind=kCustom, calls=%fused_computation | custom fusion | bytes 1056768 | tf_op jit(solution)/shard_map/jit(_take)/gather | solution.py:130
  87.8 1.1 %fusion.30 = bf16[1,2048,128]{2,1,0:T(8,128)(2,1)} fusion(bf16[2048,128]{1,0:T(8,128)(2,1)S(1)} %gather_fusion, s32[2048]{0:T(1024)S(1)} %bitcast.91), kind=kLoop, calls=%fused_computation.33 | loop fusion | flops 1048576 | bytes 1056768 | tf_op jit(solution)/shard_map/convert_element_type | solution.py:131
  (48 shorter events, 2.4 us)
Async XLA Ops:
  0.0 41.7 %copy-start = (bf16[1,48,128,128]{3,2,1,0:T(8,128)(2,1)S(1)}, bf16[1,48,128,128]{3,2,1,0:T(8,128)(2,1)}, u32[]{:S(2)}) copy-start(bf16[1,48,128,128]{3,2,1,0:T(8,128)(2,1)} %param.18) | copy-start | bytes 4718596
  0.0 4.3 %copy-start.2 = (s32[1,2048,1]{1,2,0:T(1,128)S(1)}, s32[1,2048,1]{1,2,0:T(1,128)}, u32[]{:S(2)}) copy-start(s32[1,2048,1]{1,2,0:T(1,128)} %param.14) | copy-start | bytes 24580
  0.0 4.3 %copy-start.5 = (s32[1,2048]{1,0:T(1,128)S(1)}, s32[1,2048]{1,0:T(1,128)}, u32[]{:S(2)}) copy-start(s32[1,2048]{1,0:T(1,128)} %param.15) | copy-start | bytes 24580
  6.6 2.6 %copy-start.1 = (bf16[16,2,128]{1,2,0:T(8,128)(2,1)S(1)}, bf16[16,2,128]{1,2,0:T(8,128)(2,1)}, u32[]{:S(2)}) copy-start(bf16[16,2,128]{1,2,0:T(8,128)(2,1)} %copy.24) | copy-start | bytes 24580
  9.6 8.3 %copy-start.4 = (bf16[1,64,128]{2,1,0:T(8,128)(2,1)S(1)}, bf16[1,64,128]{2,1,0:T(8,128)(2,1)}, u32[]{:S(2)}) copy-start(bf16[1,64,128]{2,1,0:T(8,128)(2,1)} %param.21) | copy-start | bytes 49156
  11.1 23.1 %all-to-all-start = ((bf16[16,272,128]{2,1,0:T(8,128)(2,1)}), bf16[16,272,128]{2,1,0:T(8,128)(2,1)S(1)}, u32[]{:S(2)}, u32[]{:S(2)}) async-start(bf16[16,272,128]{2,1,0:T(8,128)(2,1)} %copy.25), calls=%async_computation | async-start | bytes 2228224 | tf_op jit(solution)/shard_map/all_to_all | solution.py:76
  17.9 32.5 %collective-permute-start.1 = (bf16[64,128]{1,0:T(8,128)(2,1)S(1)}, bf16[64,128]{1,0:T(8,128)(2,1)S(1)}, u32[]{:S(2)}, u32[]{:S(2)}) collective-permute-start(bf16[64,128]{1,0:T(8,128)(2,1)S(1)} %bitcast.95), channel_id=1, source_target_pairs={{16,0},{32,16},{48,32},{64,48},{80,64},{96,80},{112,96},{128,112},... | collective-permute-start | bytes 49160 | tf_op jit(solution)/shard_map/ppermute | solution.py:12
  34.3 19.4 %slice-start = ((s8[8388608]{0:T(1024)(128)(4,1)}), s8[4194304]{0:T(1024)(128)(4,1)S(1)}, s32[]{:S(2)}) async-start(s8[8388608]{0:T(1024)(128)(4,1)} %bitcast.74), calls=%async_computation.2 | async-start | bytes 8388608
  35.1 6.1 %copy-start.6 = (s32[1,256]{1,0:T(1,128)S(1)}, s32[1,256]{1,0:T(1,128)}, u32[]{:S(2)}) copy-start(s32[1,256]{1,0:T(1,128)} %param.17) | copy-start | bytes 3076
  35.1 6.3 %copy-start.8 = (s32[1,48]{1,0:T(1,128)S(1)}, s32[1,48]{1,0:T(1,128)}, u32[]{:S(2)}) copy-start(s32[1,48]{1,0:T(1,128)} %param.20) | copy-start | bytes 580
  35.2 7.4 %copy-start.7 = (s32[1,48]{1,0:T(1,128)S(1)}, s32[1,48]{1,0:T(1,128)}, u32[]{:S(2)}) copy-start(s32[1,48]{1,0:T(1,128)} %param.19) | copy-start | bytes 580
  35.2 18.6 %slice-start.1 = ((s8[8388608]{0:T(1024)(128)(4,1)}), s8[4194304]{0:T(1024)(128)(4,1)S(1)}, s32[]{:S(2)}) async-start(s8[8388608]{0:T(1024)(128)(4,1)} %bitcast.74), calls=%async_computation.3 | async-start | bytes 8388608
  42.8 7.6 %collective-permute-start = (bf16[64,128]{1,0:T(8,128)(2,1)S(1)}, bf16[64,128]{1,0:T(8,128)(2,1)S(1)}, u32[]{:S(2)}, u32[]{:S(2)}) collective-permute-start(bf16[64,128]{1,0:T(8,128)(2,1)S(1)} %convolution_convert_fusion.2), channel_id=1, source_target_pairs={{0,16},{16,32},{32,48},{48,64},{64,80},{80,96},{96,112},{112,128},... | collective-permute-start | bytes 49160 | tf_op jit(solution)/shard_map/ppermute | solution.py:12
  48.4 5.1 %collective-permute-start.2 = (bf16[64,128]{1,0:T(8,128)(2,1)S(1)}, bf16[64,128]{1,0:T(8,128)(2,1)S(1)}, u32[]{:S(2)}, u32[]{:S(2)}) collective-permute-start(bf16[64,128]{1,0:T(8,128)(2,1)S(1)} %convolution_convert_fusion.2), channel_id=1, source_target_pairs={{16,0},{32,16},{48,32},{64,48},{80,64},{96,80},{112,96},{128,112},... | collective-permute-start | bytes 49160 | tf_op jit(solution)/shard_map/ppermute | solution.py:12
  59.3 22.3 %all-to-all-start.1 = ((bf16[16,256,128]{2,1,0:T(8,128)(2,1)}), bf16[16,256,128]{2,1,0:T(8,128)(2,1)S(1)}, u32[]{:S(2)}, u32[]{:S(2)}) async-start(bf16[16,256,128]{2,1,0:T(8,128)(2,1)} %bitcast.80), calls=%async_computation.1 | async-start | bytes 2097152 | tf_op jit(solution)/shard_map/all_to_all | solution.py:129
  81.6 6.2 %copy-start.3 = (s32[1,2048]{1,0:T(1,128)S(1)}, s32[1,2048]{1,0:T(1,128)}, u32[]{:S(2)}) copy-start(s32[1,2048]{1,0:T(1,128)} %param.13) | copy-start | bytes 24580

commit v9 on v8

--- a/solution.py
+++ b/solution.py
@@ -56,8 +56,11 @@
 
     rank_ids = lax.broadcasted_iota(jnp.int32, (obs_total, CAP), 1)
     ranked = (rank_ids == rank[:, None]).astype(jnp.bfloat16)
-    packed_col = jnp.dot(
-        (names * column.astype(jnp.bfloat16)[:, None]).T, ranked, preferred_element_type=jnp.float32
+    labels = jnp.concatenate(
+        [column.astype(jnp.bfloat16)[:, None], obs_count[0].astype(jnp.bfloat16)[:, None]], axis=1
+    )
+    packed_meta = jnp.einsum(
+        "jd,jr,jm->dmr", names, ranked, labels, preferred_element_type=jnp.float32
     ).astype(jnp.bfloat16)
     masked = jnp.where(
         (tile_ids == target[:, None]).T[:, :, None], weighted[None], jnp.zeros((), jnp.bfloat16)
@@ -68,8 +71,8 @@
     send = jnp.concatenate(
         [
             packed.reshape(tiles, CAP, block_width),
-            packed_col.reshape(tiles, CAP // block_width, block_width),
-            jnp.zeros((tiles, 16 - CAP // block_width, block_width), jnp.bfloat16),
+            packed_meta.reshape(tiles, 2 * CAP // block_width, block_width),
+            jnp.zeros((tiles, 16 - 2 * CAP // block_width, block_width), jnp.bfloat16),
         ],
         axis=1,
     )
@@ -78,6 +81,9 @@
     recv_col = recv[:, CAP:CAP + CAP // block_width].reshape(1, slots).astype(jnp.int32)
     jac_ids = lax.broadcasted_iota(jnp.int32, (jac_total, slots), 0)
     binner = (jac_ids == recv_col).astype(jnp.bfloat16)
+    recv_count = recv[:, CAP + CAP // block_width:CAP + 2 * CAP // block_width].reshape(slots, 1).astype(jnp.int32)
+    slot_lanes = lax.broadcasted_iota(jnp.int32, (slots, block_width), 1)
+    slot_keep = (slot_lanes < recv_count).astype(jnp.float32)
     summed = jnp.dot(binner, recv_rows, preferred_element_type=jnp.float32)
 
     merged = summed.astype(jnp.bfloat16)
@@ -125,10 +131,12 @@
         .astype(jnp.bfloat16)
     )
 
-    answer = jnp.dot(binner.T, model_obs, preferred_element_type=jnp.float32).astype(jnp.bfloat16)
+    answer = (
+        jnp.dot(binner.T, model_obs, preferred_element_type=jnp.float32) * slot_keep
+    ).astype(jnp.bfloat16)
     back = lax.all_to_all(answer.reshape(tiles, CAP, block_width), "tile", 0, 0, tiled=True)
-    gathered = jnp.take(back.reshape(slots, block_width), slot, axis=0, mode="clip").astype(jnp.float32)
-    return (gathered * keeping).astype(jnp.bfloat16)[None]
+    gathered = jnp.take(back.reshape(slots, block_width), slot, axis=0, mode="clip")
+    return gathered[None]
 
 
 def solution(mesh):

time: 89.3 us -> 91.1 us (1.020)
  local copies, waits for them, and re-layouts: 10.1 us -> 12 us
    gather x1, local copies, waits for them, and re-layouts: 6.18 us -> 8.04 us  [shards(): jnp.take(back.reshape(slots, block_width), slot, axis=0, mode='clip')]
    broadcast_in_dim x1, other arithmetic: 1.54 us -> 0.34 us  [shards(): jnp.where((tile_ids == target[:, None]).T[:, :, None], weighted[None], jn...]
where the time goes in v9:
time: 91.1 us; the launch traced here: 90.5 us
  waiting for transfers between devices  35.1 us (39%)
  starting transfers between devices  21 us (23%)
  matrix products  17.2 us (19%)
  local copies, waits for them, and re-layouts  12 us (13%)
  other arithmetic  4.78 us (5%)
    all_to_all x1, waiting for transfers between devices, shards(): lax.all_to_all(answer.reshape(tiles, CAP, block_width), 'tile', 0, 0, til...  18.5 us
    all_to_all x1, waiting for transfers between devices, shards(): recv = lax.all_to_all(send, 'tile', 0, 0, tiled=True)  13.5 us
    ppermute x3, starting transfers between devices, from_behind(): return lax.ppermute(x, axis, pairs)  10.5 us
    gather x1, local copies, waits for them, and re-layouts, shards(): jnp.take(back.reshape(slots, block_width), slot, axis=0, mode='clip')  8.04 us
    all_to_all x1, starting transfers between devices, shards(): recv = lax.all_to_all(send, 'tile', 0, 0, tiled=True)  6.75 us
    dot_general x1, matrix products, shards(): jnp.einsum('kij,ki->kj', jacobian[0], merged, preferred_element_type=jnp....  6.09 us
    all_to_all x1, starting transfers between devices, shards(): lax.all_to_all(answer.reshape(tiles, CAP, block_width), 'tile', 0, 0, til...  3.78 us
    ppermute x3, waiting for transfers between devices, from_behind(): return lax.ppermute(x, axis, pairs)  3.09 us
  transfers between devices with their start and end apart: 5, of which 3 were waited for; matrix products, arithmetic and copies ran while one was open for 9% of the time, Pallas kernels for 0%

profile of v9, /device:TPU:161, one launch (start us, length us, event | category | flops | bytes accessed | tf_op | source)
XLA Modules:
  0.0 90.5 jit_solution(9274728397701287775)
XLA Ops:
  0.0 0.9 fusion.45
  0.9 0.7 iota_compare_fusion.13
  1.6 0.9 convolution_bitcast_fusion
  3.1 0.8 multiply_reduce_fusion
  4.0 0.7 convert_bitcast_fusion
  4.7 0.5 fusion.33
  5.3 1.1 %copy.27 = bf16[16,4,128]{1,2,0:T(8,128)(2,1)} copy(bf16[16,4,128]{2,1,0:T(4,128)(2,1)S(1)} %reshape.179) | data formatting | bytes 32768 | tf_op jit(solution)/shard_map/reshape | solution.py:74
  7.0 2.5 %fusion.23 = bf16[16,256,128]{1,2,0:T(8,128)(2,1)S(1)} fusion(pred[16,2048]{1,0:T(8,128)(4,1)S(1)} %iota_compare_fusion.13, bf16[2048,128]{0,1:T(8,128)(2,1)S(1)} %copy.23, s32[2048]{0:T(1024)S(1)} %get-tuple-element.8), kind=kOutput, calls=%fused_computation.24 | convolution fusion | flops 2152726528 | bytes 1613824 | tf_op jit(solution)/shard_map/jr,djc->drc/dot_general | solution.py:68
  9.9 1.6 %copy.28 = bf16[16,272,128]{2,1,0:T(8,128)(2,1)} copy(bf16[16,272,128]{1,2,0:T(8,128)(2,1)S(1)} %maximum_maximum_fusion) | data formatting | bytes 2228224 | tf_op jit(solution)/shard_map/concatenate | solution.py:71
  11.5 6.8 %all-to-all-start = ((bf16[16,272,128]{2,1,0:T(8,128)(2,1)}), bf16[16,272,128]{2,1,0:T(8,128)(2,1)S(1)}, u32[]{:S(2)}, u32[]{:S(2)}) async-start(bf16[16,272,128]{2,1,0:T(8,128)(2,1)} %copy.28), calls=%async_computation | async-start | bytes 2228224 | tf_op jit(solution)/shard_map/all_to_all | solution.py:79
  18.3 2.9 %collective-permute-start.1 = (bf16[64,128]{1,0:T(8,128)(2,1)S(1)}, bf16[64,128]{1,0:T(8,128)(2,1)S(1)}, u32[]{:S(2)}, u32[]{:S(2)}) collective-permute-start(bf16[64,128]{1,0:T(8,128)(2,1)S(1)} %bitcast.106), channel_id=1, source_target_pairs={{16,0},{32,16},{48,32},{64,48},{80,64},{96,80},{112,96},{128,112},... | collective-permute-start | bytes 49160 | tf_op jit(solution)/shard_map/ppermute | solution.py:12
  21.1 13.5 %all-to-all-done = bf16[16,272,128]{2,1,0:T(8,128)(2,1)S(1)} async-done(((bf16[16,272,128]{2,1,0:T(8,128)(2,1)}), bf16[16,272,128]{2,1,0:T(8,128)(2,1)S(1)}, u32[]{:S(2)}, u32[]{:S(2)}) %all-to-all-start) | async-done | bytes 1114144 | tf_op jit(solution)/shard_map/all_to_all | solution.py:79
  34.8 0.7 fusion.29
  35.5 6.1 %fusion = f32[256,1,128]{2,1,0:T(1,128)S(1)} fusion(bf16[1,256,128,128]{3,2,1,0:T(8,128)(2,1)} %param.16, bf16[256,128,1]{1,0,2:T(8,128)(2,1)S(1)} %fusion.29), kind=kOutput, calls=%fused_computation.1 | convolution fusion | flops 8388608 | bytes 8585216 | tf_op jit(solution)/shard_map/kij,ki->kj/dot_general | solution.py:97
  42.0 0.9 %fusion.16 = f32[48,1,128]{2,1,0:T(1,128)S(1)} fusion(bf16[1,48,128,128]{3,2,1,0:T(8,128)(2,1)S(1)} %copy-done, bf16[48,128,1]{1,0,2:T(8,128)(2,1)S(1)} %fusion.36), kind=kOutput, calls=%fused_computation.21 | convolution fusion | flops 1572864 | bytes 1609728 | tf_op jit(solution)/shard_map/cij,cj->ci/dot_general | solution.py:107
  43.1 5.7 %collective-permute-start = (bf16[64,128]{1,0:T(8,128)(2,1)S(1)}, bf16[64,128]{1,0:T(8,128)(2,1)S(1)}, u32[]{:S(2)}, u32[]{:S(2)}) collective-permute-start(bf16[64,128]{1,0:T(8,128)(2,1)S(1)} %convolution_convert_fusion.1), channel_id=1, source_target_pairs={{0,16},{16,32},{32,48},{48,64},{64,80},{80,96},{96,112},{112,128},... | collective-permute-start | bytes 49160 | tf_op jit(solution)/shard_map/ppermute | solution.py:12
  48.8 1.9 %collective-permute-start.2 = (bf16[64,128]{1,0:T(8,128)(2,1)S(1)}, bf16[64,128]{1,0:T(8,128)(2,1)S(1)}, u32[]{:S(2)}, u32[]{:S(2)}) collective-permute-start(bf16[64,128]{1,0:T(8,128)(2,1)S(1)} %convolution_convert_fusion.1), channel_id=1, source_target_pairs={{16,0},{32,16},{48,32},{64,48},{80,64},{96,80},{112,96},{128,112},... | collective-permute-start | bytes 49160 | tf_op jit(solution)/shard_map/ppermute | solution.py:12
  50.8 3.1 %collective-permute-done.2 = bf16[64,128]{1,0:T(8,128)(2,1)S(1)} collective-permute-done((bf16[64,128]{1,0:T(8,128)(2,1)S(1)}, bf16[64,128]{1,0:T(8,128)(2,1)S(1)}, u32[]{:S(2)}, u32[]{:S(2)}) %collective-permute-start.2) | collective-permute-done | bytes 16416 | tf_op jit(solution)/shard_map/ppermute | solution.py:12
  54.1 2.3 %fusion.61 = f32[16,16,2048]{2,1,0:T(8,128)S(1)} fusion(bf16[16,16,128]{2,1,0:T(8,128)(2,1)S(1)} %bitcast.94, bf16[16,2048,128]{2,1,0:T(8,128)(2,1)S(1)} %bitcast.87), kind=kOutput, calls=%fused_computation.77 | convolution fusion | flops 134217728 | bytes 10551296 | tf_op jit(solution)/shard_map/gkj,grj->gkr/dot_general | solution.py:122
  56.8 0.6 fusion.9
  57.4 2.6 %fusion.5 = bf16[4096,128]{1,0:T(8,128)(2,1)} fusion(bf16[256,128]{1,0:T(8,128)(2,1)S(1)} %bitcast.100, s32[4096]{0:T(1024)S(1)} %convert.11, s32[4096]{0:T(1024)S(1)} %convert.10), kind=kOutput, calls=%fused_computation.7 | convolution fusion | flops 271056896 | bytes 1146880 | tf_op jit(solution)/shard_map/dot_general | solution.py:135
  60.1 3.8 %all-to-all-start.1 = ((bf16[16,256,128]{2,1,0:T(8,128)(2,1)}), bf16[16,256,128]{2,1,0:T(8,128)(2,1)S(1)}, u32[]{:S(2)}, u32[]{:S(2)}) async-start(bf16[16,256,128]{2,1,0:T(8,128)(2,1)} %bitcast.91), calls=%async_computation.1 | async-start | bytes 2097152 | tf_op jit(solution)/shard_map/all_to_all | solution.py:137
  63.9 18.5 %all-to-all-done.1 = bf16[16,256,128]{2,1,0:T(8,128)(2,1)S(1)} async-done(((bf16[16,256,128]{2,1,0:T(8,128)(2,1)}), bf16[16,256,128]{2,1,0:T(8,128)(2,1)S(1)}, u32[]{:S(2)}, u32[]{:S(2)}) %all-to-all-start.1) | async-done | bytes 1048608 | tf_op jit(solution)/shard_map/all_to_all | solution.py:137
  82.4 8.0 %gather_fusion = bf16[2048,128]{1,0:T(8,128)(2,1)} fusion(bf16[4096,128]{1,0:T(8,128)(2,1)S(1)} %bitcast.88, s32[2048]{0:T(1024)S(1)} %broadcast_clamp_fusion), kind=kCustom, calls=%fused_computation | custom fusion | bytes 1056768 | tf_op jit(solution)/shard_map/jit(_take)/gather | solution.py:138
  (53 shorter events, 3.1 us)
Async XLA Ops:
  0.0 42.0 %copy-start = (bf16[1,48,128,128]{3,2,1,0:T(8,128)(2,1)S(1)}, bf16[1,48,128,128]{3,2,1,0:T(8,128)(2,1)}, u32[]{:S(2)}) copy-start(bf16[1,48,128,128]{3,2,1,0:T(8,128)(2,1)} %param.18) | copy-start | bytes 4718596
  0.0 6.4 %copy-start.5 = (s32[1,2048]{1,0:T(1,128)S(1)}, s32[1,2048]{1,0:T(1,128)}, u32[]{:S(2)}) copy-start(s32[1,2048]{1,0:T(1,128)} %param.13) | copy-start | bytes 24580
  0.0 6.4 %copy-start.3 = (bf16[1,2048,128]{2,1,0:T(8,128)(2,1)S(1)}, bf16[1,2048,128]{2,1,0:T(8,128)(2,1)}, u32[]{:S(2)}) copy-start(bf16[1,2048,128]{2,1,0:T(8,128)(2,1)} %param.11) | copy-start | bytes 1572868
  0.0 6.4 %copy-start.2 = (bf16[1,2048,128]{2,1,0:T(8,128)(2,1)S(1)}, bf16[1,2048,128]{2,1,0:T(8,128)(2,1)}, u32[]{:S(2)}) copy-start(bf16[1,2048,128]{2,1,0:T(8,128)(2,1)} %param.12) | copy-start | bytes 1572868
  6.9 2.6 %copy-start.1 = (bf16[16,4,128]{1,2,0:T(8,128)(2,1)S(1)}, bf16[16,4,128]{1,2,0:T(8,128)(2,1)}, u32[]{:S(2)}) copy-start(bf16[16,4,128]{1,2,0:T(8,128)(2,1)} %copy.27) | copy-start | bytes 49156
  9.9 8.3 %copy-start.6 = (bf16[1,64,128]{2,1,0:T(8,128)(2,1)S(1)}, bf16[1,64,128]{2,1,0:T(8,128)(2,1)}, u32[]{:S(2)}) copy-start(bf16[1,64,128]{2,1,0:T(8,128)(2,1)} %param.21) | copy-start | bytes 49156
  11.5 23.1 %all-to-all-start = ((bf16[16,272,128]{2,1,0:T(8,128)(2,1)}), bf16[16,272,128]{2,1,0:T(8,128)(2,1)S(1)}, u32[]{:S(2)}, u32[]{:S(2)}) async-start(bf16[16,272,128]{2,1,0:T(8,128)(2,1)} %copy.28), calls=%async_computation | async-start | bytes 2228224 | tf_op jit(solution)/shard_map/all_to_all | solution.py:79
  18.3 32.5 %collective-permute-start.1 = (bf16[64,128]{1,0:T(8,128)(2,1)S(1)}, bf16[64,128]{1,0:T(8,128)(2,1)S(1)}, u32[]{:S(2)}, u32[]{:S(2)}) collective-permute-start(bf16[64,128]{1,0:T(8,128)(2,1)S(1)} %bitcast.106), channel_id=1, source_target_pairs={{16,0},{32,16},{48,32},{64,48},{80,64},{96,80},{112,96},{128,112},... | collective-permute-start | bytes 49160 | tf_op jit(solution)/shard_map/ppermute | solution.py:12
  34.6 19.4 %slice-start = ((s8[8388608]{0:T(1024)(128)(4,1)}), s8[4194304]{0:T(1024)(128)(4,1)S(1)}, s32[]{:S(2)}) async-start(s8[8388608]{0:T(1024)(128)(4,1)} %bitcast.85), calls=%async_computation.2 | async-start | bytes 8388608
  35.5 6.1 %copy-start.7 = (s32[1,256]{1,0:T(1,128)S(1)}, s32[1,256]{1,0:T(1,128)}, u32[]{:S(2)}) copy-start(s32[1,256]{1,0:T(1,128)} %param.17) | copy-start | bytes 3076
  35.5 6.3 %copy-start.9 = (s32[1,48]{1,0:T(1,128)S(1)}, s32[1,48]{1,0:T(1,128)}, u32[]{:S(2)}) copy-start(s32[1,48]{1,0:T(1,128)} %param.20) | copy-start | bytes 580
  35.5 7.4 %copy-start.8 = (s32[1,48]{1,0:T(1,128)S(1)}, s32[1,48]{1,0:T(1,128)}, u32[]{:S(2)}) copy-start(s32[1,48]{1,0:T(1,128)} %param.19) | copy-start | bytes 580
  35.5 18.6 %slice-start.1 = ((s8[8388608]{0:T(1024)(128)(4,1)}), s8[4194304]{0:T(1024)(128)(4,1)S(1)}, s32[]{:S(2)}) async-start(s8[8388608]{0:T(1024)(128)(4,1)} %bitcast.85), calls=%async_computation.3 | async-start | bytes 8388608
  43.1 7.7 %collective-permute-start = (bf16[64,128]{1,0:T(8,128)(2,1)S(1)}, bf16[64,128]{1,0:T(8,128)(2,1)S(1)}, u32[]{:S(2)}, u32[]{:S(2)}) collective-permute-start(bf16[64,128]{1,0:T(8,128)(2,1)S(1)} %convolution_convert_fusion.1), channel_id=1, source_target_pairs={{0,16},{16,32},{32,48},{48,64},{64,80},{80,96},{96,112},{112,128},... | collective-permute-start | bytes 49160 | tf_op jit(solution)/shard_map/ppermute | solution.py:12
  48.8 5.1 %collective-permute-start.2 = (bf16[64,128]{1,0:T(8,128)(2,1)S(1)}, bf16[64,128]{1,0:T(8,128)(2,1)S(1)}, u32[]{:S(2)}, u32[]{:S(2)}) collective-permute-start(bf16[64,128]{1,0:T(8,128)(2,1)S(1)} %convolution_convert_fusion.1), channel_id=1, source_target_pairs={{16,0},{32,16},{48,32},{64,48},{80,64},{96,80},{112,96},{128,112},... | collective-permute-start | bytes 49160 | tf_op jit(solution)/shard_map/ppermute | solution.py:12
  60.1 3.8 %copy-start.4 = (s32[1,2048,1]{1,2,0:T(1,128)S(1)}, s32[1,2048,1]{1,2,0:T(1,128)}, u32[]{:S(2)}) copy-start(s32[1,2048,1]{1,2,0:T(1,128)} %param.14) | copy-start | bytes 24580
  60.1 22.4 %all-to-all-start.1 = ((bf16[16,256,128]{2,1,0:T(8,128)(2,1)}), bf16[16,256,128]{2,1,0:T(8,128)(2,1)S(1)}, u32[]{:S(2)}, u32[]{:S(2)}) async-start(bf16[16,256,128]{2,1,0:T(8,128)(2,1)} %bitcast.91), calls=%async_computation.1 | async-start | bytes 2097152 | tf_op jit(solution)/shard_map/all_to_all | solution.py:137

commit v10 on v8

--- a/solution.py
+++ b/solution.py
@@ -49,7 +49,11 @@
     names_c = names.reshape(pieces, chunk, tiles)
     within = jnp.einsum("rc,pct->prt", lower, names_c, preferred_element_type=jnp.float32)
     totals = within[:, chunk - 1, :]
-    before = jnp.cumsum(totals, axis=0) - totals
+    earlier_piece = (
+        lax.broadcasted_iota(jnp.int32, (pieces, pieces), 1)
+        < lax.broadcasted_iota(jnp.int32, (pieces, pieces), 0)
+    ).astype(jnp.float32)
+    before = jnp.dot(earlier_piece, totals, precision=lax.Precision.HIGHEST)
     counts = (within + before[:, None, :]).reshape(obs_total, tiles)
     rank = jnp.sum(counts * names.astype(jnp.float32), axis=1).astype(jnp.int32) - 1
     slot = target * CAP + rank

time: 89.3 us -> 88.9 us (level)
  no operation moved by 1% of the time
where the time goes in v10:
time: 88.9 us; the launch traced here: 88.6 us
  waiting for transfers between devices  35.1 us (39%)
  starting transfers between devices  20.9 us (24%)
  matrix products  17.8 us (20%)
  local copies, waits for them, and re-layouts  9.85 us (11%)
  other arithmetic  4.61 us (5%)
    all_to_all x1, waiting for transfers between devices, shards(): lax.all_to_all(answer.reshape(tiles, CAP, block_width), 'tile', 0, 0, til...  18.5 us
    all_to_all x1, waiting for transfers between devices, shards(): recv = lax.all_to_all(send, 'tile', 0, 0, tiled=True)  13.5 us
    ppermute x3, starting transfers between devices, from_behind(): return lax.ppermute(x, axis, pairs)  10.5 us
    all_to_all x1, starting transfers between devices, shards(): recv = lax.all_to_all(send, 'tile', 0, 0, tiled=True)  6.75 us
    gather x1, local copies, waits for them, and re-layouts, shards(): jnp.take(back.reshape(slots, block_width), slot, axis=0, mode='clip')  6.18 us
    dot_general x1, matrix products, shards(): jnp.einsum('kij,ki->kj', jacobian[0], merged, preferred_element_type=jnp....  6.09 us
    all_to_all x1, starting transfers between devices, shards(): lax.all_to_all(answer.reshape(tiles, CAP, block_width), 'tile', 0, 0, til...  3.65 us
    ppermute x3, waiting for transfers between devices, from_behind(): return lax.ppermute(x, axis, pairs)  3.1 us
  transfers between devices with their start and end apart: 5, of which 3 were waited for; matrix products, arithmetic and copies ran while one was open for 9% of the time, Pallas kernels for 0%

profile of v10, /device:TPU:161, one launch (start us, length us, event | category | flops | bytes accessed | tf_op | source)
XLA Modules:
  0.0 88.6 jit_solution(17090398245681351832)
XLA Ops:
  0.0 1.0 %convolution_bitcast_fusion = f32[16,128,16]{1,2,0:T(8,128)S(1)} fusion(s32[16,128]{1,0:T(8,128)} %bitcast.84), kind=kOutput, calls=%fused_computation.23 | convolution fusion | flops 8437760 | bytes 139264 | tf_op jit(solution)/shard_map/rc,pct->prt/dot_general | solution.py:50
  1.3 0.8 multiply_reduce_fusion
  2.2 1.5 %fusion.35 = bf16[2048,128]{1,0:T(8,128)(2,1)S(1)} fusion(bf16[1,2048,128]{2,1,0:T(8,128)(2,1)} %param.12, bf16[1,2048,128]{2,1,0:T(8,128)(2,1)} %param.11, s32[2048]{0:T(1024)} %bitcast.90), kind=kLoop, calls=%fused_computation.40 | loop fusion | flops 1572864 | bytes 1581056 | tf_op jit(solution)/shard_map/jit(_where)/broadcast_in_dim | solution.py:66
  4.0 1.2 %fusion.29 = bf16[16,256]{1,0:T(8,128)(2,1)S(1)} fusion(s32[2048]{0:T(1024)S(1)} %get-tuple-element.6, s32[2048]{0:T(1024)S(1)} %bitcast.87, bf16[2048]{0:T(1024)(128)(2,1)S(1)} %convert_reduce_fusion), kind=kOutput, calls=%fused_computation.31 | convolution fusion | flops 17371136 | bytes 28672 | tf_op jit(solution)/shard_map/dot_general | solution.py:63
  5.2 1.1 %copy.18 = bf16[16,2,128]{1,2,0:T(8,128)(2,1)} copy(bf16[16,2,128]{2,1,0:T(2,128)(2,1)S(1)} %reshape.191) | data formatting | bytes 16384 | tf_op jit(solution)/shard_map/reshape | solution.py:75
  6.3 2.5 %fusion.21 = bf16[16,256,128]{1,2,0:T(8,128)(2,1)S(1)} fusion(pred[16,2048]{1,0:T(8,128)(4,1)S(1)} %iota_compare_fusion.15, bf16[2048,128]{0,1:T(8,128)(2,1)S(1)} %copy.17, s32[2048]{0:T(1024)S(1)} %get-tuple-element.6), kind=kOutput, calls=%fused_computation.22 | convolution fusion | flops 2152726528 | bytes 1613824 | tf_op jit(solution)/shard_map/jr,djc->drc/dot_general | solution.py:69
  9.3 1.5 %copy.19 = bf16[16,272,128]{2,1,0:T(8,128)(2,1)} copy(bf16[16,272,128]{1,2,0:T(8,128)(2,1)S(1)} %maximum_maximum_fusion) | data formatting | bytes 2228224 | tf_op jit(solution)/shard_map/concatenate | solution.py:72
  10.8 6.8 %all-to-all-start = ((bf16[16,272,128]{2,1,0:T(8,128)(2,1)}), bf16[16,272,128]{2,1,0:T(8,128)(2,1)S(1)}, u32[]{:S(2)}, u32[]{:S(2)}) async-start(bf16[16,272,128]{2,1,0:T(8,128)(2,1)} %copy.19), calls=%async_computation | async-start | bytes 2228224 | tf_op jit(solution)/shard_map/all_to_all | solution.py:80
  17.6 2.9 %collective-permute-start.1 = (bf16[64,128]{1,0:T(8,128)(2,1)S(1)}, bf16[64,128]{1,0:T(8,128)(2,1)S(1)}, u32[]{:S(2)}, u32[]{:S(2)}) collective-permute-start(bf16[64,128]{1,0:T(8,128)(2,1)S(1)} %bitcast.95), channel_id=1, source_target_pairs={{16,0},{32,16},{48,32},{64,48},{80,64},{96,80},{112,96},{128,112},... | collective-permute-start | bytes 49160 | tf_op jit(solution)/shard_map/ppermute | solution.py:12
  20.5 13.5 %all-to-all-done = bf16[16,272,128]{2,1,0:T(8,128)(2,1)S(1)} async-done(((bf16[16,272,128]{2,1,0:T(8,128)(2,1)}), bf16[16,272,128]{2,1,0:T(8,128)(2,1)S(1)}, u32[]{:S(2)}, u32[]{:S(2)}) %all-to-all-start) | async-done | bytes 1114144 | tf_op jit(solution)/shard_map/all_to_all | solution.py:80
  34.1 0.7 fusion.27
  34.8 6.1 %fusion = f32[256,1,128]{2,1,0:T(1,128)S(1)} fusion(bf16[1,256,128,128]{3,2,1,0:T(8,128)(2,1)} %param.16, bf16[256,128,1]{1,0,2:T(8,128)(2,1)S(1)} %fusion.27), kind=kOutput, calls=%fused_computation.1 | convolution fusion | flops 8388608 | bytes 8585216 | tf_op jit(solution)/shard_map/kij,ki->kj/dot_general | solution.py:95
  41.3 0.9 %fusion.14 = f32[48,1,128]{2,1,0:T(1,128)S(1)} fusion(bf16[1,48,128,128]{3,2,1,0:T(8,128)(2,1)S(1)} %copy-done, bf16[48,128,1]{1,0,2:T(8,128)(2,1)S(1)} %fusion.28), kind=kOutput, calls=%fused_computation.19 | convolution fusion | flops 1572864 | bytes 1609728 | tf_op jit(solution)/shard_map/cij,cj->ci/dot_general | solution.py:105
  42.4 5.7 %collective-permute-start = (bf16[64,128]{1,0:T(8,128)(2,1)S(1)}, bf16[64,128]{1,0:T(8,128)(2,1)S(1)}, u32[]{:S(2)}, u32[]{:S(2)}) collective-permute-start(bf16[64,128]{1,0:T(8,128)(2,1)S(1)} %convolution_convert_fusion.2), channel_id=1, source_target_pairs={{0,16},{16,32},{32,48},{48,64},{64,80},{80,96},{96,112},{112,128},... | collective-permute-start | bytes 49160 | tf_op jit(solution)/shard_map/ppermute | solution.py:12
  48.1 1.9 %collective-permute-start.2 = (bf16[64,128]{1,0:T(8,128)(2,1)S(1)}, bf16[64,128]{1,0:T(8,128)(2,1)S(1)}, u32[]{:S(2)}, u32[]{:S(2)}) collective-permute-start(bf16[64,128]{1,0:T(8,128)(2,1)S(1)} %convolution_convert_fusion.2), channel_id=1, source_target_pairs={{16,0},{32,16},{48,32},{64,48},{80,64},{96,80},{112,96},{128,112},... | collective-permute-start | bytes 49160 | tf_op jit(solution)/shard_map/ppermute | solution.py:12
  50.1 3.1 %collective-permute-done.2 = bf16[64,128]{1,0:T(8,128)(2,1)S(1)} collective-permute-done((bf16[64,128]{1,0:T(8,128)(2,1)S(1)}, bf16[64,128]{1,0:T(8,128)(2,1)S(1)}, u32[]{:S(2)}, u32[]{:S(2)}) %collective-permute-start.2) | collective-permute-done | bytes 16416 | tf_op jit(solution)/shard_map/ppermute | solution.py:12
  53.4 2.3 %fusion.56 = f32[16,16,2048]{2,1,0:T(8,128)S(1)} fusion(bf16[16,16,128]{2,1,0:T(8,128)(2,1)S(1)} %bitcast.83, bf16[16,2048,128]{2,1,0:T(8,128)(2,1)S(1)} %bitcast.76), kind=kOutput, calls=%fused_computation.75 | convolution fusion | flops 134217728 | bytes 10551296 | tf_op jit(solution)/shard_map/gkj,grj->gkr/dot_general | solution.py:120
  55.7 0.4 copy.24
  56.1 0.6 fusion.8
  56.7 2.2 %convolution_convert_fusion = bf16[4096,128]{1,0:T(8,128)(2,1)} fusion(bf16[256,128]{1,0:T(8,128)(2,1)S(1)} %bitcast.89, s32[4096]{0:T(1024)S(1)} %convert.2), kind=kOutput, calls=%fused_computation.6 | convolution fusion | flops 270008320 | bytes 1130496 | tf_op jit(solution)/shard_map/dot_general | solution.py:132
  59.0 3.7 %all-to-all-start.1 = ((bf16[16,256,128]{2,1,0:T(8,128)(2,1)}), bf16[16,256,128]{2,1,0:T(8,128)(2,1)S(1)}, u32[]{:S(2)}, u32[]{:S(2)}) async-start(bf16[16,256,128]{2,1,0:T(8,128)(2,1)} %bitcast.80), calls=%async_computation.1 | async-start | bytes 2097152 | tf_op jit(solution)/shard_map/all_to_all | solution.py:133
  62.7 18.5 %all-to-all-done.1 = bf16[16,256,128]{2,1,0:T(8,128)(2,1)S(1)} async-done(((bf16[16,256,128]{2,1,0:T(8,128)(2,1)}), bf16[16,256,128]{2,1,0:T(8,128)(2,1)S(1)}, u32[]{:S(2)}, u32[]{:S(2)}) %all-to-all-start.1) | async-done | bytes 1048608 | tf_op jit(solution)/shard_map/all_to_all | solution.py:133
  81.2 6.2 %gather_fusion = bf16[2048,128]{1,0:T(8,128)(2,1)S(1)} fusion(bf16[4096,128]{1,0:T(8,128)(2,1)S(1)} %bitcast.77, s32[2048]{0:T(1024)S(1)} %broadcast_clamp_fusion), kind=kCustom, calls=%fused_computation | custom fusion | bytes 1056768 | tf_op jit(solution)/shard_map/jit(_take)/gather | solution.py:134
  87.4 1.1 %fusion.30 = bf16[1,2048,128]{2,1,0:T(8,128)(2,1)} fusion(bf16[2048,128]{1,0:T(8,128)(2,1)S(1)} %gather_fusion, s32[2048]{0:T(1024)S(1)} %bitcast.91), kind=kLoop, calls=%fused_computation.33 | loop fusion | flops 1048576 | bytes 1056768 | tf_op jit(solution)/shard_map/convert_element_type | solution.py:135
  (45 shorter events, 2.0 us)
Async XLA Ops:
  0.0 41.3 %copy-start = (bf16[1,48,128,128]{3,2,1,0:T(8,128)(2,1)S(1)}, bf16[1,48,128,128]{3,2,1,0:T(8,128)(2,1)}, u32[]{:S(2)}) copy-start(bf16[1,48,128,128]{3,2,1,0:T(8,128)(2,1)} %param.18) | copy-start | bytes 4718596
  0.0 3.9 %copy-start.2 = (s32[1,2048,1]{1,2,0:T(1,128)S(1)}, s32[1,2048,1]{1,2,0:T(1,128)}, u32[]{:S(2)}) copy-start(s32[1,2048,1]{1,2,0:T(1,128)} %param.14) | copy-start | bytes 24580
  0.0 4.0 %copy-start.5 = (s32[1,2048]{1,0:T(1,128)S(1)}, s32[1,2048]{1,0:T(1,128)}, u32[]{:S(2)}) copy-start(s32[1,2048]{1,0:T(1,128)} %param.15) | copy-start | bytes 24580
  6.3 2.6 %copy-start.1 = (bf16[16,2,128]{1,2,0:T(8,128)(2,1)S(1)}, bf16[16,2,128]{1,2,0:T(8,128)(2,1)}, u32[]{:S(2)}) copy-start(bf16[16,2,128]{1,2,0:T(8,128)(2,1)} %copy.18) | copy-start | bytes 24580
  9.3 8.3 %copy-start.4 = (bf16[1,64,128]{2,1,0:T(8,128)(2,1)S(1)}, bf16[1,64,128]{2,1,0:T(8,128)(2,1)}, u32[]{:S(2)}) copy-start(bf16[1,64,128]{2,1,0:T(8,128)(2,1)} %param.21) | copy-start | bytes 49156
  10.8 23.1 %all-to-all-start = ((bf16[16,272,128]{2,1,0:T(8,128)(2,1)}), bf16[16,272,128]{2,1,0:T(8,128)(2,1)S(1)}, u32[]{:S(2)}, u32[]{:S(2)}) async-start(bf16[16,272,128]{2,1,0:T(8,128)(2,1)} %copy.19), calls=%async_computation | async-start | bytes 2228224 | tf_op jit(solution)/shard_map/all_to_all | solution.py:80
  17.6 32.5 %collective-permute-start.1 = (bf16[64,128]{1,0:T(8,128)(2,1)S(1)}, bf16[64,128]{1,0:T(8,128)(2,1)S(1)}, u32[]{:S(2)}, u32[]{:S(2)}) collective-permute-start(bf16[64,128]{1,0:T(8,128)(2,1)S(1)} %bitcast.95), channel_id=1, source_target_pairs={{16,0},{32,16},{48,32},{64,48},{80,64},{96,80},{112,96},{128,112},... | collective-permute-start | bytes 49160 | tf_op jit(solution)/shard_map/ppermute | solution.py:12
  34.0 19.4 %slice-start = ((s8[8388608]{0:T(1024)(128)(4,1)}), s8[4194304]{0:T(1024)(128)(4,1)S(1)}, s32[]{:S(2)}) async-start(s8[8388608]{0:T(1024)(128)(4,1)} %bitcast.74), calls=%async_computation.2 | async-start | bytes 8388608
  34.8 6.1 %copy-start.6 = (s32[1,256]{1,0:T(1,128)S(1)}, s32[1,256]{1,0:T(1,128)}, u32[]{:S(2)}) copy-start(s32[1,256]{1,0:T(1,128)} %param.17) | copy-start | bytes 3076
  34.8 6.3 %copy-start.8 = (s32[1,48]{1,0:T(1,128)S(1)}, s32[1,48]{1,0:T(1,128)}, u32[]{:S(2)}) copy-start(s32[1,48]{1,0:T(1,128)} %param.20) | copy-start | bytes 580
  34.8 7.4 %copy-start.7 = (s32[1,48]{1,0:T(1,128)S(1)}, s32[1,48]{1,0:T(1,128)}, u32[]{:S(2)}) copy-start(s32[1,48]{1,0:T(1,128)} %param.19) | copy-start | bytes 580
  34.8 18.6 %slice-start.1 = ((s8[8388608]{0:T(1024)(128)(4,1)}), s8[4194304]{0:T(1024)(128)(4,1)S(1)}, s32[]{:S(2)}) async-start(s8[8388608]{0:T(1024)(128)(4,1)} %bitcast.74), calls=%async_computation.3 | async-start | bytes 8388608
  42.4 7.6 %collective-permute-start = (bf16[64,128]{1,0:T(8,128)(2,1)S(1)}, bf16[64,128]{1,0:T(8,128)(2,1)S(1)}, u32[]{:S(2)}, u32[]{:S(2)}) collective-permute-start(bf16[64,128]{1,0:T(8,128)(2,1)S(1)} %convolution_convert_fusion.2), channel_id=1, source_target_pairs={{0,16},{16,32},{32,48},{48,64},{64,80},{80,96},{96,112},{112,128},... | collective-permute-start | bytes 49160 | tf_op jit(solution)/shard_map/ppermute | solution.py:12
  48.1 5.1 %collective-permute-start.2 = (bf16[64,128]{1,0:T(8,128)(2,1)S(1)}, bf16[64,128]{1,0:T(8,128)(2,1)S(1)}, u32[]{:S(2)}, u32[]{:S(2)}) collective-permute-start(bf16[64,128]{1,0:T(8,128)(2,1)S(1)} %convolution_convert_fusion.2), channel_id=1, source_target_pairs={{16,0},{32,16},{48,32},{64,48},{80,64},{96,80},{112,96},{128,112},... | collective-permute-start | bytes 49160 | tf_op jit(solution)/shard_map/ppermute | solution.py:12
  59.0 22.2 %all-to-all-start.1 = ((bf16[16,256,128]{2,1,0:T(8,128)(2,1)}), bf16[16,256,128]{2,1,0:T(8,128)(2,1)S(1)}, u32[]{:S(2)}, u32[]{:S(2)}) async-start(bf16[16,256,128]{2,1,0:T(8,128)(2,1)} %bitcast.80), calls=%async_computation.1 | async-start | bytes 2097152 | tf_op jit(solution)/shard_map/all_to_all | solution.py:133
  81.2 6.2 %copy-start.3 = (s32[1,2048]{1,0:T(1,128)S(1)}, s32[1,2048]{1,0:T(1,128)}, u32[]{:S(2)}) copy-start(s32[1,2048]{1,0:T(1,128)} %param.13) | copy-start | bytes 24580

commit v11 on v10

--- a/solution.py
+++ b/solution.py
@@ -122,9 +122,12 @@
         local_state.reshape(groups, group, block_width),
         jac_groups,
         preferred_element_type=jnp.float32,
-    ).reshape(groups, group, group, block_width)
+    ).astype(jnp.bfloat16).reshape(groups, group, group, block_width)
     model_obs = (
-        jnp.sum(wide * eye.astype(jnp.float32)[None, :, :, None], axis=2)
+        jnp.sum(
+            jnp.where(eye[None, :, :, None] > 0, wide, jnp.zeros((), jnp.bfloat16)).astype(jnp.float32),
+            axis=2,
+        )
         .reshape(jac_total, block_width)
         .astype(jnp.bfloat16)
     )

time: 88.9 us -> 89.8 us (1.010)
  no operation moved by 1% of the time
where the time goes in v11:
time: 89.8 us; the launch traced here: 89.3 us
  waiting for transfers between devices  35.1 us (39%)
  starting transfers between devices  21 us (23%)
  matrix products  17.8 us (20%)
  local copies, waits for them, and re-layouts  9.7 us (11%)
  other arithmetic  5.38 us (6%)
    all_to_all x1, waiting for transfers between devices, shards(): lax.all_to_all(answer.reshape(tiles, CAP, block_width), 'tile', 0, 0, til...  18.6 us
    all_to_all x1, waiting for transfers between devices, shards(): recv = lax.all_to_all(send, 'tile', 0, 0, tiled=True)  13.5 us
    ppermute x3, starting transfers between devices, from_behind(): return lax.ppermute(x, axis, pairs)  10.5 us
    all_to_all x1, starting transfers between devices, shards(): recv = lax.all_to_all(send, 'tile', 0, 0, tiled=True)  6.75 us
    gather x1, local copies, waits for them, and re-layouts, shards(): jnp.take(back.reshape(slots, block_width), slot, axis=0, mode='clip')  6.18 us
    dot_general x1, matrix products, shards(): jnp.einsum('kij,ki->kj', jacobian[0], merged, preferred_element_type=jnp....  6.09 us
    all_to_all x1, starting transfers between devices, shards(): lax.all_to_all(answer.reshape(tiles, CAP, block_width), 'tile', 0, 0, til...  3.78 us
    ppermute x3, waiting for transfers between devices, from_behind(): return lax.ppermute(x, axis, pairs)  3.1 us
  transfers between devices with their start and end apart: 5, of which 3 were waited for; matrix products, arithmetic and copies ran while one was open for 9% of the time, Pallas kernels for 0%

profile of v11, /device:TPU:161, one launch (start us, length us, event | category | flops | bytes accessed | tf_op | source)
XLA Modules:
  0.0 89.3 jit_solution(16952157325437926106)
XLA Ops:
  0.0 1.0 %convolution_bitcast_fusion = f32[16,128,16]{1,2,0:T(8,128)S(1)} fusion(s32[16,128]{1,0:T(8,128)} %bitcast.84), kind=kOutput, calls=%fused_computation.22 | convolution fusion | flops 8437760 | bytes 139264 | tf_op jit(solution)/shard_map/rc,pct->prt/dot_general | solution.py:50
  1.3 0.8 multiply_reduce_fusion
  2.2 1.5 %fusion.35 = bf16[2048,128]{1,0:T(8,128)(2,1)S(1)} fusion(bf16[1,2048,128]{2,1,0:T(8,128)(2,1)} %param.12, bf16[1,2048,128]{2,1,0:T(8,128)(2,1)} %param.11, s32[2048]{0:T(1024)} %bitcast.90), kind=kLoop, calls=%fused_computation.41 | loop fusion | flops 1572864 | bytes 1581056 | tf_op jit(solution)/shard_map/jit(_where)/broadcast_in_dim | solution.py:66
  3.9 0.7 iota_compare_fusion.15
  4.7 1.2 %fusion.28 = bf16[16,256]{1,0:T(8,128)(2,1)S(1)} fusion(s32[2048]{0:T(1024)S(1)} %get-tuple-element.6, s32[2048]{0:T(1024)S(1)} %bitcast.87, bf16[2048]{0:T(1024)(128)(2,1)S(1)} %convert_reduce_fusion), kind=kOutput, calls=%fused_computation.30 | convolution fusion | flops 17371136 | bytes 28672 | tf_op jit(solution)/shard_map/dot_general | solution.py:63
  5.9 1.1 %copy.18 = bf16[16,2,128]{1,2,0:T(8,128)(2,1)} copy(bf16[16,2,128]{2,1,0:T(2,128)(2,1)S(1)} %reshape.192) | data formatting | bytes 16384 | tf_op jit(solution)/shard_map/reshape | solution.py:75
  7.0 2.5 %fusion.20 = bf16[16,256,128]{1,2,0:T(8,128)(2,1)S(1)} fusion(pred[16,2048]{1,0:T(8,128)(4,1)S(1)} %iota_compare_fusion.15, bf16[2048,128]{0,1:T(8,128)(2,1)S(1)} %copy.17, s32[2048]{0:T(1024)S(1)} %get-tuple-element.6), kind=kOutput, calls=%fused_computation.21 | convolution fusion | flops 2152726528 | bytes 1613824 | tf_op jit(solution)/shard_map/jr,djc->drc/dot_general | solution.py:69
  10.0 1.5 %copy.19 = bf16[16,272,128]{2,1,0:T(8,128)(2,1)} copy(bf16[16,272,128]{1,2,0:T(8,128)(2,1)S(1)} %maximum_maximum_fusion) | data formatting | bytes 2228224 | tf_op jit(solution)/shard_map/concatenate | solution.py:72
  11.5 6.8 %all-to-all-start = ((bf16[16,272,128]{2,1,0:T(8,128)(2,1)}), bf16[16,272,128]{2,1,0:T(8,128)(2,1)S(1)}, u32[]{:S(2)}, u32[]{:S(2)}) async-start(bf16[16,272,128]{2,1,0:T(8,128)(2,1)} %copy.19), calls=%async_computation | async-start | bytes 2228224 | tf_op jit(solution)/shard_map/all_to_all | solution.py:80
  18.3 2.9 %collective-permute-start.1 = (bf16[64,128]{1,0:T(8,128)(2,1)S(1)}, bf16[64,128]{1,0:T(8,128)(2,1)S(1)}, u32[]{:S(2)}, u32[]{:S(2)}) collective-permute-start(bf16[64,128]{1,0:T(8,128)(2,1)S(1)} %bitcast.95), channel_id=1, source_target_pairs={{16,0},{32,16},{48,32},{64,48},{80,64},{96,80},{112,96},{128,112},... | collective-permute-start | bytes 49160 | tf_op jit(solution)/shard_map/ppermute | solution.py:12
  21.2 13.5 %all-to-all-done = bf16[16,272,128]{2,1,0:T(8,128)(2,1)S(1)} async-done(((bf16[16,272,128]{2,1,0:T(8,128)(2,1)}), bf16[16,272,128]{2,1,0:T(8,128)(2,1)S(1)}, u32[]{:S(2)}, u32[]{:S(2)}) %all-to-all-start) | async-done | bytes 1114144 | tf_op jit(solution)/shard_map/all_to_all | solution.py:80
  34.8 0.7 fusion.26
  35.6 6.1 %fusion = f32[256,1,128]{2,1,0:T(1,128)S(1)} fusion(bf16[1,256,128,128]{3,2,1,0:T(8,128)(2,1)} %param.16, bf16[256,128,1]{1,0,2:T(8,128)(2,1)S(1)} %fusion.26), kind=kOutput, calls=%fused_computation.1 | convolution fusion | flops 8388608 | bytes 8585216 | tf_op jit(solution)/shard_map/kij,ki->kj/dot_general | solution.py:95
  42.1 0.9 %fusion.13 = f32[48,1,128]{2,1,0:T(1,128)S(1)} fusion(bf16[1,48,128,128]{3,2,1,0:T(8,128)(2,1)S(1)} %copy-done, bf16[48,128,1]{1,0,2:T(8,128)(2,1)S(1)} %fusion.27), kind=kOutput, calls=%fused_computation.18 | convolution fusion | flops 1572864 | bytes 1609728 | tf_op jit(solution)/shard_map/cij,cj->ci/dot_general | solution.py:105
  43.1 5.7 %collective-permute-start = (bf16[64,128]{1,0:T(8,128)(2,1)S(1)}, bf16[64,128]{1,0:T(8,128)(2,1)S(1)}, u32[]{:S(2)}, u32[]{:S(2)}) collective-permute-start(bf16[64,128]{1,0:T(8,128)(2,1)S(1)} %convolution_convert_fusion.3), channel_id=1, source_target_pairs={{0,16},{16,32},{32,48},{48,64},{64,80},{80,96},{96,112},{112,128},... | collective-permute-start | bytes 49160 | tf_op jit(solution)/shard_map/ppermute | solution.py:12
  48.8 1.9 %collective-permute-start.2 = (bf16[64,128]{1,0:T(8,128)(2,1)S(1)}, bf16[64,128]{1,0:T(8,128)(2,1)S(1)}, u32[]{:S(2)}, u32[]{:S(2)}) collective-permute-start(bf16[64,128]{1,0:T(8,128)(2,1)S(1)} %convolution_convert_fusion.3), channel_id=1, source_target_pairs={{16,0},{32,16},{48,32},{64,48},{80,64},{96,80},{112,96},{128,112},... | collective-permute-start | bytes 49160 | tf_op jit(solution)/shard_map/ppermute | solution.py:12
  50.8 3.1 %collective-permute-done.2 = bf16[64,128]{1,0:T(8,128)(2,1)S(1)} collective-permute-done((bf16[64,128]{1,0:T(8,128)(2,1)S(1)}, bf16[64,128]{1,0:T(8,128)(2,1)S(1)}, u32[]{:S(2)}, u32[]{:S(2)}) %collective-permute-start.2) | collective-permute-done | bytes 16416 | tf_op jit(solution)/shard_map/ppermute | solution.py:12
  54.1 2.3 %convolution_convert_fusion.1 = bf16[16,16,2048]{2,1,0:T(8,128)(2,1)S(1)} fusion(bf16[16,16,128]{2,1,0:T(8,128)(2,1)S(1)} %bitcast.83, bf16[16,2048,128]{2,1,0:T(8,128)(2,1)S(1)} %bitcast.76), kind=kOutput, calls=%fused_computation.11 | convolution fusion | flops 134742016 | bytes 9502720 | tf_op jit(solution)/shard_map/gkj,grj->gkr/dot_general | solution.py:120
  56.7 0.7 fusion.29
  57.4 2.2 %convolution_convert_fusion = bf16[4096,128]{1,0:T(8,128)(2,1)} fusion(bf16[256,128]{1,0:T(8,128)(2,1)S(1)} %bitcast.89, s32[4096]{0:T(1024)S(1)} %convert.3), kind=kOutput, calls=%fused_computation.6 | convolution fusion | flops 270008320 | bytes 1130496 | tf_op jit(solution)/shard_map/dot_general | solution.py:135
  59.6 3.8 %all-to-all-start.1 = ((bf16[16,256,128]{2,1,0:T(8,128)(2,1)}), bf16[16,256,128]{2,1,0:T(8,128)(2,1)S(1)}, u32[]{:S(2)}, u32[]{:S(2)}) async-start(bf16[16,256,128]{2,1,0:T(8,128)(2,1)} %bitcast.80), calls=%async_computation.1 | async-start | bytes 2097152 | tf_op jit(solution)/shard_map/all_to_all | solution.py:136
  63.5 18.6 %all-to-all-done.1 = bf16[16,256,128]{2,1,0:T(8,128)(2,1)S(1)} async-done(((bf16[16,256,128]{2,1,0:T(8,128)(2,1)}), bf16[16,256,128]{2,1,0:T(8,128)(2,1)S(1)}, u32[]{:S(2)}, u32[]{:S(2)}) %all-to-all-start.1) | async-done | bytes 1048608 | tf_op jit(solution)/shard_map/all_to_all | solution.py:136
  82.0 6.2 %gather_fusion = bf16[2048,128]{1,0:T(8,128)(2,1)S(1)} fusion(bf16[4096,128]{1,0:T(8,128)(2,1)S(1)} %bitcast.77, s32[2048]{0:T(1024)S(1)} %broadcast_clamp_fusion), kind=kCustom, calls=%fused_computation | custom fusion | bytes 1056768 | tf_op jit(solution)/shard_map/jit(_take)/gather | solution.py:137
  88.2 1.1 %fusion.30 = bf16[1,2048,128]{2,1,0:T(8,128)(2,1)} fusion(bf16[2048,128]{1,0:T(8,128)(2,1)S(1)} %gather_fusion, s32[2048]{0:T(1024)S(1)} %bitcast.91), kind=kLoop, calls=%fused_computation.34 | loop fusion | flops 1048576 | bytes 1056768 | tf_op jit(solution)/shard_map/convert_element_type | solution.py:138
  (45 shorter events, 2.3 us)
Async XLA Ops:
  0.0 42.1 %copy-start = (bf16[1,48,128,128]{3,2,1,0:T(8,128)(2,1)S(1)}, bf16[1,48,128,128]{3,2,1,0:T(8,128)(2,1)}, u32[]{:S(2)}) copy-start(bf16[1,48,128,128]{3,2,1,0:T(8,128)(2,1)} %param.18) | copy-start | bytes 4718596
  0.0 4.7 %copy-start.2 = (s32[1,2048,1]{1,2,0:T(1,128)S(1)}, s32[1,2048,1]{1,2,0:T(1,128)}, u32[]{:S(2)}) copy-start(s32[1,2048,1]{1,2,0:T(1,128)} %param.14) | copy-start | bytes 24580
  0.0 4.7 %copy-start.5 = (s32[1,2048]{1,0:T(1,128)S(1)}, s32[1,2048]{1,0:T(1,128)}, u32[]{:S(2)}) copy-start(s32[1,2048]{1,0:T(1,128)} %param.15) | copy-start | bytes 24580
  7.0 2.6 %copy-start.1 = (bf16[16,2,128]{1,2,0:T(8,128)(2,1)S(1)}, bf16[16,2,128]{1,2,0:T(8,128)(2,1)}, u32[]{:S(2)}) copy-start(bf16[16,2,128]{1,2,0:T(8,128)(2,1)} %copy.18) | copy-start | bytes 24580
  10.0 8.3 %copy-start.4 = (bf16[1,64,128]{2,1,0:T(8,128)(2,1)S(1)}, bf16[1,64,128]{2,1,0:T(8,128)(2,1)}, u32[]{:S(2)}) copy-start(bf16[1,64,128]{2,1,0:T(8,128)(2,1)} %param.21) | copy-start | bytes 49156
  11.5 23.1 %all-to-all-start = ((bf16[16,272,128]{2,1,0:T(8,128)(2,1)}), bf16[16,272,128]{2,1,0:T(8,128)(2,1)S(1)}, u32[]{:S(2)}, u32[]{:S(2)}) async-start(bf16[16,272,128]{2,1,0:T(8,128)(2,1)} %copy.19), calls=%async_computation | async-start | bytes 2228224 | tf_op jit(solution)/shard_map/all_to_all | solution.py:80
  18.3 32.5 %collective-permute-start.1 = (bf16[64,128]{1,0:T(8,128)(2,1)S(1)}, bf16[64,128]{1,0:T(8,128)(2,1)S(1)}, u32[]{:S(2)}, u32[]{:S(2)}) collective-permute-start(bf16[64,128]{1,0:T(8,128)(2,1)S(1)} %bitcast.95), channel_id=1, source_target_pairs={{16,0},{32,16},{48,32},{64,48},{80,64},{96,80},{112,96},{128,112},... | collective-permute-start | bytes 49160 | tf_op jit(solution)/shard_map/ppermute | solution.py:12
  34.7 19.4 %slice-start = ((s8[8388608]{0:T(1024)(128)(4,1)}), s8[4194304]{0:T(1024)(128)(4,1)S(1)}, s32[]{:S(2)}) async-start(s8[8388608]{0:T(1024)(128)(4,1)} %bitcast.74), calls=%async_computation.2 | async-start | bytes 8388608
  35.5 6.1 %copy-start.6 = (s32[1,256]{1,0:T(1,128)S(1)}, s32[1,256]{1,0:T(1,128)}, u32[]{:S(2)}) copy-start(s32[1,256]{1,0:T(1,128)} %param.17) | copy-start | bytes 3076
  35.5 6.3 %copy-start.8 = (s32[1,48]{1,0:T(1,128)S(1)}, s32[1,48]{1,0:T(1,128)}, u32[]{:S(2)}) copy-start(s32[1,48]{1,0:T(1,128)} %param.20) | copy-start | bytes 580
  35.5 7.4 %copy-start.7 = (s32[1,48]{1,0:T(1,128)S(1)}, s32[1,48]{1,0:T(1,128)}, u32[]{:S(2)}) copy-start(s32[1,48]{1,0:T(1,128)} %param.19) | copy-start | bytes 580
  35.6 18.6 %slice-start.1 = ((s8[8388608]{0:T(1024)(128)(4,1)}), s8[4194304]{0:T(1024)(128)(4,1)S(1)}, s32[]{:S(2)}) async-start(s8[8388608]{0:T(1024)(128)(4,1)} %bitcast.74), calls=%async_computation.3 | async-start | bytes 8388608
  43.1 7.6 %collective-permute-start = (bf16[64,128]{1,0:T(8,128)(2,1)S(1)}, bf16[64,128]{1,0:T(8,128)(2,1)S(1)}, u32[]{:S(2)}, u32[]{:S(2)}) collective-permute-start(bf16[64,128]{1,0:T(8,128)(2,1)S(1)} %convolution_convert_fusion.3), channel_id=1, source_target_pairs={{0,16},{16,32},{32,48},{48,64},{64,80},{80,96},{96,112},{112,128},... | collective-permute-start | bytes 49160 | tf_op jit(solution)/shard_map/ppermute | solution.py:12
  48.8 5.1 %collective-permute-start.2 = (bf16[64,128]{1,0:T(8,128)(2,1)S(1)}, bf16[64,128]{1,0:T(8,128)(2,1)S(1)}, u32[]{:S(2)}, u32[]{:S(2)}) collective-permute-start(bf16[64,128]{1,0:T(8,128)(2,1)S(1)} %convolution_convert_fusion.3), channel_id=1, source_target_pairs={{16,0},{32,16},{48,32},{64,48},{80,64},{96,80},{112,96},{128,112},... | collective-permute-start | bytes 49160 | tf_op jit(solution)/shard_map/ppermute | solution.py:12
  59.6 28.6 %copy-start.3 = (s32[1,2048]{1,0:T(1,128)S(1)}, s32[1,2048]{1,0:T(1,128)}, u32[]{:S(2)}) copy-start(s32[1,2048]{1,0:T(1,128)} %param.13) | copy-start | bytes 24580
  59.6 22.4 %all-to-all-start.1 = ((bf16[16,256,128]{2,1,0:T(8,128)(2,1)}), bf16[16,256,128]{2,1,0:T(8,128)(2,1)S(1)}, u32[]{:S(2)}, u32[]{:S(2)}) async-start(bf16[16,256,128]{2,1,0:T(8,128)(2,1)} %bitcast.80), calls=%async_computation.1 | async-start | bytes 2097152 | tf_op jit(solution)/shard_map/all_to_all | solution.py:136

commit v12 on v10

--- a/solution.py
+++ b/solution.py
@@ -92,7 +92,19 @@
         lax.broadcasted_iota(jnp.int32, (group, group), 0)
         == lax.broadcasted_iota(jnp.int32, (group, group), 1)
     ).astype(jnp.bfloat16)
-    spread = jnp.einsum("kij,ki->kj", jacobian[0], merged, preferred_element_type=jnp.float32)
+    replicate = (
+        lax.broadcasted_iota(jnp.int32, (block_width, group * block_width), 0)
+        == lax.broadcasted_iota(jnp.int32, (block_width, group * block_width), 1) % block_width
+    ).astype(jnp.bfloat16)
+    tiled = jnp.dot(merged, replicate, preferred_element_type=jnp.float32).astype(jnp.bfloat16)
+    block_of = lax.broadcasted_iota(jnp.int32, (groups, group, group * block_width), 2) // block_width
+    own_block = lax.broadcasted_iota(jnp.int32, (groups, group, group * block_width), 1)
+    spread_left = jnp.where(
+        block_of == own_block, tiled.reshape(groups, group, group * block_width), jnp.zeros((), jnp.bfloat16)
+    )
+    spread = jnp.einsum(
+        "gkr,grj->gkj", spread_left, jac_groups, preferred_element_type=jnp.float32
+    ).reshape(jac_total, block_width)
     state_ids = lax.broadcasted_iota(jnp.int32, (state_total, jac_total), 0)
     owners = state_ids == jac_state[0][None, :]
     state = jnp.dot(owners.astype(jnp.float32), spread, precision=lax.Precision.HIGHEST).astype(

time: 88.9 us -> 90.7 us (1.020)
  local copies, waits for them, and re-layouts: 9.85 us -> 10.8 us
    slice x1, local copies, waits for them, and re-layouts: 0.1 us -> 1.07 us  [shards(): recv_rows = recv[:, :CAP].reshape(slots, block_width)]
  transfers between devices with their start and end apart: 5 -> 5, of which waited for: 3 -> 3; matrix products, arithmetic and copies ran while one was open for 9% -> 11% of each run, Pallas kernels for 0% -> 0%
where the time goes in v12:
time: 90.7 us; the launch traced here: 90.3 us
  waiting for transfers between devices  34.9 us (38%)
  starting transfers between devices  21 us (23%)
  matrix products  18.5 us (20%)
  local copies, waits for them, and re-layouts  10.8 us (12%)
  other arithmetic  4.64 us (5%)
    all_to_all x1, waiting for transfers between devices, shards(): lax.all_to_all(answer.reshape(tiles, CAP, block_width), 'tile', 0, 0, til...  18.5 us
    all_to_all x1, waiting for transfers between devices, shards(): recv = lax.all_to_all(send, 'tile', 0, 0, tiled=True)  13.4 us
    ppermute x3, starting transfers between devices, from_behind(): return lax.ppermute(x, axis, pairs)  10.6 us
    all_to_all x1, starting transfers between devices, shards(): recv = lax.all_to_all(send, 'tile', 0, 0, tiled=True)  6.76 us
    gather x1, local copies, waits for them, and re-layouts, shards(): jnp.take(back.reshape(slots, block_width), slot, axis=0, mode='clip')  6.18 us
    dot_general x1, matrix products, shards(): jnp.einsum('gkr,grj->gkj', spread_left, jac_groups, preferred_element_typ...  4.77 us
    all_to_all x1, starting transfers between devices, shards(): lax.all_to_all(answer.reshape(tiles, CAP, block_width), 'tile', 0, 0, til...  3.65 us
    ppermute x3, waiting for transfers between devices, from_behind(): return lax.ppermute(x, axis, pairs)  2.92 us
  transfers between devices with their start and end apart: 5, of which 3 were waited for; matrix products, arithmetic and copies ran while one was open for 11% of the time, Pallas kernels for 0%

profile of v12, /device:TPU:161, one launch (start us, length us, event | category | flops | bytes accessed | tf_op | source)
XLA Modules:
  0.0 90.3 jit_solution(8337587535800469905)
XLA Ops:
  0.0 1.0 %convolution_bitcast_fusion = f32[16,128,16]{1,2,0:T(8,128)S(1)} fusion(s32[16,128]{1,0:T(8,128)} %bitcast.82), kind=kOutput, calls=%fused_computation.24 | convolution fusion | flops 8437760 | bytes 139264 | tf_op jit(solution)/shard_map/rc,pct->prt/dot_general | solution.py:50
  1.3 0.8 multiply_reduce_fusion
  2.2 1.5 %fusion.38 = bf16[2048,128]{1,0:T(8,128)(2,1)S(1)} fusion(bf16[1,2048,128]{2,1,0:T(8,128)(2,1)} %param.12, bf16[1,2048,128]{2,1,0:T(8,128)(2,1)} %param.11, s32[2048]{0:T(1024)} %bitcast.88), kind=kLoop, calls=%fused_computation.45 | loop fusion | flops 1572864 | bytes 1581056 | tf_op jit(solution)/shard_map/jit(_where)/broadcast_in_dim | solution.py:66
  4.0 1.2 %fusion.27 = bf16[16,256]{1,0:T(8,128)(2,1)S(1)} fusion(s32[2048]{0:T(1024)S(1)} %get-tuple-element.6, s32[2048]{0:T(1024)S(1)} %bitcast.85, bf16[2048]{0:T(1024)(128)(2,1)S(1)} %convert_reduce_fusion), kind=kOutput, calls=%fused_computation.31 | convolution fusion | flops 17371136 | bytes 28672 | tf_op jit(solution)/shard_map/dot_general | solution.py:63
  5.2 1.1 %copy.18 = bf16[16,2,128]{1,2,0:T(8,128)(2,1)} copy(bf16[16,2,128]{2,1,0:T(2,128)(2,1)S(1)} %reshape.197) | data formatting | bytes 16384 | tf_op jit(solution)/shard_map/reshape | solution.py:75
  6.3 2.5 %fusion.20 = bf16[16,256,128]{1,2,0:T(8,128)(2,1)S(1)} fusion(pred[16,2048]{1,0:T(8,128)(4,1)S(1)} %iota_compare_fusion.16, bf16[2048,128]{0,1:T(8,128)(2,1)S(1)} %copy.17, s32[2048]{0:T(1024)S(1)} %get-tuple-element.6), kind=kOutput, calls=%fused_computation.23 | convolution fusion | flops 2152726528 | bytes 1613824 | tf_op jit(solution)/shard_map/jr,djc->drc/dot_general | solution.py:69
  9.3 1.5 %copy.19 = bf16[16,272,128]{2,1,0:T(8,128)(2,1)} copy(bf16[16,272,128]{1,2,0:T(8,128)(2,1)S(1)} %maximum_maximum_fusion) | data formatting | bytes 2228224 | tf_op jit(solution)/shard_map/concatenate | solution.py:72
  10.8 6.8 %all-to-all-start = ((bf16[16,272,128]{2,1,0:T(8,128)(2,1)}), bf16[16,272,128]{2,1,0:T(8,128)(2,1)S(1)}, u32[]{:S(2)}, u32[]{:S(2)}) async-start(bf16[16,272,128]{2,1,0:T(8,128)(2,1)} %copy.19), calls=%async_computation | async-start | bytes 2228224 | tf_op jit(solution)/shard_map/all_to_all | solution.py:80
  17.6 2.9 %collective-permute-start.1 = (bf16[64,128]{1,0:T(8,128)(2,1)S(1)}, bf16[64,128]{1,0:T(8,128)(2,1)S(1)}, u32[]{:S(2)}, u32[]{:S(2)}) collective-permute-start(bf16[64,128]{1,0:T(8,128)(2,1)S(1)} %bitcast.93), channel_id=1, source_target_pairs={{16,0},{32,16},{48,32},{64,48},{80,64},{96,80},{112,96},{128,112},... | collective-permute-start | bytes 49160 | tf_op jit(solution)/shard_map/ppermute | solution.py:12
  20.5 13.4 %all-to-all-done = bf16[16,272,128]{2,1,0:T(8,128)(2,1)S(1)} async-done(((bf16[16,272,128]{2,1,0:T(8,128)(2,1)}), bf16[16,272,128]{2,1,0:T(8,128)(2,1)S(1)}, u32[]{:S(2)}, u32[]{:S(2)}) %all-to-all-start) | async-done | bytes 1114144 | tf_op jit(solution)/shard_map/all_to_all | solution.py:80
  34.0 1.1 %slice.16 = bf16[16,256,128]{2,1,0:T(8,128)(2,1)} slice(bf16[16,272,128]{2,1,0:T(8,128)(2,1)S(1)} %all-to-all-done), slice={[0:16], [0:256], [0:128]} | slice | bytes 2097152 | tf_op jit(solution)/shard_map/slice | solution.py:81
  35.0 2.8 %convolution_convert_fusion.1 = bf16[256,2048]{1,0:T(8,128)(2,1)S(1)} fusion(bf16[4096,128]{1,0:T(8,128)(2,1)} %bitcast.79, s32[4096]{0:T(1024)S(1)} %convert.2, s32[2048]{0:T(1024)S(1)} %get-tuple-element.7, s32[2048]{0:T(1024)S(1)} %get-tuple-element.8, pred[2048]{0:T(1024)(128)(4,1)S(1)} %fusion.58), kind=kOutput, calls=%fused_computation.9 | convolution fusion | flops 404783104 | bytes 2131968 | tf_op jit(solution)/shard_map/dot_general | solution.py:99
  37.9 4.8 %fusion.28 = f32[16,16,128]{2,1,0:T(8,128)S(1)} fusion(bf16[16,2048,128]{2,1,0:T(8,128)(2,1)} %bitcast.70, bf16[16,16,2048]{2,1,0:T(8,128)(2,1)S(1)} %bitcast.77, s32[2048]{0:T(1024)S(1)} %get-tuple-element.9, s32[2048]{0:T(1024)S(1)} %get-tuple-element.10, pred[2048]{0:T(1024)(128)(4,1)S(1)} %fusion.59), kind=kOutput, calls=%fused_computation.32 | convolution fusion | flops 135790592 | bytes 9586688 | tf_op jit(solution)/shard_map/gkr,grj->gkj/dot_general | solution.py:105
  43.1 0.9 %fusion.13 = f32[48,1,128]{2,1,0:T(1,128)S(1)} fusion(bf16[1,48,128,128]{3,2,1,0:T(8,128)(2,1)S(1)} %copy-done, bf16[48,128,1]{1,0,2:T(8,128)(2,1)S(1)} %fusion.26), kind=kOutput, calls=%fused_computation.20 | convolution fusion | flops 1572864 | bytes 1609728 | tf_op jit(solution)/shard_map/cij,cj->ci/dot_general | solution.py:117
  44.2 5.7 %collective-permute-start = (bf16[64,128]{1,0:T(8,128)(2,1)S(1)}, bf16[64,128]{1,0:T(8,128)(2,1)S(1)}, u32[]{:S(2)}, u32[]{:S(2)}) collective-permute-start(bf16[64,128]{1,0:T(8,128)(2,1)S(1)} %convolution_convert_fusion.3), channel_id=1, source_target_pairs={{0,16},{16,32},{32,48},{48,64},{64,80},{80,96},{96,112},{112,128},... | collective-permute-start | bytes 49160 | tf_op jit(solution)/shard_map/ppermute | solution.py:12
  49.8 2.1 %collective-permute-start.2 = (bf16[64,128]{1,0:T(8,128)(2,1)S(1)}, bf16[64,128]{1,0:T(8,128)(2,1)S(1)}, u32[]{:S(2)}, u32[]{:S(2)}) collective-permute-start(bf16[64,128]{1,0:T(8,128)(2,1)S(1)} %convolution_convert_fusion.3), channel_id=1, source_target_pairs={{16,0},{32,16},{48,32},{64,48},{80,64},{96,80},{112,96},{128,112},... | collective-permute-start | bytes 49160 | tf_op jit(solution)/shard_map/ppermute | solution.py:12
  52.0 2.9 %collective-permute-done.2 = bf16[64,128]{1,0:T(8,128)(2,1)S(1)} collective-permute-done((bf16[64,128]{1,0:T(8,128)(2,1)S(1)}, bf16[64,128]{1,0:T(8,128)(2,1)S(1)}, u32[]{:S(2)}, u32[]{:S(2)}) %collective-permute-start.2) | collective-permute-done | bytes 16416 | tf_op jit(solution)/shard_map/ppermute | solution.py:12
  55.1 2.3 %fusion.69 = f32[16,16,2048]{2,1,0:T(8,128)S(1)} fusion(bf16[16,16,128]{2,1,0:T(8,128)(2,1)S(1)} %bitcast.81, bf16[16,2048,128]{2,1,0:T(8,128)(2,1)S(1)} %bitcast.73), kind=kOutput, calls=%fused_computation.94 | convolution fusion | flops 134217728 | bytes 10551296 | tf_op jit(solution)/shard_map/gkj,grj->gkr/dot_general | solution.py:132
  57.8 0.6 fusion.6
  58.5 2.3 %convolution_convert_fusion = bf16[4096,128]{1,0:T(8,128)(2,1)} fusion(bf16[256,128]{1,0:T(8,128)(2,1)S(1)} %bitcast.87, s32[4096]{0:T(1024)S(1)} %convert.2), kind=kOutput, calls=%fused_computation.4 | convolution fusion | flops 270008320 | bytes 1130496 | tf_op jit(solution)/shard_map/dot_general | solution.py:144
  60.7 3.7 %all-to-all-start.1 = ((bf16[16,256,128]{2,1,0:T(8,128)(2,1)}), bf16[16,256,128]{2,1,0:T(8,128)(2,1)S(1)}, u32[]{:S(2)}, u32[]{:S(2)}) async-start(bf16[16,256,128]{2,1,0:T(8,128)(2,1)} %bitcast.78), calls=%async_computation.1 | async-start | bytes 2097152 | tf_op jit(solution)/shard_map/all_to_all | solution.py:145
  64.4 18.5 %all-to-all-done.1 = bf16[16,256,128]{2,1,0:T(8,128)(2,1)S(1)} async-done(((bf16[16,256,128]{2,1,0:T(8,128)(2,1)}), bf16[16,256,128]{2,1,0:T(8,128)(2,1)S(1)}, u32[]{:S(2)}, u32[]{:S(2)}) %all-to-all-start.1) | async-done | bytes 1048608 | tf_op jit(solution)/shard_map/all_to_all | solution.py:145
  83.0 6.2 %gather_fusion = bf16[2048,128]{1,0:T(8,128)(2,1)S(1)} fusion(bf16[4096,128]{1,0:T(8,128)(2,1)S(1)} %bitcast.74, s32[2048]{0:T(1024)S(1)} %broadcast_clamp_fusion), kind=kCustom, calls=%fused_computation | custom fusion | bytes 1056768 | tf_op jit(solution)/shard_map/jit(_take)/gather | solution.py:146
  89.2 1.1 %fusion.30 = bf16[1,2048,128]{2,1,0:T(8,128)(2,1)} fusion(bf16[2048,128]{1,0:T(8,128)(2,1)S(1)} %gather_fusion, s32[2048]{0:T(1024)S(1)} %bitcast.89), kind=kLoop, calls=%fused_computation.34 | loop fusion | flops 1048576 | bytes 1056768 | tf_op jit(solution)/shard_map/convert_element_type | solution.py:147
  (49 shorter events, 2.3 us)
Async XLA Ops:
  0.0 43.1 %copy-start = (bf16[1,48,128,128]{3,2,1,0:T(8,128)(2,1)S(1)}, bf16[1,48,128,128]{3,2,1,0:T(8,128)(2,1)}, u32[]{:S(2)}) copy-start(bf16[1,48,128,128]{3,2,1,0:T(8,128)(2,1)} %param.18) | copy-start | bytes 4718596
  0.0 3.9 %copy-start.2 = (s32[1,2048,1]{1,2,0:T(1,128)S(1)}, s32[1,2048,1]{1,2,0:T(1,128)}, u32[]{:S(2)}) copy-start(s32[1,2048,1]{1,2,0:T(1,128)} %param.14) | copy-start | bytes 24580
  0.0 4.0 %copy-start.5 = (s32[1,2048]{1,0:T(1,128)S(1)}, s32[1,2048]{1,0:T(1,128)}, u32[]{:S(2)}) copy-start(s32[1,2048]{1,0:T(1,128)} %param.15) | copy-start | bytes 24580
  6.3 2.6 %copy-start.1 = (bf16[16,2,128]{1,2,0:T(8,128)(2,1)S(1)}, bf16[16,2,128]{1,2,0:T(8,128)(2,1)}, u32[]{:S(2)}) copy-start(bf16[16,2,128]{1,2,0:T(8,128)(2,1)} %copy.18) | copy-start | bytes 24580
  9.2 8.3 %copy-start.4 = (bf16[1,64,128]{2,1,0:T(8,128)(2,1)S(1)}, bf16[1,64,128]{2,1,0:T(8,128)(2,1)}, u32[]{:S(2)}) copy-start(bf16[1,64,128]{2,1,0:T(8,128)(2,1)} %param.21) | copy-start | bytes 49156
  10.8 23.1 %all-to-all-start = ((bf16[16,272,128]{2,1,0:T(8,128)(2,1)}), bf16[16,272,128]{2,1,0:T(8,128)(2,1)S(1)}, u32[]{:S(2)}, u32[]{:S(2)}) async-start(bf16[16,272,128]{2,1,0:T(8,128)(2,1)} %copy.19), calls=%async_computation | async-start | bytes 2228224 | tf_op jit(solution)/shard_map/all_to_all | solution.py:80
  17.6 34.4 %collective-permute-start.1 = (bf16[64,128]{1,0:T(8,128)(2,1)S(1)}, bf16[64,128]{1,0:T(8,128)(2,1)S(1)}, u32[]{:S(2)}, u32[]{:S(2)}) collective-permute-start(bf16[64,128]{1,0:T(8,128)(2,1)S(1)} %bitcast.93), channel_id=1, source_target_pairs={{16,0},{32,16},{48,32},{64,48},{80,64},{96,80},{112,96},{128,112},... | collective-permute-start | bytes 49160 | tf_op jit(solution)/shard_map/ppermute | solution.py:12
  37.8 17.3 %slice-start = ((s8[8388608]{0:T(1024)(128)(4,1)}), s8[4194304]{0:T(1024)(128)(4,1)S(1)}, s32[]{:S(2)}) async-start(s8[8388608]{0:T(1024)(128)(4,1)} %bitcast.71), calls=%async_computation.2 | async-start | bytes 8388608
  37.8 4.8 %copy-start.6 = (s32[1,256]{1,0:T(1,128)S(1)}, s32[1,256]{1,0:T(1,128)}, u32[]{:S(2)}) copy-start(s32[1,256]{1,0:T(1,128)} %param.17) | copy-start | bytes 3076
  37.9 5.0 %copy-start.8 = (s32[1,48]{1,0:T(1,128)S(1)}, s32[1,48]{1,0:T(1,128)}, u32[]{:S(2)}) copy-start(s32[1,48]{1,0:T(1,128)} %param.20) | copy-start | bytes 580
  37.9 6.1 %copy-start.7 = (s32[1,48]{1,0:T(1,128)S(1)}, s32[1,48]{1,0:T(1,128)}, u32[]{:S(2)}) copy-start(s32[1,48]{1,0:T(1,128)} %param.19) | copy-start | bytes 580
  37.9 17.2 %slice-start.1 = ((s8[8388608]{0:T(1024)(128)(4,1)}), s8[4194304]{0:T(1024)(128)(4,1)S(1)}, s32[]{:S(2)}) async-start(s8[8388608]{0:T(1024)(128)(4,1)} %bitcast.71), calls=%async_computation.3 | async-start | bytes 8388608
  44.2 7.8 %collective-permute-start = (bf16[64,128]{1,0:T(8,128)(2,1)S(1)}, bf16[64,128]{1,0:T(8,128)(2,1)S(1)}, u32[]{:S(2)}, u32[]{:S(2)}) collective-permute-start(bf16[64,128]{1,0:T(8,128)(2,1)S(1)} %convolution_convert_fusion.3), channel_id=1, source_target_pairs={{0,16},{16,32},{32,48},{48,64},{64,80},{80,96},{96,112},{112,128},... | collective-permute-start | bytes 49160 | tf_op jit(solution)/shard_map/ppermute | solution.py:12
  49.8 5.1 %collective-permute-start.2 = (bf16[64,128]{1,0:T(8,128)(2,1)S(1)}, bf16[64,128]{1,0:T(8,128)(2,1)S(1)}, u32[]{:S(2)}, u32[]{:S(2)}) collective-permute-start(bf16[64,128]{1,0:T(8,128)(2,1)S(1)} %convolution_convert_fusion.3), channel_id=1, source_target_pairs={{16,0},{32,16},{48,32},{64,48},{80,64},{96,80},{112,96},{128,112},... | collective-permute-start | bytes 49160 | tf_op jit(solution)/shard_map/ppermute | solution.py:12
  60.7 22.2 %all-to-all-start.1 = ((bf16[16,256,128]{2,1,0:T(8,128)(2,1)}), bf16[16,256,128]{2,1,0:T(8,128)(2,1)S(1)}, u32[]{:S(2)}, u32[]{:S(2)}) async-start(bf16[16,256,128]{2,1,0:T(8,128)(2,1)} %bitcast.78), calls=%async_computation.1 | async-start | bytes 2097152 | tf_op jit(solution)/shard_map/all_to_all | solution.py:145
  83.0 6.2 %copy-start.3 = (s32[1,2048]{1,0:T(1,128)S(1)}, s32[1,2048]{1,0:T(1,128)}, u32[]{:S(2)}) copy-start(s32[1,2048]{1,0:T(1,128)} %param.13) | copy-start | bytes 24580
